TPU v7x, 512 devices: a whole 4x4x16 slice. The times are simulated.
512 devices in a mesh: exp: 32 (over z, core), rep: 16 (over y, x).
Axes of the slice: x: 4, y: 4, z: 16, core: 2. Of those that a mesh axis runs over, the one named last changes fastest.
Arguments:
- tokens: bfloat16 [65536, 1536], P(('exp', 'rep')), may hold values from -6 to 6
- grad_out: bfloat16 [65536, 1536], P(('exp', 'rep')), may hold values from -6 to 6
- expert_ids: int32 [65536, 2], P(('exp', 'rep')), may hold values from 0 to 31, all different within a row; in each aligned block of 128 rows (0 to 127, 128 to 255, ...) at most 10 rows name the same one
- probs: bfloat16 [65536, 2], P(('exp', 'rep')), may hold values from 0.099609375 to 1
- w_gate: bfloat16 [32, 768, 1536], P('exp', 'rep'), may hold values from -0.15625 to 0.15625
- w_up: bfloat16 [32, 768, 1536], P('exp', 'rep'), may hold values from -0.15625 to 0.15625
- w_down: bfloat16 [32, 768, 1536], P('exp', 'rep'), may hold values from -0.21875 to 0.21875
Outputs:
- grad_tokens: bfloat16 [65536, 1536], P(('exp', 'rep'))
- grad_probs: float32 [65536, 2], P(('exp', 'rep'))
- grad_gate: float32 [32, 768, 1536], P('exp', 'rep')
- grad_up: float32 [32, 768, 1536], P('exp', 'rep')
- grad_down: float32 [32, 768, 1536], P('exp', 'rep')
Inputs may be any that keep to these rules, and one draw needn't show every extreme that they name: `expert_ids`: each token names two different experts; among the 128 tokens of one device no expert is named more than 10 times, a bound that some block reaches.
All inputs are finite; a program needn't handle non-finite values.
Results may differ from a plain program's by a relative error of at most 0.007.
Values may be sent and summed in bfloat16 or wider, within the bound.
No kernel may reach another device: no remote copies, remote signals or barrier semaphores. Data moves between devices by JAX's collectives and lax.ppermute only.
A program may use at most 64 MiB of HBM per device.

v0:
```python
import jax
import jax.numpy as jnp
from jax import lax
from jax.sharding import PartitionSpec as P


def swapped(value, axis, stride):
    return lax.ppermute(value, axis, [(i, i ^ 1 << stride) for i in range(lax.axis_size(axis))])


def pair_gather(parts, along, bit_list, mover):
    for bit in bit_list:
        other = mover(parts, bit)
        upper_bit = lax.axis_index("rep") // (1 << bit) % 2

        def joined_pair(mine, theirs, upper_bit=upper_bit):
            length = mine.shape[along]
            shape_out = mine.shape[:along] + (2 * length,) + mine.shape[along + 1 :]
            joined = jnp.zeros(shape_out, mine.dtype)
            joined = lax.dynamic_update_slice_in_dim(joined, mine, upper_bit * length, along)
            return lax.dynamic_update_slice_in_dim(joined, theirs, (1 - upper_bit) * length, along)

        parts = jax.tree.map(joined_pair, parts, other)
    return parts


def split_halves(parts, along, upper_bit):

    def keep_part(whole):
        length = whole.shape[along] // 2
        return lax.dynamic_slice_in_dim(whole, upper_bit * length, length, along)

    def send_part(whole):
        length = whole.shape[along] // 2
        return lax.dynamic_slice_in_dim(whole, (1 - upper_bit) * length, length, along)

    return (jax.tree.map(keep_part, parts), jax.tree.map(send_part, parts))


def pair_reduce(parts, along, bit_list, mover):
    for bit in reversed(bit_list):
        upper_bit = lax.axis_index("rep") // (1 << bit) % 2
        keep, outgoing = split_halves(parts, along, upper_bit)
        received = mover(outgoing, bit)
        parts = jax.tree.map(jnp.add, keep, received)
    return parts


def half_sum(parts, mover):
    upper_bit = lax.axis_index("rep") % 2
    keep, outgoing = split_halves(parts, 1, upper_bit)
    received = mover(outgoing)
    return jax.tree.map(
        lambda mine, theirs: (mine.astype(jnp.float32) + theirs.astype(jnp.float32)).astype(
            jnp.bfloat16
        ),
        keep,
        received,
    )


def shards(tokens, grad_out, expert_ids, probs, w_gate, w_up, w_down):
    token_count = tokens.shape[0]
    width = tokens.shape[1]
    exp_count = lax.axis_size("exp")
    capacity = 5 * token_count // (2 * exp_count)
    slots = exp_count * capacity
    chosen = expert_ids.reshape(-1)
    onehot = (chosen[:, None] == jnp.arange(exp_count, dtype=jnp.int32)[None, :]).astype(jnp.int32)
    ranks = jnp.sum((jnp.cumsum(onehot, axis=0) - 1) * onehot, axis=1)
    slot_of = chosen * capacity + ranks
    routing = (slot_of[None, :] == jnp.arange(slots, dtype=jnp.int32)[:, None]).astype(jnp.bfloat16)
    token_routing = routing.reshape(slots, token_count, 2).sum(axis=2)
    prob_pairs = probs.reshape(-1, 1)
    send_tokens = (
        jnp.dot(token_routing, tokens, preferred_element_type=jnp.float32)
        .astype(jnp.bfloat16)
        .reshape(exp_count, 1, capacity, width)
    )
    send_grads = (
        jnp.dot(token_routing, grad_out, preferred_element_type=jnp.float32)
        .astype(jnp.bfloat16)
        .reshape(exp_count, 1, capacity, width)
    )
    send_probs = (
        jnp.dot(routing, prob_pairs, preferred_element_type=jnp.float32)
        .astype(jnp.bfloat16)
        .reshape(exp_count, 1, capacity)
    )
    slice_bits = [0]
    replica_bits = list(range(1, lax.axis_size("rep").bit_length() - 1))
    arrived = (
        lax.all_to_all(send_tokens, "exp", split_axis=0, concat_axis=0, tiled=True),
        lax.all_to_all(send_grads, "exp", split_axis=0, concat_axis=0, tiled=True),
        lax.all_to_all(send_probs, "exp", split_axis=0, concat_axis=0, tiled=True),
    )
    arrived = pair_gather(
        arrived,
        1,
        slice_bits,
        lambda parts, bit: swapped((parts[0], parts[1], parts[2]), "rep", bit),
    )
    full_weights = pair_gather(
        (w_gate, w_up, w_down),
        1,
        replica_bits,
        lambda parts, bit: swapped((parts[0], parts[1], parts[2]), "rep", bit),
    )
    gate_w = full_weights[0][0]
    up_w = full_weights[1][0]
    down_w = full_weights[2][0]
    rows = arrived[0].reshape(-1, width)
    grads = arrived[1].reshape(-1, width)
    weight = arrived[2].reshape(-1, 1).astype(jnp.float32)
    gate = jnp.dot(rows, gate_w.T, preferred_element_type=jnp.float32)
    up = jnp.dot(rows, up_w.T, preferred_element_type=jnp.float32)
    sig = jax.nn.sigmoid(gate)
    act = gate * sig
    hidden = act * up
    back = jnp.dot(grads, down_w.T, preferred_element_type=jnp.float32)
    prob_part = jnp.sum(hidden * back, axis=1)
    d_gate = (weight * back * up * sig * (1.0 + gate * (1.0 - sig))).astype(jnp.bfloat16)
    d_up = (weight * back * act).astype(jnp.bfloat16)
    weighted = (weight * hidden).astype(jnp.bfloat16)
    partial_rows = jnp.dot(d_gate, gate_w, preferred_element_type=jnp.float32) + jnp.dot(
        d_up, up_w, preferred_element_type=jnp.float32
    )
    partial_rows = partial_rows.astype(jnp.bfloat16).reshape(exp_count, 2, capacity, width)
    partial_probs = prob_part.astype(jnp.bfloat16).reshape(exp_count, 2, capacity)
    local_gate = jnp.dot(d_gate.T, rows, preferred_element_type=jnp.float32)[None]
    local_up = jnp.dot(d_up.T, rows, preferred_element_type=jnp.float32)[None]
    local_down = jnp.dot(weighted.T, grads, preferred_element_type=jnp.float32)[None]
    summed = half_sum(
        (partial_rows, partial_probs), lambda parts: swapped((parts[0], parts[1]), "rep", 0)
    )
    returned = (
        lax.all_to_all(summed[0], "exp", split_axis=0, concat_axis=0, tiled=True),
        lax.all_to_all(summed[1], "exp", split_axis=0, concat_axis=0, tiled=True),
    )
    weight_grads = pair_reduce(
        (local_gate, local_up, local_down),
        1,
        replica_bits,
        lambda parts, bit: swapped((parts[0], parts[1], parts[2]), "rep", bit),
    )
    slot_rows_back = returned[0].reshape(slots, width)
    slot_probs_back = returned[1].reshape(slots, 1)
    grad_tokens = jnp.dot(
        token_routing.T, slot_rows_back, preferred_element_type=jnp.float32
    ).astype(jnp.bfloat16)
    grad_probs = jnp.dot(routing.T, slot_probs_back, preferred_element_type=jnp.float32).reshape(
        token_count, 2
    )
    return (grad_tokens, grad_probs, weight_grads[0], weight_grads[1], weight_grads[2])


def solution(mesh):
    in_specs = (
        P(("exp", "rep"), None),
        P(("exp", "rep"), None),
        P(("exp", "rep"), None),
        P(("exp", "rep"), None),
        P("exp", "rep", None),
        P("exp", "rep", None),
        P("exp", "rep", None),
    )
    out_specs = (
        P(("exp", "rep"), None),
        P(("exp", "rep"), None),
        P("exp", "rep", None),
        P("exp", "rep", None),
        P("exp", "rep", None),
    )
    return jax.shard_map(shards, mesh=mesh, in_specs=in_specs, out_specs=out_specs, check_vma=False)
```

profile of v0, /device:TPU:1, one launch (start us, length us, event | category | flops | bytes accessed | tf_op | source)
XLA Modules:
  0.0 391.2 jit_solution(15205619724733340214)
XLA Ops:
  4.6 16.7 %all-to-all-start = ((bf16[32,1,10]{2,1,0:T(2,128)(2,1)}), bf16[32,1,10]{2,1,0:T(2,128)(2,1)S(1)}, u32[]{:S(2)}, u32[]{:S(2)}) async-start(bf16[32,1,10]{2,1,0:T(2,128)(2,1)} %reshape.150), calls=%async_computation | async-start | bytes 32768 | tf_op jit(solution)/shard_map/all_to_all | solution.py:95
  24.1 9.0 %all-to-all-done = bf16[32,1,10]{2,1,0:T(2,128)(2,1)S(1)} async-done(((bf16[32,1,10]{2,1,0:T(2,128)(2,1)}), bf16[32,1,10]{2,1,0:T(2,128)(2,1)S(1)}, u32[]{:S(2)}, u32[]{:S(2)}) %all-to-all-start) | async-done | bytes 672 | tf_op jit(solution)/shard_map/all_to_all | solution.py:95
  33.1 4.7 %all-to-all-start.2 = ((bf16[32,1,10,1536]{3,2,1,0:T(8,128)(2,1)}), bf16[32,1,10,1536]{3,2,1,0:T(8,128)(2,1)S(1)}, u32[]{:S(2)}, u32[]{:S(2)}) async-start(bf16[32,1,10,1536]{3,2,1,0:T(8,128)(2,1)} %bitcast.4), calls=%async_computation.2 | async-start | bytes 3145728 | tf_op jit(solution)/shard_map/all_to_all | solution.py:93
  37.8 4.7 %collective-permute-start.9 = (bf16[1,48,1536]{2,1,0:T(8,128)(2,1)}, bf16[1,48,1536]{2,1,0:T(8,128)(2,1)}, u32[]{:S(2)}, u32[]{:S(2)}) collective-permute-start(bf16[1,48,1536]{2,1,0:T(8,128)(2,1)} %param.11), channel_id=1, source_target_pairs={{0,2},{1,3},{2,0},{3,1},{4,6},{5,7},{6,4},{7,5},{8,10},{9,11},{10,... | collective-permute-start | bytes 442376 | tf_op jit(solution)/shard_map/ppermute | solution.py:8
  44.6 4.7 %collective-permute-start.2 = (bf16[1,48,1536]{2,1,0:T(8,128)(2,1)}, bf16[1,48,1536]{2,1,0:T(8,128)(2,1)}, u32[]{:S(2)}, u32[]{:S(2)}) collective-permute-start(bf16[1,48,1536]{2,1,0:T(8,128)(2,1)} %param.13), channel_id=1, source_target_pairs={{0,2},{1,3},{2,0},{3,1},{4,6},{5,7},{6,4},{7,5},{8,10},{9,11},{10,... | collective-permute-start | bytes 442376 | tf_op jit(solution)/shard_map/ppermute | solution.py:8
  55.3 2.2 collective-permute-start
  61.3 3.2 collective-permute-start.10
  71.3 3.2 collective-permute-start.3
  74.5 41.3 %all-to-all-done.2 = bf16[32,1,10,1536]{3,2,1,0:T(8,128)(2,1)S(1)} async-done(((bf16[32,1,10,1536]{3,2,1,0:T(8,128)(2,1)}), bf16[32,1,10,1536]{3,2,1,0:T(8,128)(2,1)S(1)}, u32[]{:S(2)}, u32[]{:S(2)}) %all-to-all-start.2) | async-done | bytes 983072 | tf_op jit(solution)/shard_map/all_to_all | solution.py:93
  115.8 4.9 %all-to-all-start.1 = ((bf16[32,1,10,1536]{3,2,1,0:T(8,128)(2,1)}), bf16[32,1,10,1536]{3,2,1,0:T(8,128)(2,1)S(1)}, u32[]{:S(2)}, u32[]{:S(2)}) async-start(bf16[32,1,10,1536]{3,2,1,0:T(8,128)(2,1)} %bitcast.72), calls=%async_computation.1 | async-start | bytes 3145728 | tf_op jit(solution)/shard_map/all_to_all | solution.py:94
  123.5 4.9 %collective-permute-start.11 = (bf16[1,192,1536]{2,1,0:T(8,128)(2,1)}, bf16[1,192,1536]{2,1,0:T(8,128)(2,1)S(1)}, u32[]{:S(2)}, u32[]{:S(2)}) collective-permute-start(bf16[1,192,1536]{2,1,0:T(8,128)(2,1)} %constant_dynamic-update-slice_fusion), channel_id=1, source_target_pairs={{0,8},{1,9},{2,10},{3,11},{4,12},{5,13},{6,14},{7,15},{8,0},{9,1},... | collective-permute-start | bytes 1769480 | tf_op jit(solution)/shard_map/ppermute | solution.py:8
  136.3 4.8 %collective-permute-start.4 = (bf16[1,192,1536]{2,1,0:T(8,128)(2,1)S(1)}, bf16[1,192,1536]{2,1,0:T(8,128)(2,1)S(1)}, u32[]{:S(2)}, u32[]{:S(2)}) collective-permute-start(bf16[1,192,1536]{2,1,0:T(8,128)(2,1)S(1)} %constant_dynamic-update-slice_fusion.9), channel_id=1, source_target_pairs={{0,8},{1,9},{2,10},{3,11},{4,12},{5,13},{6,14},{7,15},{8,0},{9,1},... | collective-permute-start | bytes 1769480 | tf_op jit(solution)/shard_map/ppermute | solution.py:8
  144.0 10.4 %collective-permute-done.8 = bf16[1,192,1536]{2,1,0:T(8,128)(2,1)S(1)} collective-permute-done((bf16[1,192,1536]{2,1,0:T(8,128)(2,1)S(1)}, bf16[1,192,1536]{2,1,0:T(8,128)(2,1)S(1)}, u32[]{:S(2)}, u32[]{:S(2)}) %collective-permute-start.8) | collective-permute-done | bytes 589856 | tf_op jit(solution)/shard_map/ppermute | solution.py:8
  156.8 3.1 collective-permute-start.5
  159.9 7.2 %collective-permute-done.4 = bf16[1,192,1536]{2,1,0:T(8,128)(2,1)S(1)} collective-permute-done((bf16[1,192,1536]{2,1,0:T(8,128)(2,1)S(1)}, bf16[1,192,1536]{2,1,0:T(8,128)(2,1)S(1)}, u32[]{:S(2)}, u32[]{:S(2)}) %collective-permute-start.4) | collective-permute-done | bytes 589856 | tf_op jit(solution)/shard_map/ppermute | solution.py:8
  167.9 30.8 %all-to-all-done.1 = bf16[32,1,10,1536]{3,2,1,0:T(8,128)(2,1)S(1)} async-done(((bf16[32,1,10,1536]{3,2,1,0:T(8,128)(2,1)}), bf16[32,1,10,1536]{3,2,1,0:T(8,128)(2,1)S(1)}, u32[]{:S(2)}, u32[]{:S(2)}) %all-to-all-start.1) | async-done | bytes 983072 | tf_op jit(solution)/shard_map/all_to_all | solution.py:94
  200.2 3.3 collective-permute-start.1
  209.0 3.0 copy_dynamic-update-slice_fusion
  212.0 2.9 reshape.140
  216.3 3.4 fusion.17
  219.7 4.1 %fusion.16 = f32[640,384]{0,1:T(8,128)} fusion(bf16[640,1536]{1,0:T(8,128)(2,1)} %copy-done.12, bf16[384,1536]{1,0:T(8,128)(2,1)} %bitcast_dynamic-update-slice_fusion.2), kind=kOutput, calls=%fused_computation.78 | convolution fusion | flops 754974720 | bytes 4128768 | tf_op jit(solution)/shard_map/dot_general | solution.py:116
  226.3 2.2 reshape.138
  228.5 3.4 fusion.1
  231.9 3.5 multiply_reduce_fusion
  235.5 2.5 fusion.20
  238.0 4.5 %fusion.18 = f32[640,1536]{1,0:T(8,128)} fusion(bf16[640,384]{0,1:T(8,128)(2,1)S(1)} %get-tuple-element.7, bf16[384,1536]{1,0:T(8,128)(2,1)} %bitcast_dynamic-update-slice_fusion.2), kind=kOutput, calls=%fused_computation.80 | convolution fusion | flops 754974720 | bytes 5603328 | tf_op jit(solution)/shard_map/dot_general | solution.py:125
  243.6 4.8 %collective-permute-start.20 = (f32[1,192,1536]{2,1,0:T(8,128)}, f32[1,192,1536]{2,1,0:T(8,128)}, u32[]{:S(2)}, u32[]{:S(2)}) collective-permute-start(f32[1,192,1536]{2,1,0:T(8,128)} %dynamic-slice_bitcast_fusion), channel_id=1, source_target_pairs={{0,8},{1,9},{2,10},{3,11},{4,12},{5,13},{6,14},{7,15},{8,0},{9,1},... | collective-permute-start | bytes 3538952 | tf_op jit(solution)/shard_map/ppermute | solution.py:8
  248.4 2.6 fusion.19
  251.1 5.0 %add_convert_fusion = bf16[640,1536]{1,0:T(8,128)(2,1)} fusion(f32[640,1536]{1,0:T(8,128)} %fusion.18, bf16[640,384]{0,1:T(8,128)(2,1)S(1)} %get-tuple-element.6, bf16[384,1536]{1,0:T(8,128)(2,1)} %bitcast_dynamic-update-slice_fusion), kind=kOutput, calls=%fused_computation | convolution fusion | flops 756940800 | bytes 7569408 | tf_op jit(solution)/shard_map/dot_general | solution.py:125
  256.1 2.6 reshape.141
  260.3 3.1 collective-permute-start.12
  268.8 15.0 %collective-permute-done.13 = bf16[32,1,10]{2,1,0:T(2,128)(2,1)S(1)} collective-permute-done((bf16[32,1,10]{2,1,0:T(2,128)(2,1)S(1)}, bf16[32,1,10]{2,1,0:T(2,128)(2,1)S(1)}, u32[]{:S(2)}, u32[]{:S(2)}) %collective-permute-start.13) | collective-permute-done | bytes 672 | tf_op jit(solution)/shard_map/ppermute | solution.py:8
  284.4 6.7 %all-to-all-start.4 = ((bf16[32,1,10]{2,1,0:T(2,128)(2,1)}), bf16[32,1,10]{2,1,0:T(2,128)(2,1)S(1)}, u32[]{:S(2)}, u32[]{:S(2)}) async-start(bf16[32,1,10]{2,1,0:T(2,128)(2,1)} %add_convert_fusion.2), calls=%async_computation.4 | async-start | bytes 32768 | tf_op jit(solution)/shard_map/all_to_all | solution.py:138
  291.0 2.5 dynamic-slice_bitcast_fusion.2
  295.5 7.4 %all-to-all-done.4 = bf16[32,1,10]{2,1,0:T(2,128)(2,1)S(1)} async-done(((bf16[32,1,10]{2,1,0:T(2,128)(2,1)}), bf16[32,1,10]{2,1,0:T(2,128)(2,1)S(1)}, u32[]{:S(2)}, u32[]{:S(2)}) %all-to-all-start.4) | async-done | bytes 672 | tf_op jit(solution)/shard_map/all_to_all | solution.py:138
  303.8 3.1 add_convert_fusion.1
  306.9 5.2 %all-to-all-start.3 = ((bf16[32,1,10,1536]{3,2,1,0:T(8,128)(2,1)}), bf16[32,1,10,1536]{3,2,1,0:T(8,128)(2,1)S(1)}, u32[]{:S(2)}, u32[]{:S(2)}) async-start(bf16[32,1,10,1536]{3,2,1,0:T(8,128)(2,1)} %add_convert_fusion.1), calls=%async_computation.3 | async-start | bytes 3145728 | tf_op jit(solution)/shard_map/all_to_all | solution.py:137
  314.0 3.3 collective-permute-start.21
  321.0 4.2 %collective-permute-done.14 = f32[1,192,1536]{2,1,0:T(8,128)} collective-permute-done((f32[1,192,1536]{2,1,0:T(8,128)}, f32[1,192,1536]{2,1,0:T(8,128)}, u32[]{:S(2)}, u32[]{:S(2)}) %collective-permute-start.14) | collective-permute-done | bytes 1179680 | tf_op jit(solution)/shard_map/ppermute | solution.py:8
  326.7 2.3 collective-permute-start.15
  329.0 7.1 %collective-permute-done.21 = f32[1,96,1536]{2,1,0:T(8,128)S(1)} collective-permute-done((f32[1,96,1536]{2,1,0:T(8,128)S(1)}, f32[1,96,1536]{2,1,0:T(8,128)S(1)}, u32[]{:S(2)}, u32[]{:S(2)}) %collective-permute-start.21) | collective-permute-done | bytes 589856 | tf_op jit(solution)/shard_map/ppermute | solution.py:8
  336.2 4.7 %collective-permute-start.22 = (f32[1,48,1536]{2,1,0:T(8,128)S(1)}, f32[1,48,1536]{2,1,0:T(8,128)S(1)}, u32[]{:S(2)}, u32[]{:S(2)}) collective-permute-start(f32[1,48,1536]{2,1,0:T(8,128)S(1)} %constant_dynamic-slice_fusion), channel_id=1, source_target_pairs={{0,2},{1,3},{2,0},{3,1},{4,6},{5,7},{6,4},{7,5},{8,10},{9,11},{10,... | collective-permute-start | bytes 884744 | tf_op jit(solution)/shard_map/ppermute | solution.py:8
  340.9 7.9 %collective-permute-done.18 = f32[1,96,1536]{2,1,0:T(8,128)S(1)} collective-permute-done((f32[1,96,1536]{2,1,0:T(8,128)S(1)}, f32[1,96,1536]{2,1,0:T(8,128)S(1)}, u32[]{:S(2)}, u32[]{:S(2)}) %collective-permute-start.18) | collective-permute-done | bytes 589856 | tf_op jit(solution)/shard_map/ppermute | solution.py:8
  348.9 4.7 %collective-permute-start.19 = (f32[1,48,1536]{2,1,0:T(8,128)S(1)}, f32[1,48,1536]{2,1,0:T(8,128)S(1)}, u32[]{:S(2)}, u32[]{:S(2)}) collective-permute-start(f32[1,48,1536]{2,1,0:T(8,128)S(1)} %constant_dynamic-slice_fusion.2), channel_id=1, source_target_pairs={{0,2},{1,3},{2,0},{3,1},{4,6},{5,7},{6,4},{7,5},{8,10},{9,11},{10,... | collective-permute-start | bytes 884744 | tf_op jit(solution)/shard_map/ppermute | solution.py:8
  353.5 7.9 %collective-permute-done.15 = f32[1,96,1536]{2,1,0:T(8,128)S(1)} collective-permute-done((f32[1,96,1536]{2,1,0:T(8,128)S(1)}, f32[1,96,1536]{2,1,0:T(8,128)S(1)}, u32[]{:S(2)}, u32[]{:S(2)}) %collective-permute-start.15) | collective-permute-done | bytes 589856 | tf_op jit(solution)/shard_map/ppermute | solution.py:8
  361.5 4.7 %collective-permute-start.16 = (f32[1,48,1536]{2,1,0:T(8,128)S(1)}, f32[1,48,1536]{2,1,0:T(8,128)S(1)}, u32[]{:S(2)}, u32[]{:S(2)}) collective-permute-start(f32[1,48,1536]{2,1,0:T(8,128)S(1)} %constant_dynamic-slice_fusion.4), channel_id=1, source_target_pairs={{0,2},{1,3},{2,0},{3,1},{4,6},{5,7},{6,4},{7,5},{8,10},{9,11},{10,... | collective-permute-start | bytes 884744 | tf_op jit(solution)/shard_map/ppermute | solution.py:8
  367.7 3.1 collective-permute-done.16
  371.5 18.1 %all-to-all-done.3 = bf16[32,1,10,1536]{3,2,1,0:T(8,128)(2,1)S(1)} async-done(((bf16[32,1,10,1536]{3,2,1,0:T(8,128)(2,1)}), bf16[32,1,10,1536]{3,2,1,0:T(8,128)(2,1)S(1)}, u32[]{:S(2)}, u32[]{:S(2)}) %all-to-all-start.3) | async-done | bytes 983072 | tf_op jit(solution)/shard_map/all_to_all | solution.py:137
  (149 shorter events, 75.5 us)
Async XLA Ops:
  0.6 21.7 %copy-start = (bf16[128,1536]{1,0:T(8,128)(2,1)S(1)}, bf16[128,1536]{1,0:T(8,128)(2,1)}, u32[]{:S(2)}) copy-start(bf16[128,1536]{1,0:T(8,128)(2,1)} %param.7) | copy-start | bytes 1179652
  4.6 28.5 %all-to-all-start = ((bf16[32,1,10]{2,1,0:T(2,128)(2,1)}), bf16[32,1,10]{2,1,0:T(2,128)(2,1)S(1)}, u32[]{:S(2)}, u32[]{:S(2)}) async-start(bf16[32,1,10]{2,1,0:T(2,128)(2,1)} %reshape.150), calls=%async_computation | async-start | bytes 32768 | tf_op jit(solution)/shard_map/all_to_all | solution.py:95
  22.3 30.3 %copy-start.15 = (bf16[320,128]{1,0:T(8,128)(2,1)}, bf16[320,128]{1,0:T(8,128)(2,1)S(1)}, u32[]{:S(2)}) copy-start(bf16[320,128]{1,0:T(8,128)(2,1)S(1)} %fusion.9) | copy-start | bytes 245764
  33.1 19.5 %copy-start.17 = (bf16[128,1536]{1,0:T(8,128)(2,1)S(1)}, bf16[128,1536]{1,0:T(8,128)(2,1)}, u32[]{:S(2)}) copy-start(bf16[128,1536]{1,0:T(8,128)(2,1)} %param.8) | copy-start | bytes 1179652
  33.1 82.7 %all-to-all-start.2 = ((bf16[32,1,10,1536]{3,2,1,0:T(8,128)(2,1)}), bf16[32,1,10,1536]{3,2,1,0:T(8,128)(2,1)S(1)}, u32[]{:S(2)}, u32[]{:S(2)}) async-start(bf16[32,1,10,1536]{3,2,1,0:T(8,128)(2,1)} %bitcast.4), calls=%async_computation.2 | async-start | bytes 3145728 | tf_op jit(solution)/shard_map/all_to_all | solution.py:93
  37.8 22.6 %collective-permute-start.9 = (bf16[1,48,1536]{2,1,0:T(8,128)(2,1)}, bf16[1,48,1536]{2,1,0:T(8,128)(2,1)}, u32[]{:S(2)}, u32[]{:S(2)}) collective-permute-start(bf16[1,48,1536]{2,1,0:T(8,128)(2,1)} %param.11), channel_id=1, source_target_pairs={{0,2},{1,3},{2,0},{3,1},{4,6},{5,7},{6,4},{7,5},{8,10},{9,11},{10,... | collective-permute-start | bytes 442376 | tf_op jit(solution)/shard_map/ppermute | solution.py:8
  42.4 22.1 %collective-permute-start.6 = (bf16[1,48,1536]{2,1,0:T(8,128)(2,1)}, bf16[1,48,1536]{2,1,0:T(8,128)(2,1)}, u32[]{:S(2)}, u32[]{:S(2)}) collective-permute-start(bf16[1,48,1536]{2,1,0:T(8,128)(2,1)} %param.12), channel_id=1, source_target_pairs={{0,2},{1,3},{2,0},{3,1},{4,6},{5,7},{6,4},{7,5},{8,10},{9,11},{10,... | collective-permute-start | bytes 442376 | tf_op jit(solution)/shard_map/ppermute | solution.py:8
  44.6 24.9 %collective-permute-start.2 = (bf16[1,48,1536]{2,1,0:T(8,128)(2,1)}, bf16[1,48,1536]{2,1,0:T(8,128)(2,1)}, u32[]{:S(2)}, u32[]{:S(2)}) collective-permute-start(bf16[1,48,1536]{2,1,0:T(8,128)(2,1)} %param.13), channel_id=1, source_target_pairs={{0,2},{1,3},{2,0},{3,1},{4,6},{5,7},{6,4},{7,5},{8,10},{9,11},{10,... | collective-permute-start | bytes 442376 | tf_op jit(solution)/shard_map/ppermute | solution.py:8
  55.3 4.8 %collective-permute-start = (bf16[32,1,10]{2,1,0:T(2,128)(2,1)S(1)}, bf16[32,1,10]{2,1,0:T(2,128)(2,1)S(1)}, u32[]{:S(2)}, u32[]{:S(2)}) collective-permute-start(bf16[32,1,10]{2,1,0:T(2,128)(2,1)S(1)} %all-to-all-done), channel_id=1, source_target_pairs={{0,1},{1,0},{2,3},{3,2},{4,5},{5,4},{6,7},{7,6},{8,9},{9,8},{10,11... | collective-permute-start | bytes 1928 | tf_op jit(solution)/shard_map/ppermute | solution.py:8
  61.3 60.5 %collective-permute-start.10 = (bf16[1,96,1536]{2,1,0:T(8,128)(2,1)S(1)}, bf16[1,96,1536]{2,1,0:T(8,128)(2,1)}, u32[]{:S(2)}, u32[]{:S(2)}) collective-permute-start(bf16[1,96,1536]{2,1,0:T(8,128)(2,1)S(1)} %constant_dynamic-update-slice_fusion.2), channel_id=1, source_target_pairs={{0,4},{1,5},{2,6},{3,7},{4,0},{5,1},{6,2},{7,3},{8,12},{9,13},{10,... | collective-permute-start | bytes 884744 | tf_op jit(solution)/shard_map/ppermute | solution.py:8
  66.1 62.4 %collective-permute-start.7 = (bf16[1,96,1536]{2,1,0:T(8,128)(2,1)}, bf16[1,96,1536]{2,1,0:T(8,128)(2,1)}, u32[]{:S(2)}, u32[]{:S(2)}) collective-permute-start(bf16[1,96,1536]{2,1,0:T(8,128)(2,1)} %constant_dynamic-update-slice_fusion.6), channel_id=1, source_target_pairs={{0,4},{1,5},{2,6},{3,7},{4,0},{5,1},{6,2},{7,3},{8,12},{9,13},{10,... | collective-permute-start | bytes 884744 | tf_op jit(solution)/shard_map/ppermute | solution.py:8
  68.3 3.0 copy-start.8
  69.5 1.8 copy-start.10
  71.3 64.1 %collective-permute-start.3 = (bf16[1,96,1536]{2,1,0:T(8,128)(2,1)}, bf16[1,96,1536]{2,1,0:T(8,128)(2,1)}, u32[]{:S(2)}, u32[]{:S(2)}) collective-permute-start(bf16[1,96,1536]{2,1,0:T(8,128)(2,1)} %constant_dynamic-update-slice_fusion.11), channel_id=1, source_target_pairs={{0,4},{1,5},{2,6},{3,7},{4,0},{5,1},{6,2},{7,3},{8,12},{9,13},{10,... | collective-permute-start | bytes 884744 | tf_op jit(solution)/shard_map/ppermute | solution.py:8
  115.8 82.9 %all-to-all-start.1 = ((bf16[32,1,10,1536]{3,2,1,0:T(8,128)(2,1)}), bf16[32,1,10,1536]{3,2,1,0:T(8,128)(2,1)S(1)}, u32[]{:S(2)}, u32[]{:S(2)}) async-start(bf16[32,1,10,1536]{3,2,1,0:T(8,128)(2,1)} %bitcast.72), calls=%async_computation.1 | async-start | bytes 3145728 | tf_op jit(solution)/shard_map/all_to_all | solution.py:94
  120.7 7.8 %copy-start.11 = (bf16[1,192,1536]{2,1,0:T(8,128)(2,1)S(1)}, bf16[1,192,1536]{2,1,0:T(8,128)(2,1)}, u32[]{:S(2)}) copy-start(bf16[1,192,1536]{2,1,0:T(8,128)(2,1)} %copy-done.10) | copy-start | bytes 1769476
  123.5 9.0 %copy-start.9 = (bf16[1,192,1536]{2,1,0:T(8,128)(2,1)S(1)}, bf16[1,192,1536]{2,1,0:T(8,128)(2,1)}, u32[]{:S(2)}) copy-start(bf16[1,192,1536]{2,1,0:T(8,128)(2,1)} %constant_dynamic-update-slice_fusion) | copy-start | bytes 1769476
  123.5 19.6 %collective-permute-start.11 = (bf16[1,192,1536]{2,1,0:T(8,128)(2,1)}, bf16[1,192,1536]{2,1,0:T(8,128)(2,1)S(1)}, u32[]{:S(2)}, u32[]{:S(2)}) collective-permute-start(bf16[1,192,1536]{2,1,0:T(8,128)(2,1)} %constant_dynamic-update-slice_fusion), channel_id=1, source_target_pairs={{0,8},{1,9},{2,10},{3,11},{4,12},{5,13},{6,14},{7,15},{8,0},{9,1},... | collective-permute-start | bytes 1769480 | tf_op jit(solution)/shard_map/ppermute | solution.py:8
  129.5 24.9 %collective-permute-start.8 = (bf16[1,192,1536]{2,1,0:T(8,128)(2,1)S(1)}, bf16[1,192,1536]{2,1,0:T(8,128)(2,1)S(1)}, u32[]{:S(2)}, u32[]{:S(2)}) collective-permute-start(bf16[1,192,1536]{2,1,0:T(8,128)(2,1)S(1)} %constant_dynamic-update-slice_fusion.4), channel_id=1, source_target_pairs={{0,8},{1,9},{2,10},{3,11},{4,12},{5,13},{6,14},{7,15},{8,0},{9,1},... | collective-permute-start | bytes 1769480 | tf_op jit(solution)/shard_map/ppermute | solution.py:8
  136.3 30.7 %collective-permute-start.4 = (bf16[1,192,1536]{2,1,0:T(8,128)(2,1)S(1)}, bf16[1,192,1536]{2,1,0:T(8,128)(2,1)S(1)}, u32[]{:S(2)}, u32[]{:S(2)}) collective-permute-start(bf16[1,192,1536]{2,1,0:T(8,128)(2,1)S(1)} %constant_dynamic-update-slice_fusion.9), channel_id=1, source_target_pairs={{0,8},{1,9},{2,10},{3,11},{4,12},{5,13},{6,14},{7,15},{8,0},{9,1},... | collective-permute-start | bytes 1769480 | tf_op jit(solution)/shard_map/ppermute | solution.py:8
  156.8 52.3 %collective-permute-start.5 = (bf16[32,1,10,1536]{3,0,2,1:T(8,128)(2,1)}, bf16[32,1,10,1536]{3,0,2,1:T(8,128)(2,1)}, u32[]{:S(2)}, u32[]{:S(2)}) collective-permute-start(bf16[32,1,10,1536]{3,0,2,1:T(8,128)(2,1)} %copy.70), channel_id=1, source_target_pairs={{0,1},{1,0},{2,3},{3,2},{4,5},{5,4},{6,7},{7,6},{8,9},{9,8},{10,11... | collective-permute-start | bytes 2949128 | tf_op jit(solution)/shard_map/ppermute | solution.py:8
  200.2 24.2 %collective-permute-start.1 = (bf16[32,1,10,1536]{3,0,2,1:T(8,128)(2,1)}, bf16[32,1,10,1536]{3,0,2,1:T(8,128)(2,1)}, u32[]{:S(2)}, u32[]{:S(2)}) collective-permute-start(bf16[32,1,10,1536]{3,0,2,1:T(8,128)(2,1)} %copy.67), channel_id=1, source_target_pairs={{0,1},{1,0},{2,3},{3,2},{4,5},{5,4},{6,7},{7,6},{8,9},{9,8},{10,11... | collective-permute-start | bytes 2949128 | tf_op jit(solution)/shard_map/ppermute | solution.py:8
  207.3 1.7 copy-start.2
  214.9 1.3 copy-start.12
  219.7 4.8 %copy-start.3 = (bf16[32,2,10,1536]{3,2,1,0:T(8,128)(2,1)S(1)}, bf16[32,2,10,1536]{3,2,1,0:T(8,128)(2,1)}, u32[]{:S(2)}) copy-start(bf16[32,2,10,1536]{3,2,1,0:T(8,128)(2,1)} %copy-done.2) | copy-start | bytes 5898244
  228.5 3.4 copy-start.14
  228.5 3.4 copy-start.18
  228.5 3.4 copy-start.19
  231.9 10.6 %copy-start.7 = (f32[384,1536]{1,0:T(8,128)}, f32[384,1536]{1,0:T(8,128)S(1)}, u32[]{:S(2)}) copy-start(f32[384,1536]{1,0:T(8,128)S(1)} %fusion.1) | copy-start | bytes 7077892
  231.9 3.5 copy-start.13
  243.6 68.5 %collective-permute-start.20 = (f32[1,192,1536]{2,1,0:T(8,128)}, f32[1,192,1536]{2,1,0:T(8,128)}, u32[]{:S(2)}, u32[]{:S(2)}) collective-permute-start(f32[1,192,1536]{2,1,0:T(8,128)} %dynamic-slice_bitcast_fusion), channel_id=1, source_target_pairs={{0,8},{1,9},{2,10},{3,11},{4,12},{5,13},{6,14},{7,15},{8,0},{9,1},... | collective-permute-start | bytes 3538952 | tf_op jit(solution)/shard_map/ppermute | solution.py:8
  258.8 6.8 %copy-start.5 = (f32[384,1536]{1,0:T(8,128)S(1)}, f32[384,1536]{1,0:T(8,128)}, u32[]{:S(2)}) copy-start(f32[384,1536]{1,0:T(8,128)} %fusion.20) | copy-start | bytes 7077892
  260.3 43.5 %collective-permute-start.12 = (bf16[32,1,10,1536]{3,0,2,1:T(8,128)(2,1)}, bf16[32,1,10,1536]{3,0,2,1:T(8,128)(2,1)}, u32[]{:S(2)}, u32[]{:S(2)}) collective-permute-start(bf16[32,1,10,1536]{3,0,2,1:T(8,128)(2,1)} %copy.72), channel_id=1, source_target_pairs={{0,1},{1,0},{2,3},{3,2},{4,5},{5,4},{6,7},{7,6},{8,9},{9,8},{10,11... | collective-permute-start | bytes 2949128 | tf_op jit(solution)/shard_map/ppermute | solution.py:8
  263.5 20.3 %collective-permute-start.13 = (bf16[32,1,10]{2,1,0:T(2,128)(2,1)S(1)}, bf16[32,1,10]{2,1,0:T(2,128)(2,1)S(1)}, u32[]{:S(2)}, u32[]{:S(2)}) collective-permute-start(bf16[32,1,10]{2,1,0:T(2,128)(2,1)S(1)} %constant_dynamic-slice_fusion.6), channel_id=1, source_target_pairs={{0,1},{1,0},{2,3},{3,2},{4,5},{5,4},{6,7},{7,6},{8,9},{9,8},{10,11... | collective-permute-start | bytes 1928 | tf_op jit(solution)/shard_map/ppermute | solution.py:8
  266.8 50.6 %collective-permute-start.17 = (f32[1,192,1536]{2,1,0:T(8,128)}, f32[1,192,1536]{2,1,0:T(8,128)}, u32[]{:S(2)}, u32[]{:S(2)}) collective-permute-start(f32[1,192,1536]{2,1,0:T(8,128)} %dynamic-slice_bitcast_fusion.1), channel_id=1, source_target_pairs={{0,8},{1,9},{2,10},{3,11},{4,12},{5,13},{6,14},{7,15},{8,0},{9,1},... | collective-permute-start | bytes 3538952 | tf_op jit(solution)/shard_map/ppermute | solution.py:8
  284.4 18.5 %all-to-all-start.4 = ((bf16[32,1,10]{2,1,0:T(2,128)(2,1)}), bf16[32,1,10]{2,1,0:T(2,128)(2,1)S(1)}, u32[]{:S(2)}, u32[]{:S(2)}) async-start(bf16[32,1,10]{2,1,0:T(2,128)(2,1)} %add_convert_fusion.2), calls=%async_computation.4 | async-start | bytes 32768 | tf_op jit(solution)/shard_map/all_to_all | solution.py:138
  293.5 31.7 %collective-permute-start.14 = (f32[1,192,1536]{2,1,0:T(8,128)}, f32[1,192,1536]{2,1,0:T(8,128)}, u32[]{:S(2)}, u32[]{:S(2)}) collective-permute-start(f32[1,192,1536]{2,1,0:T(8,128)} %dynamic-slice_bitcast_fusion.2), channel_id=1, source_target_pairs={{0,8},{1,9},{2,10},{3,11},{4,12},{5,13},{6,14},{7,15},{8,0},{9,1},... | collective-permute-start | bytes 3538952 | tf_op jit(solution)/shard_map/ppermute | solution.py:8
  306.9 82.8 %all-to-all-start.3 = ((bf16[32,1,10,1536]{3,2,1,0:T(8,128)(2,1)}), bf16[32,1,10,1536]{3,2,1,0:T(8,128)(2,1)S(1)}, u32[]{:S(2)}, u32[]{:S(2)}) async-start(bf16[32,1,10,1536]{3,2,1,0:T(8,128)(2,1)} %add_convert_fusion.1), calls=%async_computation.3 | async-start | bytes 3145728 | tf_op jit(solution)/shard_map/all_to_all | solution.py:137
  312.0 5.4 %copy-start.6 = (f32[384,1536]{1,0:T(8,128)S(1)}, f32[384,1536]{1,0:T(8,128)}, u32[]{:S(2)}) copy-start(f32[384,1536]{1,0:T(8,128)} %fusion.20) | copy-start | bytes 7077892
  314.0 11.1 %copy-start.4 = (f32[384,1536]{1,0:T(8,128)S(1)}, f32[384,1536]{1,0:T(8,128)}, u32[]{:S(2)}) copy-start(f32[384,1536]{1,0:T(8,128)} %fusion.19) | copy-start | bytes 7077892
  314.0 22.1 %collective-permute-start.21 = (f32[1,96,1536]{2,1,0:T(8,128)S(1)}, f32[1,96,1536]{2,1,0:T(8,128)S(1)}, u32[]{:S(2)}, u32[]{:S(2)}) collective-permute-start(f32[1,96,1536]{2,1,0:T(8,128)S(1)} %constant_dynamic-slice_fusion.1), channel_id=1, source_target_pairs={{0,4},{1,5},{2,6},{3,7},{4,0},{5,1},{6,2},{7,3},{8,12},{9,13},{10,... | collective-permute-start | bytes 1769480 | tf_op jit(solution)/shard_map/ppermute | solution.py:8
  318.9 29.8 %collective-permute-start.18 = (f32[1,96,1536]{2,1,0:T(8,128)S(1)}, f32[1,96,1536]{2,1,0:T(8,128)S(1)}, u32[]{:S(2)}, u32[]{:S(2)}) collective-permute-start(f32[1,96,1536]{2,1,0:T(8,128)S(1)} %constant_dynamic-slice_fusion.3), channel_id=1, source_target_pairs={{0,4},{1,5},{2,6},{3,7},{4,0},{5,1},{6,2},{7,3},{8,12},{9,13},{10,... | collective-permute-start | bytes 1769480 | tf_op jit(solution)/shard_map/ppermute | solution.py:8
  326.7 34.7 %collective-permute-start.15 = (f32[1,96,1536]{2,1,0:T(8,128)S(1)}, f32[1,96,1536]{2,1,0:T(8,128)S(1)}, u32[]{:S(2)}, u32[]{:S(2)}) collective-permute-start(f32[1,96,1536]{2,1,0:T(8,128)S(1)} %constant_dynamic-slice_fusion.5), channel_id=1, source_target_pairs={{0,4},{1,5},{2,6},{3,7},{4,0},{5,1},{6,2},{7,3},{8,12},{9,13},{10,... | collective-permute-start | bytes 1769480 | tf_op jit(solution)/shard_map/ppermute | solution.py:8
  336.2 30.0 %collective-permute-start.22 = (f32[1,48,1536]{2,1,0:T(8,128)S(1)}, f32[1,48,1536]{2,1,0:T(8,128)S(1)}, u32[]{:S(2)}, u32[]{:S(2)}) collective-permute-start(f32[1,48,1536]{2,1,0:T(8,128)S(1)} %constant_dynamic-slice_fusion), channel_id=1, source_target_pairs={{0,2},{1,3},{2,0},{3,1},{4,6},{5,7},{6,4},{7,5},{8,10},{9,11},{10,... | collective-permute-start | bytes 884744 | tf_op jit(solution)/shard_map/ppermute | solution.py:8
  348.9 18.1 %collective-permute-start.19 = (f32[1,48,1536]{2,1,0:T(8,128)S(1)}, f32[1,48,1536]{2,1,0:T(8,128)S(1)}, u32[]{:S(2)}, u32[]{:S(2)}) collective-permute-start(f32[1,48,1536]{2,1,0:T(8,128)S(1)} %constant_dynamic-slice_fusion.2), channel_id=1, source_target_pairs={{0,2},{1,3},{2,0},{3,1},{4,6},{5,7},{6,4},{7,5},{8,10},{9,11},{10,... | collective-permute-start | bytes 884744 | tf_op jit(solution)/shard_map/ppermute | solution.py:8
  361.5 9.3 %collective-permute-start.16 = (f32[1,48,1536]{2,1,0:T(8,128)S(1)}, f32[1,48,1536]{2,1,0:T(8,128)S(1)}, u32[]{:S(2)}, u32[]{:S(2)}) collective-permute-start(f32[1,48,1536]{2,1,0:T(8,128)S(1)} %constant_dynamic-slice_fusion.4), channel_id=1, source_target_pairs={{0,2},{1,3},{2,0},{3,1},{4,6},{5,7},{6,4},{7,5},{8,10},{9,11},{10,... | collective-permute-start | bytes 884744 | tf_op jit(solution)/shard_map/ppermute | solution.py:8
  367.7 22.4 %copy-start.16 = (bf16[320,128]{1,0:T(8,128)(2,1)S(1)}, bf16[320,128]{1,0:T(8,128)(2,1)}, u32[]{:S(2)}) copy-start(bf16[320,128]{1,0:T(8,128)(2,1)} %copy-done.15) | copy-start | bytes 245764
  370.8 20.4 %copy-start.1 = (bf16[128,1536]{1,0:T(8,128)(2,1)S(1)}, bf16[128,1536]{1,0:T(8,128)(2,1)}, u32[]{:S(2)}) copy-start(bf16[128,1536]{1,0:T(8,128)(2,1)} %param.7) | copy-start | bytes 1179652
where the time goes:
time: 393 us; the launch traced here: 391 us
  waiting for transfers between devices  171 us (44%)
  starting transfers between devices  114 us (29%)
  local copies, waits for them, and re-layouts  60.2 us (15%)
  matrix products  31.8 us (8%)
  other arithmetic  12.5 us (3%)
    ppermute x23, starting transfers between devices, swapped(): lax.ppermute(value, axis, [(i, i ^ 1 << stride) for i in range(lax.axis_s...  76 us
    ppermute x23, waiting for transfers between devices, swapped(): lax.ppermute(value, axis, [(i, i ^ 1 << stride) for i in range(lax.axis_s...  64.4 us
    all_to_all x1, waiting for transfers between devices, shards(): lax.all_to_all(send_tokens, 'exp', split_axis=0, concat_axis=0, tiled=True)  41.3 us
    all_to_all x1, waiting for transfers between devices, shards(): lax.all_to_all(send_grads, 'exp', split_axis=0, concat_axis=0, tiled=True)  30.8 us
    all_to_all x1, waiting for transfers between devices, shards(): lax.all_to_all(summed[0], 'exp', split_axis=0, concat_axis=0, tiled=True)  18.1 us
    all_to_all x1, starting transfers between devices, shards(): lax.all_to_all(send_probs, 'exp', split_axis=0, concat_axis=0, tiled=True)  16.7 us
    dynamic_update_slice x12, local copies, waits for them, and re-layouts, joined_pair(): lax.dynamic_update_slice_in_dim(joined, theirs, (1 - upper_bit) * length,...  15.5 us
    dynamic_update_slice x12, local copies, waits for them, and re-layouts, joined_pair(): lax.dynamic_update_slice_in_dim(joined, mine, upper_bit * length, along)  10.4 us
  transfers between devices with their start and end apart: 28, of which 15 were waited for; matrix products, arithmetic and copies ran while one was open for 20% of the time, Pallas kernels for 0%

commit v1 on v0

v1 whole, which is shorter than its diff:
```python
import jax
import jax.numpy as jnp
from jax import lax
from jax.sharding import Mesh
from jax.sharding import PartitionSpec as P

LANE = 128


def swap_pair(value):
    return lax.ppermute(value, "rl", [(0, 1), (1, 0)])


def shards(tokens, grad_out, expert_ids, probs, w_gate, w_up, w_down):
    token_count = tokens.shape[0]
    width = tokens.shape[1]
    exp_count = lax.axis_size("exp")
    capacity = 5 * token_count // (2 * exp_count)
    slots = exp_count * capacity
    chosen = expert_ids.reshape(-1)
    onehot = (chosen[:, None] == jnp.arange(exp_count, dtype=jnp.int32)[None, :]).astype(jnp.int32)
    ranks = jnp.sum((jnp.cumsum(onehot, axis=0) - 1) * onehot, axis=1)
    slot_of = chosen * capacity + ranks
    routing = (slot_of[None, :] == jnp.arange(slots, dtype=jnp.int32)[:, None]).astype(jnp.bfloat16)
    token_routing = routing.reshape(slots, token_count, 2).sum(axis=2)
    prob_pairs = probs.reshape(-1, 1)

    moved = jnp.dot(
        token_routing, jnp.concatenate([tokens, grad_out], axis=1), preferred_element_type=jnp.float32
    ).astype(jnp.bfloat16)
    slot_probs = jnp.dot(routing, prob_pairs, preferred_element_type=jnp.float32).astype(jnp.bfloat16)
    prob_block = jnp.concatenate([slot_probs, jnp.zeros((slots, LANE - 1), jnp.bfloat16)], axis=1)
    send = jnp.concatenate([moved, prob_block], axis=1).reshape(exp_count, capacity, -1)
    arrived = lax.all_to_all(send, "exp", split_axis=0, concat_axis=0, tiled=True)
    arrived = arrived.reshape(slots, -1)
    joined = jnp.concatenate([arrived, swap_pair(arrived)], axis=0)

    stacked = jnp.concatenate([w_gate, w_up, w_down], axis=0)
    full = lax.all_gather(stacked, "rh", axis=1, tiled=True)
    gate_w = full[0]
    up_w = full[1]
    down_w = full[2]

    rows = joined[:, :width]
    grads = joined[:, width : 2 * width]
    weight = joined[:, 2 * width : 2 * width + 1].astype(jnp.float32)
    gate = jnp.dot(rows, gate_w.T, preferred_element_type=jnp.float32)
    up = jnp.dot(rows, up_w.T, preferred_element_type=jnp.float32)
    sig = jax.nn.sigmoid(gate)
    act = gate * sig
    hidden = act * up
    back = jnp.dot(grads, down_w.T, preferred_element_type=jnp.float32)
    prob_part = jnp.sum(hidden * back, axis=1, keepdims=True)
    d_gate = (weight * back * up * sig * (1.0 + gate * (1.0 - sig))).astype(jnp.bfloat16)
    d_up = (weight * back * act).astype(jnp.bfloat16)
    weighted = (weight * hidden).astype(jnp.bfloat16)
    partial_rows = jnp.dot(d_gate, gate_w, preferred_element_type=jnp.float32) + jnp.dot(
        d_up, up_w, preferred_element_type=jnp.float32
    )
    row_count = rows.shape[0]
    packed = jnp.concatenate(
        [
            partial_rows.astype(jnp.bfloat16),
            prob_part.astype(jnp.bfloat16),
            jnp.zeros((row_count, LANE - 1), jnp.bfloat16),
        ],
        axis=1,
    )
    local = jnp.stack(
        [
            jnp.dot(d_gate.T, rows, preferred_element_type=jnp.float32),
            jnp.dot(d_up.T, rows, preferred_element_type=jnp.float32),
            jnp.dot(weighted.T, grads, preferred_element_type=jnp.float32),
        ]
    )
    received = swap_pair(packed[slots:])
    summed = (packed[:slots].astype(jnp.float32) + received.astype(jnp.float32)).astype(jnp.bfloat16)
    returned = lax.all_to_all(
        summed.reshape(exp_count, capacity, -1), "exp", split_axis=0, concat_axis=0, tiled=True
    ).reshape(slots, -1)
    weight_grads = lax.psum_scatter(local, "rh", scatter_dimension=1, tiled=True)

    grad_tokens = jnp.dot(
        token_routing.T, returned[:, :width], preferred_element_type=jnp.float32
    ).astype(jnp.bfloat16)
    grad_probs = jnp.dot(
        routing.T, returned[:, width : width + 1], preferred_element_type=jnp.float32
    ).reshape(token_count, 2)
    return (grad_tokens, grad_probs, weight_grads[0:1], weight_grads[1:2], weight_grads[2:3])


def solution(mesh):
    exp_count = mesh.shape["exp"]
    rep_count = mesh.shape["rep"]
    view = Mesh(mesh.devices.reshape(exp_count, rep_count // 2, 2), ("exp", "rh", "rl"))
    rows_spec = P(("exp", "rh", "rl"), None)
    weight_spec = P("exp", ("rh", "rl"), None)
    in_specs = (rows_spec,) * 4 + (weight_spec,) * 3
    out_specs = (rows_spec, rows_spec, weight_spec, weight_spec, weight_spec)
    return jax.shard_map(shards, mesh=view, in_specs=in_specs, out_specs=out_specs, check_vma=False)
```

time: 393 us -> 406 us (1.033)
  blocking collectives: 0 us -> 99.6 us
  starting transfers between devices: 114 us -> 23.2 us
  waiting for transfers between devices: 171 us -> 218 us
  local copies, waits for them, and re-layouts: 60.2 us -> 23.4 us
  matrix products: 31.8 us -> 18.9 us
  between operations: 1.52 us -> 14.3 us
  other arithmetic: 12.5 us -> 7.17 us
    all_to_all x0 -> x1, blocking collectives: none -> 99.6 us  [shards(): lax.all_to_all(summed.reshape(exp_count, capacity, -1), 'exp', split_axis...]
    ppermute x23 -> x2, starting transfers between devices: 76 us -> 6.24 us  [swap_pair(): return lax.ppermute(value, 'rl', [(0, 1), (1, 0)])]
    all_to_all x5 -> x1, waiting for transfers between devices: 107 us -> 144 us  [shards(): lax.all_to_all(send, 'exp', split_axis=0, concat_axis=0, tiled=True)]
    dynamic_update_slice x24 -> x0, local copies, waits for them, and re-layouts: 25.9 us -> none  [the longest x12 15.5 us: joined_pair(): lax.dynamic_update_slice_in_dim(joined, theirs, (1 - upper_bit) * length,...]
    all_to_all x5 -> x1, starting transfers between devices: 38.1 us -> 16.9 us  [shards(): lax.all_to_all(send, 'exp', split_axis=0, concat_axis=0, tiled=True)]
    concatenate x0 -> x5, local copies, waits for them, and re-layouts: none -> 10.3 us  [the longest x3 6.71 us: shards(): jnp.concatenate([moved, prob_block], axis=1)]
    ppermute x23 -> x2, waiting for transfers between devices: 64.4 us -> 74.1 us  [swap_pair(): return lax.ppermute(value, 'rl', [(0, 1), (1, 0)])]
    reshape x7 -> x3, local copies, waits for them, and re-layouts: 11.5 us -> 2.94 us  [the longest x1 2.16 us: shards(): arrived = arrived.reshape(slots, -1)]
  transfers between devices with their start and end apart: 28 -> 5, of which waited for: 15 -> 3; matrix products, arithmetic and copies ran while one was open for 20% -> 5% of each run, Pallas kernels for 0% -> 0%
where the time goes in v1:
time: 406 us; the launch traced here: 405 us
  waiting for transfers between devices  218 us (54%)
  blocking collectives  99.6 us (25%)
  local copies, waits for them, and re-layouts  23.4 us (6%)
  starting transfers between devices  23.2 us (6%)
  matrix products  18.9 us (5%)
  between operations  14.3 us (4%)
  other arithmetic  7.17 us (2%)
    all_to_all x1, waiting for transfers between devices, shards(): lax.all_to_all(send, 'exp', split_axis=0, concat_axis=0, tiled=True)  144 us
    all_to_all x1, blocking collectives, shards(): lax.all_to_all(summed.reshape(exp_count, capacity, -1), 'exp', split_axis...  99.6 us
    ppermute x2, waiting for transfers between devices, swap_pair(): return lax.ppermute(value, 'rl', [(0, 1), (1, 0)])  74.1 us
    all_to_all x1, starting transfers between devices, shards(): lax.all_to_all(send, 'exp', split_axis=0, concat_axis=0, tiled=True)  16.9 us
  transfers between devices with their start and end apart: 5, of which 3 were waited for; matrix products, arithmetic and copies ran while one was open for 5% of the time, Pallas kernels for 0%

profile of v1, /device:TPU:1, one launch (start us, length us, event | category | flops | bytes accessed | tf_op | source)
XLA Modules:
  0.0 405.0 jit_solution(10485850288837342530)
XLA Ops:
  7.2 0.8 copy.33
  8.0 0.1 eq.64
  8.1 0.1 eq.68
  8.2 0.6 reduce-window.6
  8.8 0.2 slice_reduce_fusion.1
  9.1 0.1 fusion.26
  9.2 0.1 reduce_sum.33
  9.4 0.7 multiply_add_fusion.1
  10.2 0.6 copy-done.4
  10.8 3.1 convolution_convert_fusion
  13.8 2.6 concatenate.21
  16.5 0.1 copy.37
  16.6 0.1 reshape.109
  16.8 0.2 convolution_reduce_fusion
  17.0 0.3 concatenate.27
  17.3 3.8 concatenate.23
  21.1 16.9 %all-to-all-start = ((bf16[32,10,3200]{2,1,0:T(8,128)(2,1)}), bf16[32,10,3200]{2,1,0:T(8,128)(2,1)S(1)}, u32[]{:S(2)}, u32[]{:S(2)}) async-start(bf16[32,10,3200]{2,1,0:T(8,128)(2,1)} %concatenate.23), calls=%async_computation | async-start | bytes 6553600 | tf_op jit(solution)/shard_map/all_to_all | solution.py:34
  38.0 1.8 pad_maximum_fusion.1
  39.9 144.1 %all-to-all-done = bf16[32,10,3200]{2,1,0:T(8,128)(2,1)S(1)} async-done(((bf16[32,10,3200]{2,1,0:T(8,128)(2,1)}), bf16[32,10,3200]{2,1,0:T(8,128)(2,1)S(1)}, u32[]{:S(2)}, u32[]{:S(2)}) %all-to-all-start) | async-done | bytes 2048032 | tf_op jit(solution)/shard_map/all_to_all | solution.py:34
  184.0 2.2 reshape.104
  186.2 3.1 collective-permute-start
  189.3 1.7 constant_dynamic-update-slice_fusion.1
  191.0 42.5 %collective-permute-done = bf16[320,3200]{1,0:T(8,128)(2,1)S(1)} collective-permute-done((bf16[320,3200]{1,0:T(8,128)(2,1)}, bf16[320,3200]{1,0:T(8,128)(2,1)S(1)}, u32[]{:S(2)}, u32[]{:S(2)}) %collective-permute-start) | collective-permute-done | bytes 2048032 | tf_op jit(solution)/shard_map/ppermute | solution.py:11
  233.5 0.3 constant_dynamic-update-slice_fusion
  233.8 1.9 copy-done.2
  235.7 0.1 convert_reduce_fusion
  235.9 3.1 fusion.7
  239.0 1.0 copy-done.3
  240.1 1.1 fusion.5
  241.2 1.1 convolution_bitcast_fusion
  242.3 1.4 multiply_reduce_fusion
  243.7 1.1 convolution_bitcast_fusion.1
  244.8 1.1 convolution_bitcast_fusion.2
  245.9 3.5 pad_maximum_fusion
  249.4 0.8 convert_element_type.71
  250.2 2.3 fusion.9
  252.5 2.6 add_convert_fusion
  255.2 3.3 concatenate.26
  258.6 3.1 collective-permute-start.1
  261.7 31.7 %collective-permute-done.1 = bf16[320,1664]{1,0:T(8,128)(2,1)S(1)} collective-permute-done((bf16[320,1664]{1,0:T(8,128)(2,1)S(1)}, bf16[320,1664]{1,0:T(8,128)(2,1)S(1)}, u32[]{:S(2)}, u32[]{:S(2)}) %collective-permute-start.1) | collective-permute-done | bytes 1064992 | tf_op jit(solution)/shard_map/ppermute | solution.py:11
  293.4 0.3 add_convert_fusion.1
  293.7 0.4 reshape.105
  294.1 99.6 %all_to_all.10 = bf16[32,10,1664]{2,1,0:T(8,128)(2,1)S(1)} all-to-all(bf16[32,10,1664]{2,1,0:T(8,128)(2,1)S(1)} %reshape.105), channel_id=1, replica_groups=mesh['exp'=32,'rh'=8,'rl'=2] {'exp'}, dimensions={0} | all-to-all | bytes 2129920 | tf_op jit(solution)/shard_map/all_to_all | solution.py:78
  393.7 0.4 reshape.106
  394.1 0.1 slice_reduce_fusion
  394.2 0.7 fusion.20
  394.9 1.1 convolution_convert_fusion.1
  396.1 2.1 fusion.30
  (33 shorter events, 0.5 us)
Async XLA Ops:
  10.1 0.6 copy-start.4
  13.8 2.6 copy-start.9
  21.1 16.9 %copy-start.8 = (bf16[1,48,1536]{2,1,0:T(8,128)(2,1)S(1)}, bf16[1,48,1536]{2,1,0:T(8,128)(2,1)}, u32[]{:S(2)}) copy-start(bf16[1,48,1536]{2,1,0:T(8,128)(2,1)} %param.13) | copy-start | bytes 442372
  21.1 162.9 %all-to-all-start = ((bf16[32,10,3200]{2,1,0:T(8,128)(2,1)}), bf16[32,10,3200]{2,1,0:T(8,128)(2,1)S(1)}, u32[]{:S(2)}, u32[]{:S(2)}) async-start(bf16[32,10,3200]{2,1,0:T(8,128)(2,1)} %concatenate.23), calls=%async_computation | async-start | bytes 6553600 | tf_op jit(solution)/shard_map/all_to_all | solution.py:34
  38.0 197.9 %all-gather.2.cloned.1.call-start = ((), (), s32[]{:S(2)}) async-start(), calls=%async_computation.3 | async-start | bytes 3981312 | tf_op jit(solution)/shard_map/all_gather | solution.py:39
  39.9 356.2 %reduce-scatter.2.cloned.1.call-start = ((), (), s32[]{:S(2)}) async-start(), calls=%async_computation.4 | async-start | bytes 7962624 | tf_op jit(solution)/shard_map/reduce_scatter | solution.py:81
  186.2 47.3 %collective-permute-start = (bf16[320,3200]{1,0:T(8,128)(2,1)}, bf16[320,3200]{1,0:T(8,128)(2,1)S(1)}, u32[]{:S(2)}, u32[]{:S(2)}) collective-permute-start(bf16[320,3200]{1,0:T(8,128)(2,1)} %reshape.104), channel_id=1, source_target_pairs={{0,1},{1,0},{2,3},{3,2},{4,5},{5,4},{6,7},{7,6},{8,9},{9,8},{10,11... | collective-permute-start | bytes 6144008 | tf_op jit(solution)/shard_map/ppermute | solution.py:11
  233.8 1.9 copy-start.2
  235.9 3.2 copy-start
  235.9 4.2 %copy-start.3 = (bf16[640,3200]{1,0:T(8,128)(2,1)S(1)}, bf16[640,3200]{1,0:T(8,128)(2,1)}, u32[]{:S(2)}) copy-start(bf16[640,3200]{1,0:T(8,128)(2,1)} %copy-done.2) | copy-start | bytes 12288004
  243.7 1.1 copy-start.6
  243.7 1.1 copy-start.1
  250.2 2.3 copy-start.7
  258.6 34.8 %collective-permute-start.1 = (bf16[320,1664]{1,0:T(8,128)(2,1)S(1)}, bf16[320,1664]{1,0:T(8,128)(2,1)S(1)}, u32[]{:S(2)}, u32[]{:S(2)}) collective-permute-start(bf16[320,1664]{1,0:T(8,128)(2,1)S(1)} %slice.68), channel_id=1, source_target_pairs={{0,1},{1,0},{2,3},{3,2},{4,5},{5,4},{6,7},{7,6},{8,9},{9,8},{10,11... | collective-permute-start | bytes 3194888 | tf_op jit(solution)/shard_map/ppermute | solution.py:11
  294.1 100.8 %copy-start.5 = (bf16[320,128]{1,0:T(8,128)(2,1)S(1)}, bf16[320,128]{1,0:T(8,128)(2,1)}, u32[]{:S(2)}) copy-start(bf16[320,128]{1,0:T(8,128)(2,1)} %copy-done.4) | copy-start | bytes 245764
Sparse Core Ops, SparseCore 0:
  42.0 80.9 all-gather.1
  249.5 126.3 reduce-scatter.1

commit v2 on v1

--- a/solution.py
+++ b/solution.py
@@ -25,15 +25,16 @@
     token_routing = routing.reshape(slots, token_count, 2).sum(axis=2)
     prob_pairs = probs.reshape(-1, 1)
 
-    moved = jnp.dot(
-        token_routing, jnp.concatenate([tokens, grad_out], axis=1), preferred_element_type=jnp.float32
-    ).astype(jnp.bfloat16)
+    slot_tokens = jnp.dot(token_routing, tokens, preferred_element_type=jnp.float32).astype(jnp.bfloat16)
+    slot_grads = jnp.dot(token_routing, grad_out, preferred_element_type=jnp.float32).astype(jnp.bfloat16)
     slot_probs = jnp.dot(routing, prob_pairs, preferred_element_type=jnp.float32).astype(jnp.bfloat16)
     prob_block = jnp.concatenate([slot_probs, jnp.zeros((slots, LANE - 1), jnp.bfloat16)], axis=1)
-    send = jnp.concatenate([moved, prob_block], axis=1).reshape(exp_count, capacity, -1)
-    arrived = lax.all_to_all(send, "exp", split_axis=0, concat_axis=0, tiled=True)
-    arrived = arrived.reshape(slots, -1)
-    joined = jnp.concatenate([arrived, swap_pair(arrived)], axis=0)
+    send_t = jnp.concatenate([slot_tokens, prob_block], axis=1).reshape(exp_count, capacity, -1)
+    arrived_t = lax.all_to_all(send_t, "exp", split_axis=0, concat_axis=0, tiled=True).reshape(slots, -1)
+    send_g = slot_grads.reshape(exp_count, capacity, -1)
+    arrived_g = lax.all_to_all(send_g, "exp", split_axis=0, concat_axis=0, tiled=True).reshape(slots, -1)
+    joined_t = jnp.concatenate([arrived_t, swap_pair(arrived_t)], axis=0)
+    joined_g = jnp.concatenate([arrived_g, swap_pair(arrived_g)], axis=0)
 
     stacked = jnp.concatenate([w_gate, w_up, w_down], axis=0)
     full = lax.all_gather(stacked, "rh", axis=1, tiled=True)
@@ -41,9 +42,9 @@
     up_w = full[1]
     down_w = full[2]
 
-    rows = joined[:, :width]
-    grads = joined[:, width : 2 * width]
-    weight = joined[:, 2 * width : 2 * width + 1].astype(jnp.float32)
+    rows = joined_t[:, :width]
+    grads = joined_g
+    weight = joined_t[:, width : width + 1].astype(jnp.float32)
     gate = jnp.dot(rows, gate_w.T, preferred_element_type=jnp.float32)
     up = jnp.dot(rows, up_w.T, preferred_element_type=jnp.float32)
     sig = jax.nn.sigmoid(gate)
@@ -66,19 +67,24 @@
         ],
         axis=1,
     )
-    local = jnp.stack(
-        [
-            jnp.dot(d_gate.T, rows, preferred_element_type=jnp.float32),
-            jnp.dot(d_up.T, rows, preferred_element_type=jnp.float32),
-            jnp.dot(weighted.T, grads, preferred_element_type=jnp.float32),
-        ]
+    grad_down = lax.psum_scatter(
+        jnp.dot(weighted.T, grads, preferred_element_type=jnp.float32)[None], "rh", scatter_dimension=1, tiled=True
     )
-    received = swap_pair(packed[slots:])
-    summed = (packed[:slots].astype(jnp.float32) + received.astype(jnp.float32)).astype(jnp.bfloat16)
-    returned = lax.all_to_all(
-        summed.reshape(exp_count, capacity, -1), "exp", split_axis=0, concat_axis=0, tiled=True
-    ).reshape(slots, -1)
-    weight_grads = lax.psum_scatter(local, "rh", scatter_dimension=1, tiled=True)
+    grad_gate = lax.psum_scatter(
+        jnp.dot(d_gate.T, rows, preferred_element_type=jnp.float32)[None], "rh", scatter_dimension=1, tiled=True
+    )
+    grad_up = lax.psum_scatter(
+        jnp.dot(d_up.T, rows, preferred_element_type=jnp.float32)[None], "rh", scatter_dimension=1, tiled=True
+    )
+    mine = packed[:slots].reshape(exp_count, capacity, -1)
+    theirs = packed[slots:].reshape(exp_count, capacity, -1)
+    half = capacity // 2
+    pieces = []
+    for lo, hi in ((0, half), (half, capacity)):
+        received = swap_pair(theirs[:, lo:hi])
+        summed = (mine[:, lo:hi].astype(jnp.float32) + received.astype(jnp.float32)).astype(jnp.bfloat16)
+        pieces.append(lax.all_to_all(summed, "exp", split_axis=0, concat_axis=0, tiled=True))
+    returned = jnp.concatenate(pieces, axis=1).reshape(slots, -1)
 
     grad_tokens = jnp.dot(
         token_routing.T, returned[:, :width], preferred_element_type=jnp.float32
@@ -86,7 +92,7 @@
     grad_probs = jnp.dot(
         routing.T, returned[:, width : width + 1], preferred_element_type=jnp.float32
     ).reshape(token_count, 2)
-    return (grad_tokens, grad_probs, weight_grads[0:1], weight_grads[1:2], weight_grads[2:3])
+    return (grad_tokens, grad_probs, grad_gate, grad_up, grad_down)
 
 
 def solution(mesh):

time: 406 us -> 523 us (1.29)
  waiting for transfers between devices: 218 us -> 352 us
  blocking collectives: 99.6 us -> 50.6 us
  starting transfers between devices: 23.2 us -> 38.3 us
  matrix products: 18.9 us -> 29 us
  local copies, waits for them, and re-layouts: 23.4 us -> 30 us
    reduce_scatter x1 -> x3, waiting for transfers between devices: 0.01 us -> 115 us  [the longest x1 96.2 us: shards(): lax.psum_scatter(jnp.dot(d_up.T, rows, preferred_element_type=jnp.float32...]
    all_to_all x1, blocking collectives: 99.6 us -> 50.6 us  [shards(): lax.all_to_all(summed, 'exp', split_axis=0, concat_axis=0, tiled=True)]
    all_to_all x1 -> x3, waiting for transfers between devices: 144 us -> 188 us  [the longest x1 78 us: shards(): lax.all_to_all(send_t, 'exp', split_axis=0, concat_axis=0, tiled=True)]
    ppermute x2 -> x4, waiting for transfers between devices: 74.1 us -> 48.6 us  [swap_pair(): return lax.ppermute(value, 'rl', [(0, 1), (1, 0)])]
    all_to_all x1 -> x3, starting transfers between devices: 16.9 us -> 26.5 us  [the longest x1 16.9 us: shards(): lax.all_to_all(send_g, 'exp', split_axis=0, concat_axis=0, tiled=True)]
    ppermute x2 -> x4, starting transfers between devices: 6.24 us -> 11.7 us  [swap_pair(): return lax.ppermute(value, 'rl', [(0, 1), (1, 0)])]
    dot_general x4 -> x5, matrix products: 6.31 us -> 11 us  [the longest x1 4.21 us: shards(): jnp.dot(d_up.T, rows, preferred_element_type=jnp.float32)[None]]
  transfers between devices with their start and end apart: 5 -> 11, of which waited for: 3 -> 8; matrix products, arithmetic and copies ran while one was open for 5% -> 9% of each run, Pallas kernels for 0% -> 0%
where the time goes in v2:
time: 523 us; the launch traced here: 521 us
  waiting for transfers between devices  352 us (67%)
  blocking collectives  50.6 us (10%)
  starting transfers between devices  38.3 us (7%)
  local copies, waits for them, and re-layouts  30 us (6%)
  matrix products  29 us (6%)
  between operations  14.2 us (3%)
  other arithmetic  6.84 us (1%)
    reduce_scatter x1, waiting for transfers between devices, shards(): lax.psum_scatter(jnp.dot(d_up.T, rows, preferred_element_type=jnp.float32...  96.2 us
    all_to_all x1, waiting for transfers between devices, shards(): lax.all_to_all(send_t, 'exp', split_axis=0, concat_axis=0, tiled=True)  78 us
    all_to_all x1, waiting for transfers between devices, shards(): lax.all_to_all(send_g, 'exp', split_axis=0, concat_axis=0, tiled=True)  67.2 us
    all_to_all x1, blocking collectives, shards(): lax.all_to_all(summed, 'exp', split_axis=0, concat_axis=0, tiled=True)  50.6 us
    ppermute x4, waiting for transfers between devices, swap_pair(): return lax.ppermute(value, 'rl', [(0, 1), (1, 0)])  48.6 us
    all_to_all x1, waiting for transfers between devices, shards(): lax.all_to_all(summed, 'exp', split_axis=0, concat_axis=0, tiled=True)  43.1 us
    reduce_scatter x1, waiting for transfers between devices, shards(): lax.psum_scatter(jnp.dot(d_gate.T, rows, preferred_element_type=jnp.float...  18.8 us
    all_to_all x1, starting transfers between devices, shards(): lax.all_to_all(send_g, 'exp', split_axis=0, concat_axis=0, tiled=True)  16.9 us
  transfers between devices with their start and end apart: 11, of which 8 were waited for; matrix products, arithmetic and copies ran while one was open for 9% of the time, Pallas kernels for 0%

profile of v2, /device:TPU:1, one launch (start us, length us, event | category | flops | bytes accessed | tf_op | source)
XLA Modules:
  0.0 521.0 jit_solution(11480015289239463388)
XLA Ops:
  7.2 0.8 copy.50
  10.6 1.3 reshape.114
  12.0 16.9 %all-to-all-start.1 = ((bf16[32,10,1536]{2,1,0:T(8,128)(2,1)}), bf16[32,10,1536]{2,1,0:T(8,128)(2,1)S(1)}, u32[]{:S(2)}, u32[]{:S(2)}) async-start(bf16[32,10,1536]{2,1,0:T(8,128)(2,1)} %reshape.114), calls=%async_computation.1 | async-start | bytes 3145728 | tf_op jit(solution)/shard_map/all_to_all | solution.py:35
  28.9 0.8 pad_maximum_fusion.1
  29.8 1.3 convolution_convert_fusion.1
  31.2 1.4 concatenate.23
  32.6 0.7 copy.54
  33.3 0.9 reshape.121
  34.4 0.9 concatenate.31
  36.0 3.3 concatenate.25
  39.3 67.2 %all-to-all-done.1 = bf16[32,10,1536]{2,1,0:T(8,128)(2,1)S(1)} async-done(((bf16[32,10,1536]{2,1,0:T(8,128)(2,1)}), bf16[32,10,1536]{2,1,0:T(8,128)(2,1)S(1)}, u32[]{:S(2)}, u32[]{:S(2)}) %all-to-all-start.1) | async-done | bytes 983072 | tf_op jit(solution)/shard_map/all_to_all | solution.py:35
  106.5 1.2 copy-done.1
  107.7 4.4 all-to-all-start
  112.1 2.3 reshape.115
  114.5 3.1 collective-permute-start.1
  117.6 78.0 %all-to-all-done = bf16[32,10,1664]{2,1,0:T(8,128)(2,1)S(1)} async-done(((bf16[32,10,1664]{2,1,0:T(8,128)(2,1)}), bf16[32,10,1664]{2,1,0:T(8,128)(2,1)S(1)}, u32[]{:S(2)}, u32[]{:S(2)}) %all-to-all-start) | async-done | bytes 1064992 | tf_op jit(solution)/shard_map/all_to_all | solution.py:33
  195.9 3.1 collective-permute-start
  199.1 1.3 constant_dynamic-update-slice_fusion.3
  200.4 1.3 constant_dynamic-update-slice_fusion.2
  201.7 19.7 %collective-permute-done = bf16[320,1664]{1,0:T(8,128)(2,1)S(1)} collective-permute-done((bf16[320,1664]{1,0:T(8,128)(2,1)S(1)}, bf16[320,1664]{1,0:T(8,128)(2,1)S(1)}, u32[]{:S(2)}, u32[]{:S(2)}) %collective-permute-start) | collective-permute-done | bytes 1064992 | tf_op jit(solution)/shard_map/ppermute | solution.py:11
  221.6 1.4 copy-done.6
  223.2 3.1 fusion.2
  226.3 2.8 fusion.4
  229.1 0.9 copy-done.17
  230.1 2.5 convolution_bitcast_fusion
  232.7 3.8 multiply_reduce_fusion
  236.5 2.5 convolution_bitcast_fusion.2
  239.2 2.5 fusion.7
  241.6 3.8 add_convert_fusion
  245.5 3.3 concatenate.29
  248.8 1.5 fusion.24
  250.3 1.4 reshape.117
  252.0 0.8 copy.57
  252.8 3.1 collective-permute-start.2
  256.0 0.9 copy.59
  256.8 2.3 collective-permute-start.3
  259.6 13.1 %collective-permute-done.2 = bf16[32,5,1664]{2,0,1:T(8,128)(2,1)} collective-permute-done((bf16[32,5,1664]{2,0,1:T(8,128)(2,1)}, bf16[32,5,1664]{2,0,1:T(8,128)(2,1)}, u32[]{:S(2)}, u32[]{:S(2)}) %collective-permute-start.2) | collective-permute-done | bytes 532512 | tf_op jit(solution)/shard_map/ppermute | solution.py:11
  272.6 15.9 %collective-permute-done.3 = bf16[32,5,1664]{2,0,1:T(8,128)(2,1)} collective-permute-done((bf16[32,5,1664]{2,0,1:T(8,128)(2,1)}, bf16[32,5,1664]{2,0,1:T(8,128)(2,1)}, u32[]{:S(2)}, u32[]{:S(2)}) %collective-permute-start.3) | collective-permute-done | bytes 532512 | tf_op jit(solution)/shard_map/ppermute | solution.py:11
  288.5 2.7 add_convert_fusion.2
  291.2 5.2 all-to-all-start.2
  296.4 4.2 convolution_bitcast_fusion.1
  300.6 43.1 %all-to-all-done.2 = bf16[32,5,1664]{2,1,0:T(8,128)(2,1)S(1)} async-done(((bf16[32,5,1664]{2,1,0:T(8,128)(2,1)}), bf16[32,5,1664]{2,1,0:T(8,128)(2,1)S(1)}, u32[]{:S(2)}, u32[]{:S(2)}) %all-to-all-start.2) | async-done | bytes 532512 | tf_op jit(solution)/shard_map/all_to_all | solution.py:86
  343.7 0.9 copy-done.3
  344.7 50.6 %all_to_all.20 = bf16[32,5,1664]{2,1,0:T(8,128)(2,1)S(1)} all-to-all(bf16[32,5,1664]{2,1,0:T(8,128)(2,1)S(1)} %get-tuple-element.11), channel_id=1, replica_groups=mesh['exp'=32,'rh'=8,'rl'=2] {'exp'}, dimensions={0} | all-to-all | bytes 1064960 | tf_op jit(solution)/shard_map/all_to_all | solution.py:86
  395.3 1.7 pad_maximum_fusion
  398.3 1.1 convolution_convert_fusion.2
  399.4 18.8 %reduce-scatter.4.cloned.1.call-done = f32[1,48,1536]{2,1,0:T(8,128)} async-done(((f32[1,384,1536]{2,1,0:T(8,128)}), f32[1,48,1536]{2,1,0:T(8,128)}) %reduce-scatter.4.cloned.1.call-update) | async-done | bytes 294928 | tf_op jit(solution)/shard_map/reduce_scatter | solution.py:73
  418.3 96.2 %reduce-scatter.6.cloned.1.call-done = f32[1,48,1536]{2,1,0:T(8,128)} async-done(((f32[1,384,1536]{2,1,0:T(8,128)}), f32[1,48,1536]{2,1,0:T(8,128)}) %reduce-scatter.6.cloned.1.call-update) | async-done | bytes 294928 | tf_op jit(solution)/shard_map/reduce_scatter | solution.py:76
  (71 shorter events, 6.6 us)
Async XLA Ops:
  7.2 3.0 copy-start
  10.2 19.6 %copy-start.4 = (bf16[320,128]{1,0:T(8,128)(2,1)}, bf16[320,128]{1,0:T(8,128)(2,1)S(1)}, u32[]{:S(2)}) copy-start(bf16[320,128]{1,0:T(8,128)(2,1)S(1)} %fusion.17) | copy-start | bytes 245764
  11.9 17.0 %copy-start.12 = (bf16[1,48,1536]{2,1,0:T(8,128)(2,1)S(1)}, bf16[1,48,1536]{2,1,0:T(8,128)(2,1)}, u32[]{:S(2)}) copy-start(bf16[1,48,1536]{2,1,0:T(8,128)(2,1)} %param.13) | copy-start | bytes 442372
  11.9 17.0 %copy-start.13 = (bf16[1,48,1536]{2,1,0:T(8,128)(2,1)S(1)}, bf16[1,48,1536]{2,1,0:T(8,128)(2,1)}, u32[]{:S(2)}) copy-start(bf16[1,48,1536]{2,1,0:T(8,128)(2,1)} %param.12) | copy-start | bytes 442372
  12.0 17.0 %copy-start.14 = (bf16[1,48,1536]{2,1,0:T(8,128)(2,1)S(1)}, bf16[1,48,1536]{2,1,0:T(8,128)(2,1)}, u32[]{:S(2)}) copy-start(bf16[1,48,1536]{2,1,0:T(8,128)(2,1)} %param.11) | copy-start | bytes 442372
  12.0 17.9 %copy-start.11 = (bf16[128,1536]{1,0:T(8,128)(2,1)S(1)}, bf16[128,1536]{1,0:T(8,128)(2,1)}, u32[]{:S(2)}) copy-start(bf16[128,1536]{1,0:T(8,128)(2,1)} %param.7) | copy-start | bytes 1179652
  12.0 94.5 %all-to-all-start.1 = ((bf16[32,10,1536]{2,1,0:T(8,128)(2,1)}), bf16[32,10,1536]{2,1,0:T(8,128)(2,1)S(1)}, u32[]{:S(2)}, u32[]{:S(2)}) async-start(bf16[32,10,1536]{2,1,0:T(8,128)(2,1)} %reshape.114), calls=%async_computation.1 | async-start | bytes 3145728 | tf_op jit(solution)/shard_map/all_to_all | solution.py:35
  28.8 194.3 %all-gather.2.cloned.1.call-start = ((), (), s32[]{:S(2)}) async-start(), calls=%async_computation.7 | async-start | bytes 3981312 | tf_op jit(solution)/shard_map/all_gather | solution.py:40
  29.8 2.7 copy-start.15
  106.5 1.2 copy-start.1
  107.7 87.9 %all-to-all-start = ((bf16[32,10,1664]{2,1,0:T(8,128)(2,1)}), bf16[32,10,1664]{2,1,0:T(8,128)(2,1)S(1)}, u32[]{:S(2)}, u32[]{:S(2)}) async-start(bf16[32,10,1664]{2,1,0:T(8,128)(2,1)} %concatenate.25), calls=%async_computation | async-start | bytes 3407872 | tf_op jit(solution)/shard_map/all_to_all | solution.py:33
  112.1 287.3 %reduce-scatter.8.cloned.1.call-start = ((), (), s32[]{:S(2)}) async-start(), calls=%async_computation.10 | async-start | bytes 2654208 | tf_op jit(solution)/shard_map/reduce_scatter | solution.py:70
  114.5 86.0 %collective-permute-start.1 = (bf16[320,1536]{1,0:T(8,128)(2,1)}, bf16[320,1536]{1,0:T(8,128)(2,1)}, u32[]{:S(2)}, u32[]{:S(2)}) collective-permute-start(bf16[320,1536]{1,0:T(8,128)(2,1)} %reshape.115), channel_id=1, source_target_pairs={{0,1},{1,0},{2,3},{3,2},{4,5},{5,4},{6,7},{7,6},{8,9},{9,8},{10,11... | collective-permute-start | bytes 2949128 | tf_op jit(solution)/shard_map/ppermute | solution.py:11
  195.9 25.5 %collective-permute-start = (bf16[320,1664]{1,0:T(8,128)(2,1)S(1)}, bf16[320,1664]{1,0:T(8,128)(2,1)S(1)}, u32[]{:S(2)}, u32[]{:S(2)}) collective-permute-start(bf16[320,1664]{1,0:T(8,128)(2,1)S(1)} %reshape.113), channel_id=1, source_target_pairs={{0,1},{1,0},{2,3},{3,2},{4,5},{5,4},{6,7},{7,6},{8,9},{9,8},{10,11... | collective-permute-start | bytes 3194888 | tf_op jit(solution)/shard_map/ppermute | solution.py:11
  201.7 19.9 %copy-start.8 = (bf16[640,1536]{1,0:T(8,128)(2,1)}, bf16[640,1536]{1,0:T(8,128)(2,1)S(1)}, u32[]{:S(2)}) copy-start(bf16[640,1536]{1,0:T(8,128)(2,1)S(1)} %constant_dynamic-update-slice_fusion.2) | copy-start | bytes 5898244
  221.6 1.4 copy-start.6
  223.1 3.2 copy-start.7
  226.3 2.8 copy-start.16
  226.3 3.8 copy-start.9
  229.1 1.0 copy-start.17
  232.6 185.6 %reduce-scatter.4.cloned.1.call-start = ((), (), s32[]{:S(2)}) async-start(), calls=%async_computation.8 | async-start | bytes 2654208 | tf_op jit(solution)/shard_map/reduce_scatter | solution.py:73
  236.5 5.2 copy-start.10
  252.0 7.2 %copy-start.2 = (bf16[320,1664]{1,0:T(8,128)(2,1)S(1)}, bf16[320,1664]{1,0:T(8,128)(2,1)}, u32[]{:S(2)}) copy-start(bf16[320,1664]{1,0:T(8,128)(2,1)} %get-tuple-element.8) | copy-start | bytes 3194884
  252.8 19.8 %collective-permute-start.2 = (bf16[32,5,1664]{2,0,1:T(8,128)(2,1)}, bf16[32,5,1664]{2,0,1:T(8,128)(2,1)}, u32[]{:S(2)}, u32[]{:S(2)}) collective-permute-start(bf16[32,5,1664]{2,0,1:T(8,128)(2,1)} %copy.57), channel_id=1, source_target_pairs={{0,1},{1,0},{2,3},{3,2},{4,5},{5,4},{6,7},{7,6},{8,9},{9,8},{10,11... | collective-permute-start | bytes 1597448 | tf_op jit(solution)/shard_map/ppermute | solution.py:11
  256.8 31.7 %collective-permute-start.3 = (bf16[32,5,1664]{2,0,1:T(8,128)(2,1)}, bf16[32,5,1664]{2,0,1:T(8,128)(2,1)}, u32[]{:S(2)}, u32[]{:S(2)}) collective-permute-start(bf16[32,5,1664]{2,0,1:T(8,128)(2,1)} %copy.59), channel_id=1, source_target_pairs={{0,1},{1,0},{2,3},{3,2},{4,5},{5,4},{6,7},{7,6},{8,9},{9,8},{10,11... | collective-permute-start | bytes 1597448 | tf_op jit(solution)/shard_map/ppermute | solution.py:11
  291.2 52.6 %all-to-all-start.2 = ((bf16[32,5,1664]{2,1,0:T(8,128)(2,1)}), bf16[32,5,1664]{2,1,0:T(8,128)(2,1)S(1)}, u32[]{:S(2)}, u32[]{:S(2)}) async-start(bf16[32,5,1664]{2,1,0:T(8,128)(2,1)} %get-tuple-element.10), calls=%async_computation.2 | async-start | bytes 1703936 | tf_op jit(solution)/shard_map/all_to_all | solution.py:86
  296.4 218.1 %reduce-scatter.6.cloned.1.call-start = ((), (), s32[]{:S(2)}) async-start(), calls=%async_computation.9 | async-start | bytes 2654208 | tf_op jit(solution)/shard_map/reduce_scatter | solution.py:76
  343.7 0.9 copy-start.3
  397.0 1.3 copy-start.5
Sparse Core Ops, SparseCore 0:
  32.9 80.9 all-gather.1
  232.7 89.0 reduce-scatter.7
  327.1 91.1 reduce-scatter.3
  423.3 91.0 reduce-scatter.5

commit v3 on v2

--- a/solution.py
+++ b/solution.py
@@ -11,10 +11,18 @@
     return lax.ppermute(value, "rl", [(0, 1), (1, 0)])
 
 
+def exchange(blocks):
+    shape = blocks.shape
+    split = blocks.reshape((lax.axis_size("ez"), lax.axis_size("ec")) + shape[1:])
+    split = lax.all_to_all(split, "ez", split_axis=0, concat_axis=0, tiled=True)
+    split = lax.all_to_all(split, "ec", split_axis=1, concat_axis=1, tiled=True)
+    return split.reshape(shape)
+
+
 def shards(tokens, grad_out, expert_ids, probs, w_gate, w_up, w_down):
     token_count = tokens.shape[0]
     width = tokens.shape[1]
-    exp_count = lax.axis_size("exp")
+    exp_count = lax.axis_size("ez") * lax.axis_size("ec")
     capacity = 5 * token_count // (2 * exp_count)
     slots = exp_count * capacity
     chosen = expert_ids.reshape(-1)
@@ -30,9 +38,9 @@
     slot_probs = jnp.dot(routing, prob_pairs, preferred_element_type=jnp.float32).astype(jnp.bfloat16)
     prob_block = jnp.concatenate([slot_probs, jnp.zeros((slots, LANE - 1), jnp.bfloat16)], axis=1)
     send_t = jnp.concatenate([slot_tokens, prob_block], axis=1).reshape(exp_count, capacity, -1)
-    arrived_t = lax.all_to_all(send_t, "exp", split_axis=0, concat_axis=0, tiled=True).reshape(slots, -1)
+    arrived_t = exchange(send_t).reshape(slots, -1)
     send_g = slot_grads.reshape(exp_count, capacity, -1)
-    arrived_g = lax.all_to_all(send_g, "exp", split_axis=0, concat_axis=0, tiled=True).reshape(slots, -1)
+    arrived_g = exchange(send_g).reshape(slots, -1)
     joined_t = jnp.concatenate([arrived_t, swap_pair(arrived_t)], axis=0)
     joined_g = jnp.concatenate([arrived_g, swap_pair(arrived_g)], axis=0)
 
@@ -67,15 +75,14 @@
         ],
         axis=1,
     )
-    grad_down = lax.psum_scatter(
-        jnp.dot(weighted.T, grads, preferred_element_type=jnp.float32)[None], "rh", scatter_dimension=1, tiled=True
+    local = jnp.stack(
+        [
+            jnp.dot(d_gate.T, rows, preferred_element_type=jnp.float32),
+            jnp.dot(d_up.T, rows, preferred_element_type=jnp.float32),
+            jnp.dot(weighted.T, grads, preferred_element_type=jnp.float32),
+        ]
     )
-    grad_gate = lax.psum_scatter(
-        jnp.dot(d_gate.T, rows, preferred_element_type=jnp.float32)[None], "rh", scatter_dimension=1, tiled=True
-    )
-    grad_up = lax.psum_scatter(
-        jnp.dot(d_up.T, rows, preferred_element_type=jnp.float32)[None], "rh", scatter_dimension=1, tiled=True
-    )
+    weight_grads = lax.psum_scatter(local, "rh", scatter_dimension=1, tiled=True)
     mine = packed[:slots].reshape(exp_count, capacity, -1)
     theirs = packed[slots:].reshape(exp_count, capacity, -1)
     half = capacity // 2
@@ -83,7 +90,7 @@
     for lo, hi in ((0, half), (half, capacity)):
         received = swap_pair(theirs[:, lo:hi])
         summed = (mine[:, lo:hi].astype(jnp.float32) + received.astype(jnp.float32)).astype(jnp.bfloat16)
-        pieces.append(lax.all_to_all(summed, "exp", split_axis=0, concat_axis=0, tiled=True))
+        pieces.append(exchange(summed))
     returned = jnp.concatenate(pieces, axis=1).reshape(slots, -1)
 
     grad_tokens = jnp.dot(
@@ -92,15 +99,15 @@
     grad_probs = jnp.dot(
         routing.T, returned[:, width : width + 1], preferred_element_type=jnp.float32
     ).reshape(token_count, 2)
-    return (grad_tokens, grad_probs, grad_gate, grad_up, grad_down)
+    return (grad_tokens, grad_probs, weight_grads[0:1], weight_grads[1:2], weight_grads[2:3])
 
 
 def solution(mesh):
     exp_count = mesh.shape["exp"]
     rep_count = mesh.shape["rep"]
-    view = Mesh(mesh.devices.reshape(exp_count, rep_count // 2, 2), ("exp", "rh", "rl"))
-    rows_spec = P(("exp", "rh", "rl"), None)
-    weight_spec = P("exp", ("rh", "rl"), None)
+    view = Mesh(mesh.devices.reshape(exp_count // 2, 2, rep_count // 2, 2), ("ez", "ec", "rh", "rl"))
+    rows_spec = P(("ez", "ec", "rh", "rl"), None)
+    weight_spec = P(("ez", "ec"), ("rh", "rl"), None)
     in_specs = (rows_spec,) * 4 + (weight_spec,) * 3
     out_specs = (rows_spec, rows_spec, weight_spec, weight_spec, weight_spec)
     return jax.shard_map(shards, mesh=view, in_specs=in_specs, out_specs=out_specs, check_vma=False)

time: 523 us -> 343 us (0.66)
  waiting for transfers between devices: 352 us -> 173 us
  matrix products: 29 us -> 18 us
  starting transfers between devices: 38.3 us -> 48.8 us
  blocking collectives: 50.6 us -> 42.4 us
    reduce_scatter x3 -> x1, waiting for transfers between devices: 115 us -> 0.01 us  [shards(): lax.psum_scatter(local, 'rh', scatter_dimension=1, tiled=True)]
    all_to_all x3 -> x4, waiting for transfers between devices: 188 us -> 118 us  [exchange(): split = lax.all_to_all(split, 'ez', split_axis=0, concat_axis=0, tiled=True)]
    all_to_all x3 -> x4, starting transfers between devices: 26.5 us -> 37.1 us  [exchange(): split = lax.all_to_all(split, 'ez', split_axis=0, concat_axis=0, tiled=True)]
    all_to_all x1 -> x4, blocking collectives: 50.6 us -> 42.4 us  [exchange(): split = lax.all_to_all(split, 'ec', split_axis=1, concat_axis=1, tiled=True)]
    ppermute x4, waiting for transfers between devices: 48.6 us -> 55.3 us  [swap_pair(): return lax.ppermute(value, 'rl', [(0, 1), (1, 0)])]
    dot_general x3, matrix products: 9.24 us -> 3.26 us  [the longest x1 1.1 us: shards(): jnp.dot(weighted.T, grads, preferred_element_type=jnp.float32)]
  transfers between devices with their start and end apart: 11 -> 10, of which waited for: 8 -> 7; matrix products, arithmetic and copies ran while one was open for 9% -> 11% of each run, Pallas kernels for 0% -> 0%
where the time goes in v3:
time: 343 us; the launch traced here: 340 us
  waiting for transfers between devices  173 us (50%)
  starting transfers between devices  48.8 us (14%)
  blocking collectives  42.4 us (12%)
  local copies, waits for them, and re-layouts  34.4 us (10%)
  matrix products  18 us (5%)
  between operations  14.6 us (4%)
  other arithmetic  7.78 us (2%)
    all_to_all x4, waiting for transfers between devices, exchange(): split = lax.all_to_all(split, 'ez', split_axis=0, concat_axis=0, tiled=True)  118 us
    ppermute x4, waiting for transfers between devices, swap_pair(): return lax.ppermute(value, 'rl', [(0, 1), (1, 0)])  55.3 us
    all_to_all x4, blocking collectives, exchange(): split = lax.all_to_all(split, 'ec', split_axis=1, concat_axis=1, tiled=True)  42.4 us
    all_to_all x4, starting transfers between devices, exchange(): split = lax.all_to_all(split, 'ez', split_axis=0, concat_axis=0, tiled=True)  37.1 us
    ppermute x4, starting transfers between devices, swap_pair(): return lax.ppermute(value, 'rl', [(0, 1), (1, 0)])  11.7 us
  transfers between devices with their start and end apart: 10, of which 7 were waited for; matrix products, arithmetic and copies ran while one was open for 11% of the time, Pallas kernels for 0%

profile of v3, /device:TPU:1, one launch (start us, length us, event | category | flops | bytes accessed | tf_op | source)
XLA Modules:
  0.0 339.6 jit_solution(5337200922584595419)
XLA Ops:
  7.2 0.8 copy.99
  11.0 1.9 copy.108
  13.0 15.9 %all-to-all-start.2 = ((bf16[16,2,10,1536]{3,1,2,0:T(2,128)(2,1)}), bf16[16,2,10,1536]{3,1,2,0:T(2,128)(2,1)S(1)}, u32[]{:S(2)}, u32[]{:S(2)}) async-start(bf16[16,2,10,1536]{3,1,2,0:T(2,128)(2,1)} %copy.108), calls=%async_computation.2 | async-start | bytes 1966080 | tf_op jit(solution)/shard_map/all_to_all | solution.py:17
  30.2 1.3 concatenate.23
  32.3 2.4 concatenate.25
  34.7 1.8 copy.105
  36.5 35.1 %all-to-all-done.2 = bf16[16,2,10,1536]{3,1,2,0:T(2,128)(2,1)S(1)} async-done(((bf16[16,2,10,1536]{3,1,2,0:T(2,128)(2,1)}), bf16[16,2,10,1536]{3,1,2,0:T(2,128)(2,1)S(1)}, u32[]{:S(2)}, u32[]{:S(2)}) %all-to-all-start.2) | async-done | bytes 983072 | tf_op jit(solution)/shard_map/all_to_all | solution.py:17
  71.7 10.5 %all_to_all.40 = bf16[16,2,10,1536]{3,0,2,1:T(8,128)(2,1)} all-to-all(bf16[16,2,10,1536]{3,0,2,1:T(8,128)(2,1)S(1)} %copy.109), channel_id=1, replica_groups=mesh['ez'=16,'ec'=2,'rh'=8,'rl'=2] {'ec'}, dimensions={1} | all-to-all | bytes 1966080 | tf_op jit(solution)/shard_map/all_to_all | solution.py:18
  82.3 7.5 %all-to-all-start = ((bf16[16,2,10,1664]{3,1,2,0:T(2,128)(2,1)}), bf16[16,2,10,1664]{3,1,2,0:T(2,128)(2,1)S(1)}, u32[]{:S(2)}, u32[]{:S(2)}) async-start(bf16[16,2,10,1664]{3,1,2,0:T(2,128)(2,1)} %copy.105), calls=%async_computation | async-start | bytes 2129920 | tf_op jit(solution)/shard_map/all_to_all | solution.py:17
  89.8 1.8 copy.110
  91.6 1.2 reshape_reshape.12
  92.8 3.1 collective-permute-start.1
  95.9 39.9 %all-to-all-done = bf16[16,2,10,1664]{3,1,2,0:T(2,128)(2,1)S(1)} async-done(((bf16[16,2,10,1664]{3,1,2,0:T(2,128)(2,1)}), bf16[16,2,10,1664]{3,1,2,0:T(2,128)(2,1)S(1)}, u32[]{:S(2)}, u32[]{:S(2)}) %all-to-all-start) | async-done | bytes 1064992 | tf_op jit(solution)/shard_map/all_to_all | solution.py:17
  135.9 9.6 %all_to_all.41 = bf16[16,2,10,1664]{3,0,2,1:T(8,128)(2,1)S(1)} all-to-all(bf16[16,2,10,1664]{3,0,2,1:T(8,128)(2,1)S(1)} %copy.106), channel_id=1, replica_groups=mesh['ez'=16,'ec'=2,'rh'=8,'rl'=2] {'ec'}, dimensions={1} | all-to-all | bytes 2129920 | tf_op jit(solution)/shard_map/all_to_all | solution.py:18
  146.2 3.3 collective-permute-start
  149.5 1.3 constant_dynamic-update-slice_fusion.3
  150.8 1.3 constant_dynamic-update-slice_fusion.2
  152.1 20.6 %collective-permute-done = bf16[320,1664]{1,0:T(8,128)(2,1)S(1)} collective-permute-done((bf16[320,1664]{1,0:T(8,128)(2,1)S(1)}, bf16[320,1664]{1,0:T(8,128)(2,1)S(1)}, u32[]{:S(2)}, u32[]{:S(2)}) %collective-permute-start) | collective-permute-done | bytes 1064992 | tf_op jit(solution)/shard_map/ppermute | solution.py:11
  172.9 1.3 copy-done.4
  174.5 3.1 fusion.4
  178.0 1.1 fusion.2
  179.6 1.1 convolution_bitcast_fusion
  180.7 1.4 multiply_reduce_fusion
  182.0 1.1 convolution_bitcast_fusion.1
  183.1 1.1 convolution_bitcast_fusion.2
  184.2 3.5 %pad_maximum_fusion = f32[3,384,1536]{2,1,0:T(8,128)} fusion(f32[1,384,1536]{2,1,0:T(8,128)S(1)} %convolution_bitcast_fusion, f32[1,384,1536]{2,1,0:T(8,128)S(1)} %convolution_bitcast_fusion.1, f32[1,384,1536]{2,1,0:T(8,128)S(1)} %convolution_bitcast_fusion.2), kind=kLoop, calls=%fused_computation | loop fusion | flops 3538944 | bytes 14155776 | tf_op jit(solution)/shard_map/stack | solution.py:78
  187.9 2.5 fusion.7
  190.4 3.8 %add_convert_fusion = bf16[640,1536]{1,0:T(8,128)(2,1)} fusion(f32[640,1536]{1,0:T(8,128)S(1)} %fusion.7, bf16[640,384]{0,1:T(8,128)(2,1)S(1)} %copy-done.9, bf16[3,384,1536]{2,1,0:T(8,128)(2,1)} %all-gather.2.cloned.1.call-done), kind=kOutput, calls=%fused_computation.1 | convolution fusion | flops 756940800 | bytes 7569408 | tf_op jit(solution)/shard_map/dot_general | solution.py:66
  194.3 3.3 concatenate.29
  197.6 1.5 fusion.24
  199.1 1.4 reshape.116
  200.8 0.9 copy.112
  201.8 3.1 collective-permute-start.2
  204.9 0.9 copy.117
  205.7 2.2 collective-permute-start.3
  208.3 16.9 %collective-permute-done.2 = bf16[32,5,1664]{2,0,1:T(8,128)(2,1)} collective-permute-done((bf16[32,5,1664]{2,0,1:T(8,128)(2,1)}, bf16[32,5,1664]{2,0,1:T(8,128)(2,1)}, u32[]{:S(2)}, u32[]{:S(2)}) %collective-permute-start.2) | collective-permute-done | bytes 532512 | tf_op jit(solution)/shard_map/ppermute | solution.py:11
  225.2 17.7 %collective-permute-done.3 = bf16[32,5,1664]{2,0,1:T(8,128)(2,1)} collective-permute-done((bf16[32,5,1664]{2,0,1:T(8,128)(2,1)}, bf16[32,5,1664]{2,0,1:T(8,128)(2,1)}, u32[]{:S(2)}, u32[]{:S(2)}) %collective-permute-start.3) | collective-permute-done | bytes 532512 | tf_op jit(solution)/shard_map/ppermute | solution.py:11
  242.9 1.8 add_convert_fusion.2
  244.7 1.2 copy.119
  245.9 6.9 %all-to-all-start.6 = ((bf16[16,2,5,1664]{3,1,2,0:T(2,128)(2,1)}), bf16[16,2,5,1664]{3,1,2,0:T(2,128)(2,1)S(1)}, u32[]{:S(2)}, u32[]{:S(2)}) async-start(bf16[16,2,5,1664]{3,1,2,0:T(2,128)(2,1)} %copy.119), calls=%async_computation.6 | async-start | bytes 1064960 | tf_op jit(solution)/shard_map/all_to_all | solution.py:17
  252.9 1.2 copy.114
  254.1 20.7 %all-to-all-done.6 = bf16[16,2,5,1664]{3,1,2,0:T(2,128)(2,1)S(1)} async-done(((bf16[16,2,5,1664]{3,1,2,0:T(2,128)(2,1)}), bf16[16,2,5,1664]{3,1,2,0:T(2,128)(2,1)S(1)}, u32[]{:S(2)}, u32[]{:S(2)}) %all-to-all-start.6) | async-done | bytes 532512 | tf_op jit(solution)/shard_map/all_to_all | solution.py:17
  274.9 11.4 %all_to_all.42 = bf16[16,2,5,1664]{3,0,2,1:T(8,128)(2,1)S(1)} all-to-all(bf16[16,2,5,1664]{3,0,2,1:T(8,128)(2,1)S(1)} %copy.120), channel_id=1, replica_groups=mesh['ez'=16,'ec'=2,'rh'=8,'rl'=2] {'ec'}, dimensions={1} | all-to-all | bytes 1064960 | tf_op jit(solution)/shard_map/all_to_all | solution.py:18
  286.3 6.8 %all-to-all-start.4 = ((bf16[16,2,5,1664]{3,1,2,0:T(2,128)(2,1)}), bf16[16,2,5,1664]{3,1,2,0:T(2,128)(2,1)S(1)}, u32[]{:S(2)}, u32[]{:S(2)}) async-start(bf16[16,2,5,1664]{3,1,2,0:T(2,128)(2,1)} %copy.114), calls=%async_computation.4 | async-start | bytes 1064960 | tf_op jit(solution)/shard_map/all_to_all | solution.py:17
  293.7 22.4 %all-to-all-done.4 = bf16[16,2,5,1664]{3,1,2,0:T(2,128)(2,1)S(1)} async-done(((bf16[16,2,5,1664]{3,1,2,0:T(2,128)(2,1)}), bf16[16,2,5,1664]{3,1,2,0:T(2,128)(2,1)S(1)}, u32[]{:S(2)}, u32[]{:S(2)}) %all-to-all-start.4) | async-done | bytes 532512 | tf_op jit(solution)/shard_map/all_to_all | solution.py:17
  316.2 10.9 %all_to_all.43 = bf16[16,2,5,1664]{3,0,2,1:T(8,128)(2,1)S(1)} all-to-all(bf16[16,2,5,1664]{3,0,2,1:T(8,128)(2,1)S(1)} %copy.115), channel_id=1, replica_groups=mesh['ez'=16,'ec'=2,'rh'=8,'rl'=2] {'ec'}, dimensions={1} | all-to-all | bytes 1064960 | tf_op jit(solution)/shard_map/all_to_all | solution.py:18
  329.5 1.1 convolution_convert_fusion.2
  330.6 2.1 fusion.26
  (81 shorter events, 11.1 us)
Async XLA Ops:
  7.2 3.0 copy-start
  11.0 17.9 %copy-start.11 = (bf16[1,48,1536]{2,1,0:T(8,128)(2,1)S(1)}, bf16[1,48,1536]{2,1,0:T(8,128)(2,1)}, u32[]{:S(2)}) copy-start(bf16[1,48,1536]{2,1,0:T(8,128)(2,1)} %param.13) | copy-start | bytes 442372
  11.0 17.9 %copy-start.12 = (bf16[1,48,1536]{2,1,0:T(8,128)(2,1)S(1)}, bf16[1,48,1536]{2,1,0:T(8,128)(2,1)}, u32[]{:S(2)}) copy-start(bf16[1,48,1536]{2,1,0:T(8,128)(2,1)} %param.12) | copy-start | bytes 442372
  11.0 17.9 %copy-start.13 = (bf16[1,48,1536]{2,1,0:T(8,128)(2,1)S(1)}, bf16[1,48,1536]{2,1,0:T(8,128)(2,1)}, u32[]{:S(2)}) copy-start(bf16[1,48,1536]{2,1,0:T(8,128)(2,1)} %param.11) | copy-start | bytes 442372
  13.0 16.8 %copy-start.10 = (bf16[128,1536]{1,0:T(8,128)(2,1)S(1)}, bf16[128,1536]{1,0:T(8,128)(2,1)}, u32[]{:S(2)}) copy-start(bf16[128,1536]{1,0:T(8,128)(2,1)} %param.7) | copy-start | bytes 1179652
  13.0 58.6 %all-to-all-start.2 = ((bf16[16,2,10,1536]{3,1,2,0:T(2,128)(2,1)}), bf16[16,2,10,1536]{3,1,2,0:T(2,128)(2,1)S(1)}, u32[]{:S(2)}, u32[]{:S(2)}) async-start(bf16[16,2,10,1536]{3,1,2,0:T(2,128)(2,1)} %copy.108), calls=%async_computation.2 | async-start | bytes 1966080 | tf_op jit(solution)/shard_map/all_to_all | solution.py:17
  28.8 145.6 %all-gather.2.cloned.1.call-start = ((), (), s32[]{:S(2)}) async-start(), calls=%async_computation.9 | async-start | bytes 3981312 | tf_op jit(solution)/shard_map/all_gather | solution.py:48
  29.8 1.7 copy-start.14
  82.3 53.5 %all-to-all-start = ((bf16[16,2,10,1664]{3,1,2,0:T(2,128)(2,1)}), bf16[16,2,10,1664]{3,1,2,0:T(2,128)(2,1)S(1)}, u32[]{:S(2)}, u32[]{:S(2)}) async-start(bf16[16,2,10,1664]{3,1,2,0:T(2,128)(2,1)} %copy.105), calls=%async_computation | async-start | bytes 2129920 | tf_op jit(solution)/shard_map/all_to_all | solution.py:17
  89.7 240.9 %reduce-scatter.2.cloned.1.call-start = ((), (), s32[]{:S(2)}) async-start(), calls=%async_computation.10 | async-start | bytes 7962624 | tf_op jit(solution)/shard_map/reduce_scatter | solution.py:85
  92.8 58.1 %collective-permute-start.1 = (bf16[320,1536]{1,0:T(8,128)(2,1)}, bf16[320,1536]{1,0:T(8,128)(2,1)}, u32[]{:S(2)}, u32[]{:S(2)}) collective-permute-start(bf16[320,1536]{1,0:T(8,128)(2,1)} %reshape_reshape.12), channel_id=1, source_target_pairs={{0,1},{1,0},{2,3},{3,2},{4,5},{5,4},{6,7},{7,6},{8,9},{9,8},{10,11... | collective-permute-start | bytes 2949128 | tf_op jit(solution)/shard_map/ppermute | solution.py:11
  146.2 26.6 %collective-permute-start = (bf16[320,1664]{1,0:T(8,128)(2,1)S(1)}, bf16[320,1664]{1,0:T(8,128)(2,1)S(1)}, u32[]{:S(2)}, u32[]{:S(2)}) collective-permute-start(bf16[320,1664]{1,0:T(8,128)(2,1)S(1)} %reshape_reshape.10), channel_id=1, source_target_pairs={{0,1},{1,0},{2,3},{3,2},{4,5},{5,4},{6,7},{7,6},{8,9},{9,8},{10,11... | collective-permute-start | bytes 3194888 | tf_op jit(solution)/shard_map/ppermute | solution.py:11
  152.1 20.8 %copy-start.6 = (bf16[640,1536]{1,0:T(8,128)(2,1)}, bf16[640,1536]{1,0:T(8,128)(2,1)S(1)}, u32[]{:S(2)}) copy-start(bf16[640,1536]{1,0:T(8,128)(2,1)S(1)} %constant_dynamic-update-slice_fusion.2) | copy-start | bytes 5898244
  172.9 1.3 copy-start.4
  174.4 3.2 copy-start.5
  174.4 3.6 %copy-start.3 = (bf16[3,384,1536]{2,1,0:T(8,128)(2,1)S(1)}, bf16[3,384,1536]{2,1,0:T(8,128)(2,1)}, u32[]{:S(2)}) copy-start(bf16[3,384,1536]{2,1,0:T(8,128)(2,1)} %all-gather.2.cloned.1.call-done) | copy-start | bytes 10616836
  178.0 1.5 copy-start.7
  182.0 1.1 copy-start.8
  187.9 2.5 copy-start.9
  200.8 7.1 %copy-start.2 = (bf16[320,1664]{1,0:T(8,128)(2,1)S(1)}, bf16[320,1664]{1,0:T(8,128)(2,1)}, u32[]{:S(2)}) copy-start(bf16[320,1664]{1,0:T(8,128)(2,1)} %get-tuple-element.8) | copy-start | bytes 3194884
  201.8 23.5 %collective-permute-start.2 = (bf16[32,5,1664]{2,0,1:T(8,128)(2,1)}, bf16[32,5,1664]{2,0,1:T(8,128)(2,1)}, u32[]{:S(2)}, u32[]{:S(2)}) collective-permute-start(bf16[32,5,1664]{2,0,1:T(8,128)(2,1)} %copy.112), channel_id=1, source_target_pairs={{0,1},{1,0},{2,3},{3,2},{4,5},{5,4},{6,7},{7,6},{8,9},{9,8},{10,11... | collective-permute-start | bytes 1597448 | tf_op jit(solution)/shard_map/ppermute | solution.py:11
  205.7 37.2 %collective-permute-start.3 = (bf16[32,5,1664]{2,0,1:T(8,128)(2,1)}, bf16[32,5,1664]{2,0,1:T(8,128)(2,1)}, u32[]{:S(2)}, u32[]{:S(2)}) collective-permute-start(bf16[32,5,1664]{2,0,1:T(8,128)(2,1)} %copy.117), channel_id=1, source_target_pairs={{0,1},{1,0},{2,3},{3,2},{4,5},{5,4},{6,7},{7,6},{8,9},{9,8},{10,11... | collective-permute-start | bytes 1597448 | tf_op jit(solution)/shard_map/ppermute | solution.py:11
  245.9 28.9 %all-to-all-start.6 = ((bf16[16,2,5,1664]{3,1,2,0:T(2,128)(2,1)}), bf16[16,2,5,1664]{3,1,2,0:T(2,128)(2,1)S(1)}, u32[]{:S(2)}, u32[]{:S(2)}) async-start(bf16[16,2,5,1664]{3,1,2,0:T(2,128)(2,1)} %copy.119), calls=%async_computation.6 | async-start | bytes 1064960 | tf_op jit(solution)/shard_map/all_to_all | solution.py:17
  286.3 29.8 %all-to-all-start.4 = ((bf16[16,2,5,1664]{3,1,2,0:T(2,128)(2,1)}), bf16[16,2,5,1664]{3,1,2,0:T(2,128)(2,1)S(1)}, u32[]{:S(2)}, u32[]{:S(2)}) async-start(bf16[16,2,5,1664]{3,1,2,0:T(2,128)(2,1)} %copy.114), calls=%async_computation.4 | async-start | bytes 1064960 | tf_op jit(solution)/shard_map/all_to_all | solution.py:17
  328.2 4.5 %copy-start.1 = (bf16[128,1536]{1,0:T(8,128)(2,1)S(1)}, bf16[128,1536]{1,0:T(8,128)(2,1)}, u32[]{:S(2)}) copy-start(bf16[128,1536]{1,0:T(8,128)(2,1)} %param.8) | copy-start | bytes 1179652
Sparse Core Ops, SparseCore 0:
  32.9 86.9 all-gather.1
  187.8 130.8 reduce-scatter.1

commit v4 on v3

v4 whole, which is shorter than its diff:
```python
import jax
import jax.numpy as jnp
from jax import lax
from jax.sharding import Mesh
from jax.sharding import PartitionSpec as P

LANE = 128


def swap_pair(value):
    return lax.ppermute(value, "rl", [(0, 1), (1, 0)])


def exchange(blocks):
    shape = blocks.shape
    split = blocks.reshape((lax.axis_size("ez"), lax.axis_size("ec")) + shape[1:])
    split = lax.all_to_all(split, "ez", split_axis=0, concat_axis=0, tiled=True)
    split = lax.all_to_all(split, "ec", split_axis=1, concat_axis=1, tiled=True)
    return split.reshape(shape)


def shards(tokens, grad_out, expert_ids, probs, w_gate, w_up, w_down):
    token_count = tokens.shape[0]
    width = tokens.shape[1]
    exp_count = lax.axis_size("ez") * lax.axis_size("ec")
    capacity = 5 * token_count // (2 * exp_count)
    slots = exp_count * capacity
    chosen = expert_ids.reshape(-1)
    onehot = (chosen[:, None] == jnp.arange(exp_count, dtype=jnp.int32)[None, :]).astype(jnp.int32)
    ranks = jnp.sum((jnp.cumsum(onehot, axis=0) - 1) * onehot, axis=1)
    slot_of = chosen * capacity + ranks
    routing = (slot_of[None, :] == jnp.arange(slots, dtype=jnp.int32)[:, None]).astype(jnp.bfloat16)
    token_routing = routing.reshape(slots, token_count, 2).sum(axis=2)
    prob_pairs = probs.reshape(-1, 1)

    slot_tokens = jnp.dot(token_routing, tokens, preferred_element_type=jnp.float32).astype(jnp.bfloat16)
    slot_grads = jnp.dot(token_routing, grad_out, preferred_element_type=jnp.float32).astype(jnp.bfloat16)
    slot_probs = jnp.dot(routing, prob_pairs, preferred_element_type=jnp.float32).astype(jnp.bfloat16)
    prob_block = jnp.concatenate([slot_probs, jnp.zeros((slots, LANE - 1), jnp.bfloat16)], axis=1)
    send = jnp.concatenate([slot_tokens, slot_grads, prob_block], axis=1).reshape(exp_count, capacity, -1)

    stacked = jnp.concatenate([w_gate, w_up, w_down], axis=0)
    full = lax.all_gather(stacked, "rh", axis=1, tiled=True)
    gate_w = full[0]
    up_w = full[1]
    down_w = full[2]

    half = capacity // 2
    pieces = []
    local = None
    for lo, hi in ((0, half), (half, capacity)):
        arrived = exchange(send[:, lo:hi]).reshape(exp_count * (hi - lo), -1)
        chunk_rows = arrived.shape[0]
        joined = jnp.concatenate([arrived, swap_pair(arrived)], axis=0)
        rows = joined[:, :width]
        grads = joined[:, width : 2 * width]
        weight = joined[:, 2 * width : 2 * width + 1].astype(jnp.float32)
        gate = jnp.dot(rows, gate_w.T, preferred_element_type=jnp.float32)
        up = jnp.dot(rows, up_w.T, preferred_element_type=jnp.float32)
        sig = jax.nn.sigmoid(gate)
        act = gate * sig
        hidden = act * up
        back = jnp.dot(grads, down_w.T, preferred_element_type=jnp.float32)
        prob_part = jnp.sum(hidden * back, axis=1, keepdims=True)
        d_gate = (weight * back * up * sig * (1.0 + gate * (1.0 - sig))).astype(jnp.bfloat16)
        d_up = (weight * back * act).astype(jnp.bfloat16)
        weighted = (weight * hidden).astype(jnp.bfloat16)
        partial_rows = jnp.dot(d_gate, gate_w, preferred_element_type=jnp.float32) + jnp.dot(
            d_up, up_w, preferred_element_type=jnp.float32
        )
        packed = jnp.concatenate(
            [
                partial_rows.astype(jnp.bfloat16),
                prob_part.astype(jnp.bfloat16),
                jnp.zeros((2 * chunk_rows, LANE - 1), jnp.bfloat16),
            ],
            axis=1,
        )
        part = jnp.stack(
            [
                jnp.dot(d_gate.T, rows, preferred_element_type=jnp.float32),
                jnp.dot(d_up.T, rows, preferred_element_type=jnp.float32),
                jnp.dot(weighted.T, grads, preferred_element_type=jnp.float32),
            ]
        )
        local = part if local is None else local + part
        received = swap_pair(packed[chunk_rows:])
        summed = (packed[:chunk_rows].astype(jnp.float32) + received.astype(jnp.float32)).astype(jnp.bfloat16)
        pieces.append(exchange(summed.reshape(exp_count, hi - lo, -1)))
    weight_grads = lax.psum_scatter(local, "rh", scatter_dimension=1, tiled=True)
    returned = jnp.concatenate(pieces, axis=1).reshape(slots, -1)

    grad_tokens = jnp.dot(
        token_routing.T, returned[:, :width], preferred_element_type=jnp.float32
    ).astype(jnp.bfloat16)
    grad_probs = jnp.dot(
        routing.T, returned[:, width : width + 1], preferred_element_type=jnp.float32
    ).reshape(token_count, 2)
    return (grad_tokens, grad_probs, weight_grads[0:1], weight_grads[1:2], weight_grads[2:3])


def solution(mesh):
    exp_count = mesh.shape["exp"]
    rep_count = mesh.shape["rep"]
    view = Mesh(mesh.devices.reshape(exp_count // 2, 2, rep_count // 2, 2), ("ez", "ec", "rh", "rl"))
    rows_spec = P(("ez", "ec", "rh", "rl"), None)
    weight_spec = P(("ez", "ec"), ("rh", "rl"), None)
    in_specs = (rows_spec,) * 4 + (weight_spec,) * 3
    out_specs = (rows_spec, rows_spec, weight_spec, weight_spec, weight_spec)
    return jax.shard_map(shards, mesh=view, in_specs=in_specs, out_specs=out_specs, check_vma=False)
```

time: 343 us -> 353 us (1.029)
  waiting for transfers between devices: 173 us -> 158 us
  local copies, waits for them, and re-layouts: 34.4 us -> 45.4 us
  matrix products: 18 us -> 27.1 us
  starting transfers between devices: 48.8 us -> 57.6 us
  blocking collectives: 42.4 us -> 38.8 us
    all_to_all x4, waiting for transfers between devices: 118 us -> 102 us  [exchange(): split = lax.all_to_all(split, 'ez', split_axis=0, concat_axis=0, tiled=True)]
    all_to_all x4, starting transfers between devices: 37.1 us -> 43.6 us  [exchange(): split = lax.all_to_all(split, 'ez', split_axis=0, concat_axis=0, tiled=True)]
    another operation x2 -> x4, local copies, waits for them, and re-layouts: 2.31 us -> 6.16 us  [exchange(): blocks.reshape((lax.axis_size('ez'), lax.axis_size('ec')) + shape[1:])]
    all_to_all x4, blocking collectives: 42.4 us -> 38.8 us  [exchange(): split = lax.all_to_all(split, 'ec', split_axis=1, concat_axis=1, tiled=True)]
    add x0 -> x1, other arithmetic: none -> 3.56 us  [shards(): local = part if local is None else local + part]
    concatenate x6 -> x7, local copies, waits for them, and re-layouts: 7.14 us -> 10.2 us  [the longest x5 7.81 us: shards(): jnp.concatenate([slot_tokens, slot_grads, prob_block], axis=1)]
  transfers between devices with their start and end apart: 10 -> 10, of which waited for: 7 -> 6; matrix products, arithmetic and copies ran while one was open for 11% -> 12% of each run, Pallas kernels for 0% -> 0%
where the time goes in v4:
time: 353 us; the launch traced here: 351 us
  waiting for transfers between devices  158 us (45%)
  starting transfers between devices  57.6 us (16%)
  local copies, waits for them, and re-layouts  45.4 us (13%)
  blocking collectives  38.8 us (11%)
  matrix products  27.1 us (8%)
  between operations  14.6 us (4%)
  other arithmetic  9.2 us (3%)
    all_to_all x4, waiting for transfers between devices, exchange(): split = lax.all_to_all(split, 'ez', split_axis=0, concat_axis=0, tiled=True)  102 us
    ppermute x4, waiting for transfers between devices, swap_pair(): return lax.ppermute(value, 'rl', [(0, 1), (1, 0)])  55.3 us
    all_to_all x4, starting transfers between devices, exchange(): split = lax.all_to_all(split, 'ez', split_axis=0, concat_axis=0, tiled=True)  43.6 us
    all_to_all x4, blocking collectives, exchange(): split = lax.all_to_all(split, 'ec', split_axis=1, concat_axis=1, tiled=True)  38.8 us
    ppermute x4, starting transfers between devices, swap_pair(): return lax.ppermute(value, 'rl', [(0, 1), (1, 0)])  13.8 us
    concatenate x5, local copies, waits for them, and re-layouts, shards(): jnp.concatenate([slot_tokens, slot_grads, prob_block], axis=1)  7.81 us
  transfers between devices with their start and end apart: 10, of which 6 were waited for; matrix products, arithmetic and copies ran while one was open for 12% of the time, Pallas kernels for 0%

profile of v4, /device:TPU:1, one launch (start us, length us, event | category | flops | bytes accessed | tf_op | source)
XLA Modules:
  0.0 350.6 jit_solution(12847839016403951617)
XLA Ops:
  12.0 1.3 concatenate.31
  13.8 1.3 concatenate.30
  15.1 4.9 %concatenate.34 = bf16[32,10,3200]{2,1,0:T(8,128)(2,1)S(1)} concatenate(bf16[32,10,1536]{2,1,0:T(8,128)(2,1)} %concatenate.30, bf16[32,10,1536]{2,1,0:T(8,128)(2,1)} %concatenate.31, bf16[32,10,1]{2,1,0:T(8,128)(2,1)S(1)} %concatenate.41, bf16[32,10,127]{2,1,0:T(8,128)(2,1)S(1)} %concatenate.33), dimensions={2} | concatenate | bytes 4096000 | tf_op jit(solution)/shard_map/concatenate | solution.py:40
  20.0 1.7 fusion.42
  21.7 1.9 copy.104
  23.5 15.9 %all-to-all-start.4 = ((bf16[16,2,5,3200]{3,1,2,0:T(2,128)(2,1)}), bf16[16,2,5,3200]{3,1,2,0:T(2,128)(2,1)S(1)}, u32[]{:S(2)}, u32[]{:S(2)}) async-start(bf16[16,2,5,3200]{3,1,2,0:T(2,128)(2,1)} %copy.104), calls=%async_computation.4 | async-start | bytes 2048000 | tf_op jit(solution)/shard_map/all_to_all | solution.py:17
  40.4 1.8 copy.97
  42.2 41.4 %all-to-all-done.4 = bf16[16,2,5,3200]{3,1,2,0:T(2,128)(2,1)S(1)} async-done(((bf16[16,2,5,3200]{3,1,2,0:T(2,128)(2,1)}), bf16[16,2,5,3200]{3,1,2,0:T(2,128)(2,1)S(1)}, u32[]{:S(2)}, u32[]{:S(2)}) %all-to-all-start.4) | async-done | bytes 1024032 | tf_op jit(solution)/shard_map/all_to_all | solution.py:17
  83.6 10.8 %all_to_all.40 = bf16[16,2,5,3200]{3,0,2,1:T(8,128)(2,1)} all-to-all(bf16[16,2,5,3200]{3,0,2,1:T(8,128)(2,1)S(1)} %copy.105), channel_id=1, replica_groups=mesh['ez'=16,'ec'=2,'rh'=8,'rl'=2] {'ec'}, dimensions={1} | all-to-all | bytes 2048000 | tf_op jit(solution)/shard_map/all_to_all | solution.py:18
  94.5 7.5 %all-to-all-start = ((bf16[16,2,5,3200]{3,1,2,0:T(2,128)(2,1)}), bf16[16,2,5,3200]{3,1,2,0:T(2,128)(2,1)S(1)}, u32[]{:S(2)}, u32[]{:S(2)}) async-start(bf16[16,2,5,3200]{3,1,2,0:T(2,128)(2,1)} %copy.97), calls=%async_computation | async-start | bytes 2048000 | tf_op jit(solution)/shard_map/all_to_all | solution.py:17
  102.0 1.5 copy.106
  103.5 1.3 reshape_reshape.14
  104.8 3.1 collective-permute-start.2
  107.9 38.7 %all-to-all-done = bf16[16,2,5,3200]{3,1,2,0:T(2,128)(2,1)S(1)} async-done(((bf16[16,2,5,3200]{3,1,2,0:T(2,128)(2,1)}), bf16[16,2,5,3200]{3,1,2,0:T(2,128)(2,1)S(1)}, u32[]{:S(2)}, u32[]{:S(2)}) %all-to-all-start) | async-done | bytes 1024032 | tf_op jit(solution)/shard_map/all_to_all | solution.py:17
  146.7 9.6 %all_to_all.41 = bf16[16,2,5,3200]{3,0,2,1:T(8,128)(2,1)S(1)} all-to-all(bf16[16,2,5,3200]{3,0,2,1:T(8,128)(2,1)S(1)} %copy.98), channel_id=1, replica_groups=mesh['ez'=16,'ec'=2,'rh'=8,'rl'=2] {'ec'}, dimensions={1} | all-to-all | bytes 2048000 | tf_op jit(solution)/shard_map/all_to_all | solution.py:18
  156.5 1.3 reshape_reshape.12
  157.9 3.4 collective-permute-start
  162.4 1.3 constant_dynamic-update-slice_fusion.2
  163.8 1.3 copy-done.4
  165.2 18.7 %collective-permute-done = bf16[160,3200]{1,0:T(8,128)(2,1)S(1)} collective-permute-done((bf16[160,3200]{1,0:T(8,128)(2,1)}, bf16[160,3200]{1,0:T(8,128)(2,1)S(1)}, u32[]{:S(2)}, u32[]{:S(2)}) %collective-permute-start) | collective-permute-done | bytes 1024032 | tf_op jit(solution)/shard_map/ppermute | solution.py:11
  186.0 2.4 fusion.14
  188.7 1.9 fusion.10
  190.5 2.1 convolution_bitcast_fusion.3
  192.7 2.1 multiply_reduce_fusion.1
  194.8 2.2 convolution_bitcast_fusion.4
  197.0 2.1 convolution_bitcast_fusion.5
  204.1 3.6 %maximum_add_fusion = f32[3,384,1536]{2,1,0:T(8,128)} fusion(f32[1,384,1536]{2,1,0:T(8,128)S(1)} %convolution_bitcast_fusion.3, f32[1,384,1536]{2,1,0:T(8,128)S(1)} %convolution_bitcast_fusion.4, f32[1,384,1536]{2,1,0:T(8,128)S(1)} %convolution_bitcast_fusion.5, f32[1,384,1536]{2,1,0:T(8,128)S(1)} %convolution_bitcast_fusion, ...), kind=kLoop, calls=%fused_computation | loop fusion | flops 8847360 | bytes 21233664 | tf_op jit(solution)/shard_map/add | solution.py:86
  208.5 1.6 fusion.11
  210.1 1.6 fusion.1
  212.4 3.1 concatenate.39
  216.5 3.1 collective-permute-start.3
  219.7 17.6 %collective-permute-done.3 = bf16[160,1664]{1,0:T(8,128)(2,1)S(1)} collective-permute-done((bf16[160,1664]{1,0:T(8,128)(2,1)S(1)}, bf16[160,1664]{1,0:T(8,128)(2,1)S(1)}, u32[]{:S(2)}, u32[]{:S(2)}) %collective-permute-start.3) | collective-permute-done | bytes 532512 | tf_op jit(solution)/shard_map/ppermute | solution.py:11
  237.3 2.0 add_convert_fusion
  239.3 2.2 reshape_reshape.15
  241.5 2.5 copy.108
  244.0 9.3 %all-to-all-start.6 = ((bf16[16,2,5,1664]{3,1,2,0:T(2,128)(2,1)}), bf16[16,2,5,1664]{3,1,2,0:T(2,128)(2,1)}, u32[]{:S(2)}, u32[]{:S(2)}) async-start(bf16[16,2,5,1664]{3,1,2,0:T(2,128)(2,1)} %copy.108), calls=%async_computation.6 | async-start | bytes 1064960 | tf_op jit(solution)/shard_map/all_to_all | solution.py:17
  254.0 1.6 fusion.13
  255.7 1.6 fusion
  257.3 2.3 concatenate.37
  259.7 4.2 %collective-permute-start.1 = (bf16[160,1664]{1,0:T(8,128)(2,1)S(1)}, bf16[160,1664]{1,0:T(8,128)(2,1)S(1)}, u32[]{:S(2)}, u32[]{:S(2)}) collective-permute-start(bf16[160,1664]{1,0:T(8,128)(2,1)S(1)} %slice.97), channel_id=1, source_target_pairs={{0,1},{1,0},{2,3},{3,2},{4,5},{5,4},{6,7},{7,6},{8,9},{9,8},{10,11... | collective-permute-start | bytes 1597448 | tf_op jit(solution)/shard_map/ppermute | solution.py:11
  263.9 19.0 %collective-permute-done.1 = bf16[160,1664]{1,0:T(8,128)(2,1)S(1)} collective-permute-done((bf16[160,1664]{1,0:T(8,128)(2,1)S(1)}, bf16[160,1664]{1,0:T(8,128)(2,1)S(1)}, u32[]{:S(2)}, u32[]{:S(2)}) %collective-permute-start.1) | collective-permute-done | bytes 532512 | tf_op jit(solution)/shard_map/ppermute | solution.py:11
  283.2 1.3 copy.101
  285.6 7.5 %all_to_all.42 = bf16[16,2,5,1664]{3,0,2,1:T(8,128)(2,1)S(1)} all-to-all(bf16[16,2,5,1664]{3,0,2,1:T(8,128)(2,1)S(1)} %copy.109), channel_id=1, replica_groups=mesh['ez'=16,'ec'=2,'rh'=8,'rl'=2] {'ec'}, dimensions={1} | all-to-all | bytes 1064960 | tf_op jit(solution)/shard_map/all_to_all | solution.py:18
  293.1 11.0 %all-to-all-start.2 = ((bf16[16,2,5,1664]{3,1,2,0:T(2,128)(2,1)}), bf16[16,2,5,1664]{3,1,2,0:T(2,128)(2,1)S(1)}, u32[]{:S(2)}, u32[]{:S(2)}) async-start(bf16[16,2,5,1664]{3,1,2,0:T(2,128)(2,1)} %copy.101), calls=%async_computation.2 | async-start | bytes 1064960 | tf_op jit(solution)/shard_map/all_to_all | solution.py:17
  304.7 22.4 %all-to-all-done.2 = bf16[16,2,5,1664]{3,1,2,0:T(2,128)(2,1)S(1)} async-done(((bf16[16,2,5,1664]{3,1,2,0:T(2,128)(2,1)}), bf16[16,2,5,1664]{3,1,2,0:T(2,128)(2,1)S(1)}, u32[]{:S(2)}, u32[]{:S(2)}) %all-to-all-start.2) | async-done | bytes 532512 | tf_op jit(solution)/shard_map/all_to_all | solution.py:17
  327.2 10.9 %all_to_all.43 = bf16[16,2,5,1664]{3,0,2,1:T(8,128)(2,1)S(1)} all-to-all(bf16[16,2,5,1664]{3,0,2,1:T(8,128)(2,1)S(1)} %copy.102), channel_id=1, replica_groups=mesh['ez'=16,'ec'=2,'rh'=8,'rl'=2] {'ec'}, dimensions={1} | all-to-all | bytes 1064960 | tf_op jit(solution)/shard_map/all_to_all | solution.py:18
  340.5 1.2 convolution_convert_fusion.2
  341.7 2.1 fusion.43
  (102 shorter events, 22.8 us)
Async XLA Ops:
  7.2 4.5 %copy-start = (bf16[128,1536]{1,0:T(8,128)(2,1)S(1)}, bf16[128,1536]{1,0:T(8,128)(2,1)}, u32[]{:S(2)}) copy-start(bf16[128,1536]{1,0:T(8,128)(2,1)} %param.8) | copy-start | bytes 1179652
  11.1 2.2 copy-start.8
  11.4 2.0 copy-start.16
  21.7 17.8 %copy-start.17 = (bf16[1,48,1536]{2,1,0:T(8,128)(2,1)S(1)}, bf16[1,48,1536]{2,1,0:T(8,128)(2,1)}, u32[]{:S(2)}) copy-start(bf16[1,48,1536]{2,1,0:T(8,128)(2,1)} %param.13) | copy-start | bytes 442372
  21.7 17.8 %copy-start.18 = (bf16[1,48,1536]{2,1,0:T(8,128)(2,1)S(1)}, bf16[1,48,1536]{2,1,0:T(8,128)(2,1)}, u32[]{:S(2)}) copy-start(bf16[1,48,1536]{2,1,0:T(8,128)(2,1)} %param.12) | copy-start | bytes 442372
  21.7 17.8 %copy-start.19 = (bf16[1,48,1536]{2,1,0:T(8,128)(2,1)S(1)}, bf16[1,48,1536]{2,1,0:T(8,128)(2,1)}, u32[]{:S(2)}) copy-start(bf16[1,48,1536]{2,1,0:T(8,128)(2,1)} %param.11) | copy-start | bytes 442372
  23.5 16.8 %copy-start.2 = (bf16[32,5,3200]{2,1,0:T(8,128)(2,1)S(1)}, bf16[32,5,3200]{2,1,0:T(8,128)(2,1)}, u32[]{:S(2)}) copy-start(bf16[32,5,3200]{2,1,0:T(8,128)(2,1)} %get-tuple-element.5) | copy-start | bytes 3072004
  23.5 60.0 %all-to-all-start.4 = ((bf16[16,2,5,3200]{3,1,2,0:T(2,128)(2,1)}), bf16[16,2,5,3200]{3,1,2,0:T(2,128)(2,1)S(1)}, u32[]{:S(2)}, u32[]{:S(2)}) async-start(bf16[16,2,5,3200]{3,1,2,0:T(2,128)(2,1)} %copy.104), calls=%async_computation.4 | async-start | bytes 2048000 | tf_op jit(solution)/shard_map/all_to_all | solution.py:17
  39.4 146.6 %all-gather.2.cloned.1.call-start = ((), (), s32[]{:S(2)}) async-start(), calls=%async_computation.9 | async-start | bytes 3981312 | tf_op jit(solution)/shard_map/all_gather | solution.py:43
  94.5 52.1 %all-to-all-start = ((bf16[16,2,5,3200]{3,1,2,0:T(2,128)(2,1)}), bf16[16,2,5,3200]{3,1,2,0:T(2,128)(2,1)S(1)}, u32[]{:S(2)}, u32[]{:S(2)}) async-start(bf16[16,2,5,3200]{3,1,2,0:T(2,128)(2,1)} %copy.97), calls=%async_computation | async-start | bytes 2048000 | tf_op jit(solution)/shard_map/all_to_all | solution.py:17
  102.0 239.7 %reduce-scatter.2.cloned.1.call-start = ((), (), s32[]{:S(2)}) async-start(), calls=%async_computation.10 | async-start | bytes 7962624 | tf_op jit(solution)/shard_map/reduce_scatter | solution.py:90
  104.8 57.7 %collective-permute-start.2 = (bf16[160,3200]{1,0:T(8,128)(2,1)}, bf16[160,3200]{1,0:T(8,128)(2,1)}, u32[]{:S(2)}, u32[]{:S(2)}) collective-permute-start(bf16[160,3200]{1,0:T(8,128)(2,1)} %reshape_reshape.14), channel_id=1, source_target_pairs={{0,1},{1,0},{2,3},{3,2},{4,5},{5,4},{6,7},{7,6},{8,9},{9,8},{10,11... | collective-permute-start | bytes 3072008 | tf_op jit(solution)/shard_map/ppermute | solution.py:11
  156.3 5.0 %copy-start.6 = (bf16[160,3200]{1,0:T(8,128)(2,1)S(1)}, bf16[160,3200]{1,0:T(8,128)(2,1)}, u32[]{:S(2)}) copy-start(bf16[160,3200]{1,0:T(8,128)(2,1)} %reshape_reshape.14) | copy-start | bytes 3072004
  157.9 3.5 %copy-start.7 = (bf16[160,3200]{1,0:T(8,128)(2,1)S(1)}, bf16[160,3200]{1,0:T(8,128)(2,1)}, u32[]{:S(2)}) copy-start(bf16[160,3200]{1,0:T(8,128)(2,1)} %reshape_reshape.12) | copy-start | bytes 3072004
  157.9 26.0 %collective-permute-start = (bf16[160,3200]{1,0:T(8,128)(2,1)}, bf16[160,3200]{1,0:T(8,128)(2,1)S(1)}, u32[]{:S(2)}, u32[]{:S(2)}) collective-permute-start(bf16[160,3200]{1,0:T(8,128)(2,1)} %reshape_reshape.12), channel_id=1, source_target_pairs={{0,1},{1,0},{2,3},{3,2},{4,5},{5,4},{6,7},{7,6},{8,9},{9,8},{10,11... | collective-permute-start | bytes 3072008 | tf_op jit(solution)/shard_map/ppermute | solution.py:11
  163.8 1.3 copy-start.4
  186.0 2.7 copy-start.3
  194.8 2.2 copy-start.10
  194.8 4.4 %copy-start.12 = (bf16[320,384]{1,0:T(8,128)(2,1)}, bf16[320,384]{1,0:T(8,128)(2,1)S(1)}, u32[]{:S(2)}) copy-start(bf16[320,384]{1,0:T(8,128)(2,1)S(1)} %get-tuple-element.8) | copy-start | bytes 737284
  197.0 2.2 copy-start.5
  202.5 0.8 copy-start.13
  202.5 0.8 copy-start.15
  207.7 2.4 copy-start.14
  216.5 20.8 %collective-permute-start.3 = (bf16[160,1664]{1,0:T(8,128)(2,1)S(1)}, bf16[160,1664]{1,0:T(8,128)(2,1)S(1)}, u32[]{:S(2)}, u32[]{:S(2)}) collective-permute-start(bf16[160,1664]{1,0:T(8,128)(2,1)S(1)} %slice.103), channel_id=1, source_target_pairs={{0,1},{1,0},{2,3},{3,2},{4,5},{5,4},{6,7},{7,6},{8,9},{9,8},{10,11... | collective-permute-start | bytes 1597448 | tf_op jit(solution)/shard_map/ppermute | solution.py:11
  244.0 40.5 %all-to-all-start.6 = ((bf16[16,2,5,1664]{3,1,2,0:T(2,128)(2,1)}), bf16[16,2,5,1664]{3,1,2,0:T(2,128)(2,1)}, u32[]{:S(2)}, u32[]{:S(2)}) async-start(bf16[16,2,5,1664]{3,1,2,0:T(2,128)(2,1)} %copy.108), calls=%async_computation.6 | async-start | bytes 1064960 | tf_op jit(solution)/shard_map/all_to_all | solution.py:17
  253.3 2.4 copy-start.11
  259.7 23.2 %collective-permute-start.1 = (bf16[160,1664]{1,0:T(8,128)(2,1)S(1)}, bf16[160,1664]{1,0:T(8,128)(2,1)S(1)}, u32[]{:S(2)}, u32[]{:S(2)}) collective-permute-start(bf16[160,1664]{1,0:T(8,128)(2,1)S(1)} %slice.97), channel_id=1, source_target_pairs={{0,1},{1,0},{2,3},{3,2},{4,5},{5,4},{6,7},{7,6},{8,9},{9,8},{10,11... | collective-permute-start | bytes 1597448 | tf_op jit(solution)/shard_map/ppermute | solution.py:11
  293.1 34.0 %all-to-all-start.2 = ((bf16[16,2,5,1664]{3,1,2,0:T(2,128)(2,1)}), bf16[16,2,5,1664]{3,1,2,0:T(2,128)(2,1)S(1)}, u32[]{:S(2)}, u32[]{:S(2)}) async-start(bf16[16,2,5,1664]{3,1,2,0:T(2,128)(2,1)} %copy.101), calls=%async_computation.2 | async-start | bytes 1064960 | tf_op jit(solution)/shard_map/all_to_all | solution.py:17
  339.2 1.3 copy-start.9
  339.2 4.5 %copy-start.1 = (bf16[128,1536]{1,0:T(8,128)(2,1)S(1)}, bf16[128,1536]{1,0:T(8,128)(2,1)}, u32[]{:S(2)}) copy-start(bf16[128,1536]{1,0:T(8,128)(2,1)} %param.8) | copy-start | bytes 1179652
Sparse Core Ops, SparseCore 0:
  43.4 85.5 all-gather.1
  207.8 132.6 reduce-scatter.1

commit v5 on v3

--- a/solution.py
+++ b/solution.py
@@ -83,15 +83,9 @@
         ]
     )
     weight_grads = lax.psum_scatter(local, "rh", scatter_dimension=1, tiled=True)
-    mine = packed[:slots].reshape(exp_count, capacity, -1)
-    theirs = packed[slots:].reshape(exp_count, capacity, -1)
-    half = capacity // 2
-    pieces = []
-    for lo, hi in ((0, half), (half, capacity)):
-        received = swap_pair(theirs[:, lo:hi])
-        summed = (mine[:, lo:hi].astype(jnp.float32) + received.astype(jnp.float32)).astype(jnp.bfloat16)
-        pieces.append(exchange(summed))
-    returned = jnp.concatenate(pieces, axis=1).reshape(slots, -1)
+    received = swap_pair(packed[slots:])
+    summed = (packed[:slots].astype(jnp.float32) + received.astype(jnp.float32)).astype(jnp.bfloat16)
+    returned = exchange(summed.reshape(exp_count, capacity, -1)).reshape(slots, -1)
 
     grad_tokens = jnp.dot(
         token_routing.T, returned[:, :width], preferred_element_type=jnp.float32

time: 343 us -> 325 us (0.948)
  blocking collectives: 42.4 us -> 90.7 us
  waiting for transfers between devices: 173 us -> 133 us
  starting transfers between devices: 48.8 us -> 32.9 us
  local copies, waits for them, and re-layouts: 34.4 us -> 27.7 us
    all_to_all x0 -> x1, blocking collectives: none -> 60.8 us  [exchange(): split = lax.all_to_all(split, 'ez', split_axis=0, concat_axis=0, tiled=True)]
    all_to_all x4 -> x2, waiting for transfers between devices: 118 us -> 75 us  [exchange(): split = lax.all_to_all(split, 'ez', split_axis=0, concat_axis=0, tiled=True)]
    all_to_all x4 -> x2, starting transfers between devices: 37.1 us -> 23.3 us  [exchange(): split = lax.all_to_all(split, 'ez', split_axis=0, concat_axis=0, tiled=True)]
    all_to_all x4 -> x3, blocking collectives: 42.4 us -> 30 us  [exchange(): split = lax.all_to_all(split, 'ec', split_axis=1, concat_axis=1, tiled=True)]
    reshape x7 -> x0, local copies, waits for them, and re-layouts: 5.1 us -> none  [the longest x2 2.48 us: exchange(): blocks.reshape((lax.axis_size('ez'), lax.axis_size('ec')) + shape[1:])]
    reduce_scatter x1, waiting for transfers between devices: 0.01 us -> 4.95 us  [shards(): lax.psum_scatter(local, 'rh', scatter_dimension=1, tiled=True)]
    slice x5 -> x2, local copies, waits for them, and re-layouts: 3.73 us -> 0.26 us  [the longest x3 2.07 us: shards(): received = swap_pair(theirs[:, lo:hi])]
    ppermute x4 -> x3, waiting for transfers between devices: 55.3 us -> 52.8 us  [swap_pair(): return lax.ppermute(value, 'rl', [(0, 1), (1, 0)])]
  transfers between devices with their start and end apart: 10 -> 7, of which waited for: 7 -> 5; matrix products, arithmetic and copies ran while one was open for 11% -> 9% of each run, Pallas kernels for 0% -> 0%
where the time goes in v5:
time: 325 us; the launch traced here: 324 us
  waiting for transfers between devices  133 us (41%)
  blocking collectives  90.7 us (28%)
  starting transfers between devices  32.9 us (10%)
  local copies, waits for them, and re-layouts  27.7 us (9%)
  matrix products  18 us (6%)
  between operations  14.5 us (4%)
  other arithmetic  7.17 us (2%)
    all_to_all x2, waiting for transfers between devices, exchange(): split = lax.all_to_all(split, 'ez', split_axis=0, concat_axis=0, tiled=True)  75 us
    all_to_all x1, blocking collectives, exchange(): split = lax.all_to_all(split, 'ez', split_axis=0, concat_axis=0, tiled=True)  60.8 us
    ppermute x3, waiting for transfers between devices, swap_pair(): return lax.ppermute(value, 'rl', [(0, 1), (1, 0)])  52.8 us
    all_to_all x3, blocking collectives, exchange(): split = lax.all_to_all(split, 'ec', split_axis=1, concat_axis=1, tiled=True)  30 us
    all_to_all x2, starting transfers between devices, exchange(): split = lax.all_to_all(split, 'ez', split_axis=0, concat_axis=0, tiled=True)  23.3 us
    ppermute x3, starting transfers between devices, swap_pair(): return lax.ppermute(value, 'rl', [(0, 1), (1, 0)])  9.54 us
  transfers between devices with their start and end apart: 7, of which 5 were waited for; matrix products, arithmetic and copies ran while one was open for 9% of the time, Pallas kernels for 0%

profile of v5, /device:TPU:1, one launch (start us, length us, event | category | flops | bytes accessed | tf_op | source)
XLA Modules:
  0.0 323.9 jit_solution(17888947934584770297)
XLA Ops:
  7.2 0.8 copy.60
  8.3 0.6 reduce-window.6
  9.5 0.7 multiply_add_fusion.1
  10.2 0.4 convolution_convert_fusion
  11.0 1.9 copy.69
  13.0 15.9 %all-to-all-start.2 = ((bf16[16,2,10,1536]{3,1,2,0:T(2,128)(2,1)}), bf16[16,2,10,1536]{3,1,2,0:T(2,128)(2,1)S(1)}, u32[]{:S(2)}, u32[]{:S(2)}) async-start(bf16[16,2,10,1536]{3,1,2,0:T(2,128)(2,1)} %copy.69), calls=%async_computation.2 | async-start | bytes 1966080 | tf_op jit(solution)/shard_map/all_to_all | solution.py:17
  28.9 0.8 pad_maximum_fusion.1
  30.2 1.3 concatenate.20
  32.3 2.4 concatenate.22
  34.7 1.8 copy.66
  36.5 35.1 %all-to-all-done.2 = bf16[16,2,10,1536]{3,1,2,0:T(2,128)(2,1)S(1)} async-done(((bf16[16,2,10,1536]{3,1,2,0:T(2,128)(2,1)}), bf16[16,2,10,1536]{3,1,2,0:T(2,128)(2,1)S(1)}, u32[]{:S(2)}, u32[]{:S(2)}) %all-to-all-start.2) | async-done | bytes 983072 | tf_op jit(solution)/shard_map/all_to_all | solution.py:17
  71.7 10.5 %all_to_all.30 = bf16[16,2,10,1536]{3,0,2,1:T(8,128)(2,1)} all-to-all(bf16[16,2,10,1536]{3,0,2,1:T(8,128)(2,1)S(1)} %copy.70), channel_id=1, replica_groups=mesh['ez'=16,'ec'=2,'rh'=8,'rl'=2] {'ec'}, dimensions={1} | all-to-all | bytes 1966080 | tf_op jit(solution)/shard_map/all_to_all | solution.py:18
  82.2 7.5 %all-to-all-start = ((bf16[16,2,10,1664]{3,1,2,0:T(2,128)(2,1)}), bf16[16,2,10,1664]{3,1,2,0:T(2,128)(2,1)S(1)}, u32[]{:S(2)}, u32[]{:S(2)}) async-start(bf16[16,2,10,1664]{3,1,2,0:T(2,128)(2,1)} %copy.66), calls=%async_computation | async-start | bytes 2129920 | tf_op jit(solution)/shard_map/all_to_all | solution.py:17
  89.8 1.8 copy.71
  91.6 1.2 reshape_reshape.18
  92.7 3.1 collective-permute-start.1
  95.9 39.9 %all-to-all-done = bf16[16,2,10,1664]{3,1,2,0:T(2,128)(2,1)S(1)} async-done(((bf16[16,2,10,1664]{3,1,2,0:T(2,128)(2,1)}), bf16[16,2,10,1664]{3,1,2,0:T(2,128)(2,1)S(1)}, u32[]{:S(2)}, u32[]{:S(2)}) %all-to-all-start) | async-done | bytes 1064992 | tf_op jit(solution)/shard_map/all_to_all | solution.py:17
  135.9 9.6 %all_to_all.31 = bf16[16,2,10,1664]{3,0,2,1:T(8,128)(2,1)S(1)} all-to-all(bf16[16,2,10,1664]{3,0,2,1:T(8,128)(2,1)S(1)} %copy.67), channel_id=1, replica_groups=mesh['ez'=16,'ec'=2,'rh'=8,'rl'=2] {'ec'}, dimensions={1} | all-to-all | bytes 2129920 | tf_op jit(solution)/shard_map/all_to_all | solution.py:18
  145.7 0.4 reshape_reshape.16
  146.2 3.3 %collective-permute-start = (bf16[320,1664]{1,0:T(8,128)(2,1)S(1)}, bf16[320,1664]{1,0:T(8,128)(2,1)S(1)}, u32[]{:S(2)}, u32[]{:S(2)}) collective-permute-start(bf16[320,1664]{1,0:T(8,128)(2,1)S(1)} %reshape_reshape.16), channel_id=1, source_target_pairs={{0,1},{1,0},{2,3},{3,2},{4,5},{5,4},{6,7},{7,6},{8,9},{9,8},{10,11... | collective-permute-start | bytes 3194888 | tf_op jit(solution)/shard_map/ppermute | solution.py:11
  149.5 1.3 constant_dynamic-update-slice_fusion.3
  150.8 1.3 constant_dynamic-update-slice_fusion.2
  152.1 20.6 %collective-permute-done = bf16[320,1664]{1,0:T(8,128)(2,1)S(1)} collective-permute-done((bf16[320,1664]{1,0:T(8,128)(2,1)S(1)}, bf16[320,1664]{1,0:T(8,128)(2,1)S(1)}, u32[]{:S(2)}, u32[]{:S(2)}) %collective-permute-start) | collective-permute-done | bytes 1064992 | tf_op jit(solution)/shard_map/ppermute | solution.py:11
  172.9 1.3 copy-done.3
  174.4 3.1 fusion.4
  177.6 0.4 copy-done.2
  178.0 1.1 fusion.2
  179.1 0.4 copy-done.6
  179.5 1.1 convolution_bitcast_fusion
  180.7 1.4 multiply_reduce_fusion
  182.0 1.1 convolution_bitcast_fusion.1
  183.1 1.1 convolution_bitcast_fusion.2
  184.2 3.5 %pad_maximum_fusion = f32[3,384,1536]{2,1,0:T(8,128)} fusion(f32[1,384,1536]{2,1,0:T(8,128)S(1)} %convolution_bitcast_fusion, f32[1,384,1536]{2,1,0:T(8,128)S(1)} %convolution_bitcast_fusion.1, f32[1,384,1536]{2,1,0:T(8,128)S(1)} %convolution_bitcast_fusion.2), kind=kLoop, calls=%fused_computation | loop fusion | flops 3538944 | bytes 14155776 | tf_op jit(solution)/shard_map/stack | solution.py:78
  187.9 2.5 fusion.7
  190.4 3.8 %add_convert_fusion = bf16[640,1536]{1,0:T(8,128)(2,1)} fusion(f32[640,1536]{1,0:T(8,128)S(1)} %fusion.7, bf16[640,384]{0,1:T(8,128)(2,1)S(1)} %copy-done.8, bf16[3,384,1536]{2,1,0:T(8,128)(2,1)} %all-gather.2.cloned.1.call-done), kind=kOutput, calls=%fused_computation.1 | convolution fusion | flops 756940800 | bytes 7569408 | tf_op jit(solution)/shard_map/dot_general | solution.py:66
  194.2 3.3 %concatenate.26 = bf16[640,1664]{1,0:T(8,128)(2,1)S(1)} concatenate(bf16[640,1536]{1,0:T(8,128)(2,1)} %add_convert_fusion, bf16[640,1]{1,0:T(8,128)(2,1)S(1)} %convert_element_type.75, bf16[640,127]{1,0:T(8,128)(2,1)S(1)} %broadcast_in_dim.5), dimensions={1} | concatenate | bytes 4259840 | tf_op jit(solution)/shard_map/concatenate | solution.py:70
  197.7 3.1 collective-permute-start.2
  200.8 32.2 %collective-permute-done.2 = bf16[320,1664]{1,0:T(8,128)(2,1)S(1)} collective-permute-done((bf16[320,1664]{1,0:T(8,128)(2,1)S(1)}, bf16[320,1664]{1,0:T(8,128)(2,1)S(1)}, u32[]{:S(2)}, u32[]{:S(2)}) %collective-permute-start.2) | collective-permute-done | bytes 1064992 | tf_op jit(solution)/shard_map/ppermute | solution.py:11
  233.0 1.3 add_convert_fusion.1
  234.2 1.5 reshape_reshape.19
  235.7 0.8 copy.73
  236.6 60.8 %all_to_all.32 = bf16[16,2,10,1664]{3,1,2,0:T(2,128)(2,1)S(1)} all-to-all(bf16[16,2,10,1664]{3,1,2,0:T(2,128)(2,1)S(1)} %copy.73), channel_id=1, replica_groups=mesh['ez'=16,'ec'=2,'rh'=8,'rl'=2] {'ez'}, dimensions={0} | all-to-all | bytes 2129920 | tf_op jit(solution)/shard_map/all_to_all | solution.py:17
  297.4 9.9 %all_to_all.33 = bf16[16,2,10,1664]{3,0,2,1:T(8,128)(2,1)S(1)} all-to-all(bf16[16,2,10,1664]{3,0,2,1:T(8,128)(2,1)S(1)} %copy.74), channel_id=1, replica_groups=mesh['ez'=16,'ec'=2,'rh'=8,'rl'=2] {'ec'}, dimensions={1} | all-to-all | bytes 2129920 | tf_op jit(solution)/shard_map/all_to_all | solution.py:18
  307.6 0.4 reshape_reshape.20
  308.1 0.7 fusion.15
  308.9 1.1 convolution_convert_fusion.2
  310.0 4.9 %reduce-scatter.2.cloned.1.call-done = f32[3,48,1536]{2,1,0:T(8,128)} async-done(((f32[3,384,1536]{2,1,0:T(8,128)}), f32[3,48,1536]{2,1,0:T(8,128)}) %reduce-scatter.2.cloned.1.call-update) | async-done | bytes 884752 | tf_op jit(solution)/shard_map/reduce_scatter | solution.py:85
  314.9 2.1 fusion.24
  (62 shorter events, 4.2 us)
Async XLA Ops:
  7.2 3.0 copy-start
  11.0 17.9 %copy-start.10 = (bf16[1,48,1536]{2,1,0:T(8,128)(2,1)S(1)}, bf16[1,48,1536]{2,1,0:T(8,128)(2,1)}, u32[]{:S(2)}) copy-start(bf16[1,48,1536]{2,1,0:T(8,128)(2,1)} %param.13) | copy-start | bytes 442372
  11.0 17.9 %copy-start.11 = (bf16[1,48,1536]{2,1,0:T(8,128)(2,1)S(1)}, bf16[1,48,1536]{2,1,0:T(8,128)(2,1)}, u32[]{:S(2)}) copy-start(bf16[1,48,1536]{2,1,0:T(8,128)(2,1)} %param.12) | copy-start | bytes 442372
  11.0 17.9 %copy-start.12 = (bf16[1,48,1536]{2,1,0:T(8,128)(2,1)S(1)}, bf16[1,48,1536]{2,1,0:T(8,128)(2,1)}, u32[]{:S(2)}) copy-start(bf16[1,48,1536]{2,1,0:T(8,128)(2,1)} %param.11) | copy-start | bytes 442372
  13.0 16.8 %copy-start.9 = (bf16[128,1536]{1,0:T(8,128)(2,1)S(1)}, bf16[128,1536]{1,0:T(8,128)(2,1)}, u32[]{:S(2)}) copy-start(bf16[128,1536]{1,0:T(8,128)(2,1)} %param.7) | copy-start | bytes 1179652
  13.0 58.6 %all-to-all-start.2 = ((bf16[16,2,10,1536]{3,1,2,0:T(2,128)(2,1)}), bf16[16,2,10,1536]{3,1,2,0:T(2,128)(2,1)S(1)}, u32[]{:S(2)}, u32[]{:S(2)}) async-start(bf16[16,2,10,1536]{3,1,2,0:T(2,128)(2,1)} %copy.69), calls=%async_computation.2 | async-start | bytes 1966080 | tf_op jit(solution)/shard_map/all_to_all | solution.py:17
  28.8 145.6 %all-gather.2.cloned.1.call-start = ((), (), s32[]{:S(2)}) async-start(), calls=%async_computation.7 | async-start | bytes 3981312 | tf_op jit(solution)/shard_map/all_gather | solution.py:48
  29.8 1.7 copy-start.13
  82.2 53.5 %all-to-all-start = ((bf16[16,2,10,1664]{3,1,2,0:T(2,128)(2,1)}), bf16[16,2,10,1664]{3,1,2,0:T(2,128)(2,1)S(1)}, u32[]{:S(2)}, u32[]{:S(2)}) async-start(bf16[16,2,10,1664]{3,1,2,0:T(2,128)(2,1)} %copy.66), calls=%async_computation | async-start | bytes 2129920 | tf_op jit(solution)/shard_map/all_to_all | solution.py:17
  89.7 225.2 %reduce-scatter.2.cloned.1.call-start = ((), (), s32[]{:S(2)}) async-start(), calls=%async_computation.8 | async-start | bytes 7962624 | tf_op jit(solution)/shard_map/reduce_scatter | solution.py:85
  92.7 58.1 %collective-permute-start.1 = (bf16[320,1536]{1,0:T(8,128)(2,1)}, bf16[320,1536]{1,0:T(8,128)(2,1)}, u32[]{:S(2)}, u32[]{:S(2)}) collective-permute-start(bf16[320,1536]{1,0:T(8,128)(2,1)} %reshape_reshape.18), channel_id=1, source_target_pairs={{0,1},{1,0},{2,3},{3,2},{4,5},{5,4},{6,7},{7,6},{8,9},{9,8},{10,11... | collective-permute-start | bytes 2949128 | tf_op jit(solution)/shard_map/ppermute | solution.py:11
  146.2 26.6 %collective-permute-start = (bf16[320,1664]{1,0:T(8,128)(2,1)S(1)}, bf16[320,1664]{1,0:T(8,128)(2,1)S(1)}, u32[]{:S(2)}, u32[]{:S(2)}) collective-permute-start(bf16[320,1664]{1,0:T(8,128)(2,1)S(1)} %reshape_reshape.16), channel_id=1, source_target_pairs={{0,1},{1,0},{2,3},{3,2},{4,5},{5,4},{6,7},{7,6},{8,9},{9,8},{10,11... | collective-permute-start | bytes 3194888 | tf_op jit(solution)/shard_map/ppermute | solution.py:11
  152.1 20.8 %copy-start.5 = (bf16[640,1536]{1,0:T(8,128)(2,1)}, bf16[640,1536]{1,0:T(8,128)(2,1)S(1)}, u32[]{:S(2)}) copy-start(bf16[640,1536]{1,0:T(8,128)(2,1)S(1)} %constant_dynamic-update-slice_fusion.2) | copy-start | bytes 5898244
  172.9 1.4 copy-start.3
  174.4 3.2 copy-start.4
  174.4 3.6 %copy-start.2 = (bf16[3,384,1536]{2,1,0:T(8,128)(2,1)S(1)}, bf16[3,384,1536]{2,1,0:T(8,128)(2,1)}, u32[]{:S(2)}) copy-start(bf16[3,384,1536]{2,1,0:T(8,128)(2,1)} %all-gather.2.cloned.1.call-done) | copy-start | bytes 10616836
  178.0 1.5 copy-start.6
  182.0 1.1 copy-start.7
  187.9 2.5 copy-start.8
  197.7 35.3 %collective-permute-start.2 = (bf16[320,1664]{1,0:T(8,128)(2,1)S(1)}, bf16[320,1664]{1,0:T(8,128)(2,1)S(1)}, u32[]{:S(2)}, u32[]{:S(2)}) collective-permute-start(bf16[320,1664]{1,0:T(8,128)(2,1)S(1)} %slice.63), channel_id=1, source_target_pairs={{0,1},{1,0},{2,3},{3,2},{4,5},{5,4},{6,7},{7,6},{8,9},{9,8},{10,11... | collective-permute-start | bytes 3194888 | tf_op jit(solution)/shard_map/ppermute | solution.py:11
  307.6 9.4 %copy-start.1 = (bf16[128,1536]{1,0:T(8,128)(2,1)S(1)}, bf16[128,1536]{1,0:T(8,128)(2,1)}, u32[]{:S(2)}) copy-start(bf16[128,1536]{1,0:T(8,128)(2,1)} %param.8) | copy-start | bytes 1179652
Sparse Core Ops, SparseCore 0:
  32.8 87.0 all-gather.1
  187.8 127.0 reduce-scatter.1

commit v6 on v4

--- a/solution.py
+++ b/solution.py
@@ -37,7 +37,10 @@
     slot_grads = jnp.dot(token_routing, grad_out, preferred_element_type=jnp.float32).astype(jnp.bfloat16)
     slot_probs = jnp.dot(routing, prob_pairs, preferred_element_type=jnp.float32).astype(jnp.bfloat16)
     prob_block = jnp.concatenate([slot_probs, jnp.zeros((slots, LANE - 1), jnp.bfloat16)], axis=1)
-    send = jnp.concatenate([slot_tokens, slot_grads, prob_block], axis=1).reshape(exp_count, capacity, -1)
+    send_t = jnp.concatenate([slot_tokens, prob_block], axis=1).reshape(exp_count, capacity, -1)
+    arrived_t = exchange(send_t).reshape(slots, -1)
+    send_g = slot_grads.reshape(exp_count, capacity, -1)
+    arrived_g = exchange(send_g).reshape(slots, -1)
 
     stacked = jnp.concatenate([w_gate, w_up, w_down], axis=0)
     full = lax.all_gather(stacked, "rh", axis=1, tiled=True)
@@ -45,16 +48,9 @@
     up_w = full[1]
     down_w = full[2]
 
-    half = capacity // 2
-    pieces = []
-    local = None
-    for lo, hi in ((0, half), (half, capacity)):
-        arrived = exchange(send[:, lo:hi]).reshape(exp_count * (hi - lo), -1)
-        chunk_rows = arrived.shape[0]
-        joined = jnp.concatenate([arrived, swap_pair(arrived)], axis=0)
-        rows = joined[:, :width]
-        grads = joined[:, width : 2 * width]
-        weight = joined[:, 2 * width : 2 * width + 1].astype(jnp.float32)
+    def block(arrived_rows, grads):
+        rows = arrived_rows[:, :width]
+        weight = arrived_rows[:, width : width + 1].astype(jnp.float32)
         gate = jnp.dot(rows, gate_w.T, preferred_element_type=jnp.float32)
         up = jnp.dot(rows, up_w.T, preferred_element_type=jnp.float32)
         sig = jax.nn.sigmoid(gate)
@@ -72,23 +68,27 @@
             [
                 partial_rows.astype(jnp.bfloat16),
                 prob_part.astype(jnp.bfloat16),
-                jnp.zeros((2 * chunk_rows, LANE - 1), jnp.bfloat16),
+                jnp.zeros((rows.shape[0], LANE - 1), jnp.bfloat16),
             ],
             axis=1,
         )
-        part = jnp.stack(
+        local = jnp.stack(
             [
                 jnp.dot(d_gate.T, rows, preferred_element_type=jnp.float32),
                 jnp.dot(d_up.T, rows, preferred_element_type=jnp.float32),
                 jnp.dot(weighted.T, grads, preferred_element_type=jnp.float32),
             ]
         )
-        local = part if local is None else local + part
-        received = swap_pair(packed[chunk_rows:])
-        summed = (packed[:chunk_rows].astype(jnp.float32) + received.astype(jnp.float32)).astype(jnp.bfloat16)
-        pieces.append(exchange(summed.reshape(exp_count, hi - lo, -1)))
-    weight_grads = lax.psum_scatter(local, "rh", scatter_dimension=1, tiled=True)
-    returned = jnp.concatenate(pieces, axis=1).reshape(slots, -1)
+        return packed, local
+
+    partner_t = swap_pair(arrived_t)
+    partner_g = swap_pair(arrived_g)
+    packed_own, local_own = block(arrived_t, arrived_g)
+    packed_partner, local_partner = block(partner_t, partner_g)
+    received = swap_pair(packed_partner)
+    weight_grads = lax.psum_scatter(local_own + local_partner, "rh", scatter_dimension=1, tiled=True)
+    summed = (packed_own.astype(jnp.float32) + received.astype(jnp.float32)).astype(jnp.bfloat16)
+    returned = exchange(summed.reshape(exp_count, capacity, -1)).reshape(slots, -1)
 
     grad_tokens = jnp.dot(
         token_routing.T, returned[:, :width], preferred_element_type=jnp.float32

time: 353 us -> 323 us (0.915)
  blocking collectives: 38.8 us -> 88.7 us
  waiting for transfers between devices: 158 us -> 122 us
  starting transfers between devices: 57.6 us -> 33.4 us
  local copies, waits for them, and re-layouts: 45.4 us -> 28.5 us
    all_to_all x0 -> x1, blocking collectives: none -> 58.4 us  [exchange(): split = lax.all_to_all(split, 'ez', split_axis=0, concat_axis=0, tiled=True)]
    all_to_all x4 -> x2, waiting for transfers between devices: 102 us -> 79.3 us  [exchange(): split = lax.all_to_all(split, 'ez', split_axis=0, concat_axis=0, tiled=True)]
    all_to_all x4 -> x2, starting transfers between devices: 43.6 us -> 23.6 us  [exchange(): split = lax.all_to_all(split, 'ez', split_axis=0, concat_axis=0, tiled=True)]
    ppermute x4 -> x3, waiting for transfers between devices: 55.3 us -> 35.8 us  [swap_pair(): return lax.ppermute(value, 'rl', [(0, 1), (1, 0)])]
    all_to_all x4 -> x3, blocking collectives: 38.8 us -> 30.3 us  [exchange(): split = lax.all_to_all(split, 'ec', split_axis=1, concat_axis=1, tiled=True)]
    reduce_scatter x1, waiting for transfers between devices: 0.01 us -> 6.6 us  [shards(): lax.psum_scatter(local_own + local_partner, 'rh', scatter_dimension=1, ti...]
    concatenate x10 -> x7, local copies, waits for them, and re-layouts: 16 us -> 10.4 us  [the longest x2 5.41 us: block(): jnp.concatenate([partial_rows.astype(jnp.bfloat16), prob_part.astype(jnp....]
    reshape x5 -> x0, local copies, waits for them, and re-layouts: 4.48 us -> none  [the longest x2 3.66 us: exchange(): blocks.reshape((lax.axis_size('ez'), lax.axis_size('ec')) + shape[1:])]
  transfers between devices with their start and end apart: 10 -> 7, of which waited for: 6 -> 5; matrix products, arithmetic and copies ran while one was open for 12% -> 13% of each run, Pallas kernels for 0% -> 0%
where the time goes in v6:
time: 323 us; the launch traced here: 322 us
  waiting for transfers between devices  122 us (38%)
  blocking collectives  88.7 us (27%)
  starting transfers between devices  33.4 us (10%)
  local copies, waits for them, and re-layouts  28.5 us (9%)
  matrix products  26.3 us (8%)
  between operations  14.5 us (4%)
  other arithmetic  8.49 us (3%)
    all_to_all x2, waiting for transfers between devices, exchange(): split = lax.all_to_all(split, 'ez', split_axis=0, concat_axis=0, tiled=True)  79.3 us
    all_to_all x1, blocking collectives, exchange(): split = lax.all_to_all(split, 'ez', split_axis=0, concat_axis=0, tiled=True)  58.4 us
    ppermute x3, waiting for transfers between devices, swap_pair(): return lax.ppermute(value, 'rl', [(0, 1), (1, 0)])  35.8 us
    all_to_all x3, blocking collectives, exchange(): split = lax.all_to_all(split, 'ec', split_axis=1, concat_axis=1, tiled=True)  30.3 us
    all_to_all x2, starting transfers between devices, exchange(): split = lax.all_to_all(split, 'ez', split_axis=0, concat_axis=0, tiled=True)  23.6 us
    ppermute x3, starting transfers between devices, swap_pair(): return lax.ppermute(value, 'rl', [(0, 1), (1, 0)])  9.67 us
    reduce_scatter x1, waiting for transfers between devices, shards(): lax.psum_scatter(local_own + local_partner, 'rh', scatter_dimension=1, ti...  6.6 us
  transfers between devices with their start and end apart: 7, of which 5 were waited for; matrix products, arithmetic and copies ran while one was open for 13% of the time, Pallas kernels for 0%

profile of v6, /device:TPU:1, one launch (start us, length us, event | category | flops | bytes accessed | tf_op | source)
XLA Modules:
  0.0 321.6 jit_solution(1365934853504875361)
XLA Ops:
  7.2 0.8 copy.63
  9.4 0.8 copy.67
  13.1 1.9 concatenate.22
  15.0 1.8 copy.69
  16.8 15.9 %all-to-all-start = ((bf16[16,2,10,1664]{3,1,2,0:T(2,128)(2,1)}), bf16[16,2,10,1664]{3,1,2,0:T(2,128)(2,1)S(1)}, u32[]{:S(2)}, u32[]{:S(2)}) async-start(bf16[16,2,10,1664]{3,1,2,0:T(2,128)(2,1)} %copy.69), calls=%async_computation | async-start | bytes 2129920 | tf_op jit(solution)/shard_map/all_to_all | solution.py:17
  32.8 0.8 pad_maximum_fusion
  33.7 1.4 convolution_convert_fusion
  35.1 1.4 reshape_reshape.17
  36.4 2.0 copy.72
  38.4 39.9 %all-to-all-done = bf16[16,2,10,1664]{3,1,2,0:T(2,128)(2,1)S(1)} async-done(((bf16[16,2,10,1664]{3,1,2,0:T(2,128)(2,1)}), bf16[16,2,10,1664]{3,1,2,0:T(2,128)(2,1)S(1)}, u32[]{:S(2)}, u32[]{:S(2)}) %all-to-all-start) | async-done | bytes 1064992 | tf_op jit(solution)/shard_map/all_to_all | solution.py:17
  78.5 10.1 %all_to_all.30 = bf16[16,2,10,1664]{3,0,2,1:T(8,128)(2,1)S(1)} all-to-all(bf16[16,2,10,1664]{3,0,2,1:T(8,128)(2,1)S(1)} %copy.70), channel_id=1, replica_groups=mesh['ez'=16,'ec'=2,'rh'=8,'rl'=2] {'ec'}, dimensions={1} | all-to-all | bytes 2129920 | tf_op jit(solution)/shard_map/all_to_all | solution.py:18
  88.5 7.7 %all-to-all-start.2 = ((bf16[16,2,10,1536]{3,1,2,0:T(2,128)(2,1)}), bf16[16,2,10,1536]{3,1,2,0:T(2,128)(2,1)}, u32[]{:S(2)}, u32[]{:S(2)}) async-start(bf16[16,2,10,1536]{3,1,2,0:T(2,128)(2,1)} %copy.72), calls=%async_computation.2 | async-start | bytes 1966080 | tf_op jit(solution)/shard_map/all_to_all | solution.py:17
  97.0 3.1 collective-permute-start
  100.2 39.4 %all-to-all-done.2 = bf16[16,2,10,1536]{3,1,2,0:T(2,128)(2,1)} async-done(((bf16[16,2,10,1536]{3,1,2,0:T(2,128)(2,1)}), bf16[16,2,10,1536]{3,1,2,0:T(2,128)(2,1)}, u32[]{:S(2)}, u32[]{:S(2)}) %all-to-all-start.2) | async-done | bytes 983072 | tf_op jit(solution)/shard_map/all_to_all | solution.py:17
  139.5 1.4 copy.73
  140.9 9.5 %all_to_all.31 = bf16[16,2,10,1536]{3,0,2,1:T(8,128)(2,1)S(1)} all-to-all(bf16[16,2,10,1536]{3,0,2,1:T(8,128)(2,1)S(1)} %copy.73), channel_id=1, replica_groups=mesh['ez'=16,'ec'=2,'rh'=8,'rl'=2] {'ec'}, dimensions={1} | all-to-all | bytes 1966080 | tf_op jit(solution)/shard_map/all_to_all | solution.py:18
  151.0 1.2 reshape_reshape.18
  152.2 3.3 %collective-permute-start.1 = (bf16[320,1536]{1,0:T(8,128)(2,1)}, bf16[320,1536]{1,0:T(8,128)(2,1)S(1)}, u32[]{:S(2)}, u32[]{:S(2)}) collective-permute-start(bf16[320,1536]{1,0:T(8,128)(2,1)} %reshape_reshape.18), channel_id=1, source_target_pairs={{0,1},{1,0},{2,3},{3,2},{4,5},{5,4},{6,7},{7,6},{8,9},{9,8},{10,11... | collective-permute-start | bytes 2949128 | tf_op jit(solution)/shard_map/ppermute | solution.py:11
  155.6 1.0 convert_reduce_fusion
  156.6 2.1 fusion.10
  160.2 0.9 multiply_reduce_fusion.1
  161.1 0.8 convolution_bitcast_fusion.4
  161.9 0.8 convolution_bitcast_fusion.5
  162.8 0.9 convolution_bitcast_fusion.3
  163.7 1.9 fusion.8
  165.6 1.9 fusion.5
  167.5 9.7 %collective-permute-done.1 = bf16[320,1536]{1,0:T(8,128)(2,1)S(1)} collective-permute-done((bf16[320,1536]{1,0:T(8,128)(2,1)}, bf16[320,1536]{1,0:T(8,128)(2,1)S(1)}, u32[]{:S(2)}, u32[]{:S(2)}) %collective-permute-start.1) | collective-permute-done | bytes 983072 | tf_op jit(solution)/shard_map/ppermute | solution.py:11
  177.2 0.9 multiply_reduce_fusion
  178.1 0.9 convolution_bitcast_fusion
  179.1 2.0 convolution_bitcast_fusion.1
  181.1 2.0 convolution_bitcast_fusion.2
  183.1 3.5 %maximum_add_fusion = f32[3,384,1536]{2,1,0:T(8,128)} fusion(f32[1,384,1536]{2,1,0:T(8,128)S(1)} %convolution_bitcast_fusion.3, f32[1,384,1536]{2,1,0:T(8,128)S(1)} %convolution_bitcast_fusion.4, f32[1,384,1536]{2,1,0:T(8,128)S(1)} %convolution_bitcast_fusion.5, f32[1,384,1536]{2,1,0:T(8,128)S(1)} %convolution_bitcast_fusion, ...), kind=kLoop, calls=%fused_computation | loop fusion | flops 8847360 | bytes 21233664 | tf_op jit(solution)/shard_map/add | solution.py:89
  187.4 1.2 copy-done.3
  188.7 1.6 fusion.7
  190.3 1.7 fusion.1
  192.6 3.1 concatenate.25
  195.7 3.2 %collective-permute-start.2 = (bf16[320,1664]{1,0:T(8,128)(2,1)}, bf16[320,1664]{1,0:T(8,128)(2,1)}, u32[]{:S(2)}, u32[]{:S(2)}) collective-permute-start(bf16[320,1664]{1,0:T(8,128)(2,1)} %concatenate.25), channel_id=1, source_target_pairs={{0,1},{1,0},{2,3},{3,2},{4,5},{5,4},{6,7},{7,6},{8,9},{9,8},{10,11... | collective-permute-start | bytes 3194888 | tf_op jit(solution)/shard_map/ppermute | solution.py:11
  199.7 1.6 fusion.9
  201.3 1.6 fusion
  203.0 2.3 concatenate.24
  205.3 26.0 %collective-permute-done.2 = bf16[320,1664]{1,0:T(8,128)(2,1)} collective-permute-done((bf16[320,1664]{1,0:T(8,128)(2,1)}, bf16[320,1664]{1,0:T(8,128)(2,1)}, u32[]{:S(2)}, u32[]{:S(2)}) %collective-permute-start.2) | collective-permute-done | bytes 1064992 | tf_op jit(solution)/shard_map/ppermute | solution.py:11
  231.4 1.5 add_convert_fusion
  233.3 0.8 copy.77
  234.1 58.4 %all_to_all.32 = bf16[16,2,10,1664]{3,1,2,0:T(2,128)(2,1)S(1)} all-to-all(bf16[16,2,10,1664]{3,1,2,0:T(2,128)(2,1)S(1)} %copy.77), channel_id=1, replica_groups=mesh['ez'=16,'ec'=2,'rh'=8,'rl'=2] {'ez'}, dimensions={0} | all-to-all | bytes 2129920 | tf_op jit(solution)/shard_map/all_to_all | solution.py:17
  292.7 10.7 %all_to_all.33 = bf16[16,2,10,1664]{3,0,2,1:T(8,128)(2,1)S(1)} all-to-all(bf16[16,2,10,1664]{3,0,2,1:T(8,128)(2,1)S(1)} %copy.78), channel_id=1, replica_groups=mesh['ez'=16,'ec'=2,'rh'=8,'rl'=2] {'ec'}, dimensions={1} | all-to-all | bytes 2129920 | tf_op jit(solution)/shard_map/all_to_all | solution.py:18
  304.9 1.1 convolution_convert_fusion.2
  306.1 6.6 %reduce-scatter.2.cloned.1.call-done = f32[3,48,1536]{2,1,0:T(8,128)} async-done(((f32[3,384,1536]{2,1,0:T(8,128)}), f32[3,48,1536]{2,1,0:T(8,128)}) %reduce-scatter.2.cloned.1.call-update) | async-done | bytes 884752 | tf_op jit(solution)/shard_map/reduce_scatter | solution.py:89
  312.7 2.1 fusion.38
  (74 shorter events, 11.4 us)
Async XLA Ops:
  7.2 4.4 %copy-start = (bf16[128,1536]{1,0:T(8,128)(2,1)S(1)}, bf16[128,1536]{1,0:T(8,128)(2,1)}, u32[]{:S(2)}) copy-start(bf16[128,1536]{1,0:T(8,128)(2,1)} %param.7) | copy-start | bytes 1179652
  11.1 22.5 %copy-start.5 = (bf16[320,128]{1,0:T(8,128)(2,1)}, bf16[320,128]{1,0:T(8,128)(2,1)S(1)}, u32[]{:S(2)}) copy-start(bf16[320,128]{1,0:T(8,128)(2,1)S(1)} %fusion.30) | copy-start | bytes 245764
  15.0 17.8 %copy-start.14 = (bf16[1,48,1536]{2,1,0:T(8,128)(2,1)S(1)}, bf16[1,48,1536]{2,1,0:T(8,128)(2,1)}, u32[]{:S(2)}) copy-start(bf16[1,48,1536]{2,1,0:T(8,128)(2,1)} %param.13) | copy-start | bytes 442372
  15.0 17.8 %copy-start.15 = (bf16[1,48,1536]{2,1,0:T(8,128)(2,1)S(1)}, bf16[1,48,1536]{2,1,0:T(8,128)(2,1)}, u32[]{:S(2)}) copy-start(bf16[1,48,1536]{2,1,0:T(8,128)(2,1)} %param.12) | copy-start | bytes 442372
  16.8 15.9 %copy-start.16 = (bf16[1,48,1536]{2,1,0:T(8,128)(2,1)S(1)}, bf16[1,48,1536]{2,1,0:T(8,128)(2,1)}, u32[]{:S(2)}) copy-start(bf16[1,48,1536]{2,1,0:T(8,128)(2,1)} %param.11) | copy-start | bytes 442372
  16.8 16.8 %copy-start.13 = (bf16[128,1536]{1,0:T(8,128)(2,1)S(1)}, bf16[128,1536]{1,0:T(8,128)(2,1)}, u32[]{:S(2)}) copy-start(bf16[128,1536]{1,0:T(8,128)(2,1)} %param.8) | copy-start | bytes 1179652
  16.8 61.5 %all-to-all-start = ((bf16[16,2,10,1664]{3,1,2,0:T(2,128)(2,1)}), bf16[16,2,10,1664]{3,1,2,0:T(2,128)(2,1)S(1)}, u32[]{:S(2)}, u32[]{:S(2)}) async-start(bf16[16,2,10,1664]{3,1,2,0:T(2,128)(2,1)} %copy.69), calls=%async_computation | async-start | bytes 2129920 | tf_op jit(solution)/shard_map/all_to_all | solution.py:17
  32.7 123.9 %all-gather.2.cloned.1.call-start = ((), (), s32[]{:S(2)}) async-start(), calls=%async_computation.7 | async-start | bytes 3981312 | tf_op jit(solution)/shard_map/all_gather | solution.py:46
  88.5 51.0 %all-to-all-start.2 = ((bf16[16,2,10,1536]{3,1,2,0:T(2,128)(2,1)}), bf16[16,2,10,1536]{3,1,2,0:T(2,128)(2,1)}, u32[]{:S(2)}, u32[]{:S(2)}) async-start(bf16[16,2,10,1536]{3,1,2,0:T(2,128)(2,1)} %copy.72), calls=%async_computation.2 | async-start | bytes 1966080 | tf_op jit(solution)/shard_map/all_to_all | solution.py:17
  96.3 216.4 %reduce-scatter.2.cloned.1.call-start = ((), (), s32[]{:S(2)}) async-start(), calls=%async_computation.8 | async-start | bytes 7962624 | tf_op jit(solution)/shard_map/reduce_scatter | solution.py:89
  97.0 58.6 %collective-permute-start = (bf16[320,1664]{1,0:T(8,128)(2,1)S(1)}, bf16[320,1664]{1,0:T(8,128)(2,1)}, u32[]{:S(2)}, u32[]{:S(2)}) collective-permute-start(bf16[320,1664]{1,0:T(8,128)(2,1)S(1)} %reshape_reshape.16), channel_id=1, source_target_pairs={{0,1},{1,0},{2,3},{3,2},{4,5},{5,4},{6,7},{7,6},{8,9},{9,8},{10,11... | collective-permute-start | bytes 3194888 | tf_op jit(solution)/shard_map/ppermute | solution.py:11
  152.2 25.0 %collective-permute-start.1 = (bf16[320,1536]{1,0:T(8,128)(2,1)}, bf16[320,1536]{1,0:T(8,128)(2,1)S(1)}, u32[]{:S(2)}, u32[]{:S(2)}) collective-permute-start(bf16[320,1536]{1,0:T(8,128)(2,1)} %reshape_reshape.18), channel_id=1, source_target_pairs={{0,1},{1,0},{2,3},{3,2},{4,5},{5,4},{6,7},{7,6},{8,9},{9,8},{10,11... | collective-permute-start | bytes 2949128 | tf_op jit(solution)/shard_map/ppermute | solution.py:11
  156.6 2.4 copy-start.2
  159.0 1.2 copy-start.4
  161.1 0.8 copy-start.7
  161.1 1.6 copy-start.9
  178.1 0.9 copy-start.10
  178.1 3.0 copy-start.12
  186.6 2.0 copy-start.3
  186.7 3.6 %copy-start.11 = (bf16[320,384]{1,0:T(8,128)(2,1)S(1)}, bf16[320,384]{1,0:T(8,128)(2,1)}, u32[]{:S(2)}) copy-start(bf16[320,384]{1,0:T(8,128)(2,1)} %copy-done.10) | copy-start | bytes 737284
  195.7 5.6 %copy-start.8 = (bf16[320,384]{1,0:T(8,128)(2,1)S(1)}, bf16[320,384]{1,0:T(8,128)(2,1)}, u32[]{:S(2)}) copy-start(bf16[320,384]{1,0:T(8,128)(2,1)} %copy-done.7) | copy-start | bytes 737284
  195.7 35.7 %collective-permute-start.2 = (bf16[320,1664]{1,0:T(8,128)(2,1)}, bf16[320,1664]{1,0:T(8,128)(2,1)}, u32[]{:S(2)}, u32[]{:S(2)}) collective-permute-start(bf16[320,1664]{1,0:T(8,128)(2,1)} %concatenate.25), channel_id=1, source_target_pairs={{0,1},{1,0},{2,3},{3,2},{4,5},{5,4},{6,7},{7,6},{8,9},{9,8},{10,11... | collective-permute-start | bytes 3194888 | tf_op jit(solution)/shard_map/ppermute | solution.py:11
  303.6 1.3 copy-start.6
  303.6 11.1 %copy-start.1 = (bf16[128,1536]{1,0:T(8,128)(2,1)S(1)}, bf16[128,1536]{1,0:T(8,128)(2,1)}, u32[]{:S(2)}) copy-start(bf16[128,1536]{1,0:T(8,128)(2,1)} %param.7) | copy-start | bytes 1179652
Sparse Core Ops, SparseCore 0:
  36.7 86.7 all-gather.1
  186.8 125.8 reduce-scatter.1

commit v7 on v6

--- a/solution.py
+++ b/solution.py
@@ -86,7 +86,9 @@
     packed_own, local_own = block(arrived_t, arrived_g)
     packed_partner, local_partner = block(partner_t, partner_g)
     received = swap_pair(packed_partner)
-    weight_grads = lax.psum_scatter(local_own + local_partner, "rh", scatter_dimension=1, tiled=True)
+    weight_grads = lax.psum_scatter(
+        (local_own + local_partner).astype(jnp.bfloat16), "rh", scatter_dimension=1, tiled=True
+    ).astype(jnp.float32)
     summed = (packed_own.astype(jnp.float32) + received.astype(jnp.float32)).astype(jnp.bfloat16)
     returned = exchange(summed.reshape(exp_count, capacity, -1)).reshape(slots, -1)
 

time: 323 us -> 314 us (0.972)
  waiting for transfers between devices: 122 us -> 115 us
    reduce_scatter x1, waiting for transfers between devices: 6.6 us -> 0.01 us  [shards(): lax.psum_scatter((local_own + local_partner).astype(jnp.bfloat16), 'rh',...]
    add x1 -> x0, other arithmetic: 3.53 us -> none  [shards(): local_own + local_partner]
  transfers between devices with their start and end apart: 7 -> 7, of which waited for: 5 -> 4; matrix products, arithmetic and copies ran while one was open for 13% -> 13% of each run, Pallas kernels for 0% -> 0%
where the time goes in v7:
time: 314 us; the launch traced here: 313 us
  waiting for transfers between devices  115 us (37%)
  blocking collectives  87.9 us (28%)
  starting transfers between devices  33.4 us (11%)
  local copies, waits for them, and re-layouts  28.4 us (9%)
  matrix products  26.3 us (8%)
  between operations  14.5 us (5%)
  other arithmetic  7.28 us (2%)
    all_to_all x2, waiting for transfers between devices, exchange(): split = lax.all_to_all(split, 'ez', split_axis=0, concat_axis=0, tiled=True)  79.3 us
    all_to_all x1, blocking collectives, exchange(): split = lax.all_to_all(split, 'ez', split_axis=0, concat_axis=0, tiled=True)  60 us
    ppermute x3, waiting for transfers between devices, swap_pair(): return lax.ppermute(value, 'rl', [(0, 1), (1, 0)])  35.5 us
    all_to_all x3, blocking collectives, exchange(): split = lax.all_to_all(split, 'ec', split_axis=1, concat_axis=1, tiled=True)  27.9 us
    all_to_all x2, starting transfers between devices, exchange(): split = lax.all_to_all(split, 'ez', split_axis=0, concat_axis=0, tiled=True)  23.6 us
    ppermute x3, starting transfers between devices, swap_pair(): return lax.ppermute(value, 'rl', [(0, 1), (1, 0)])  9.67 us
  transfers between devices with their start and end apart: 7, of which 4 were waited for; matrix products, arithmetic and copies ran while one was open for 13% of the time, Pallas kernels for 0%

profile of v7, /device:TPU:1, one launch (start us, length us, event | category | flops | bytes accessed | tf_op | source)
XLA Modules:
  0.0 312.6 jit_solution(7887945041732350293)
XLA Ops:
  7.2 0.8 copy.63
  9.4 0.8 copy.67
  13.1 1.9 concatenate.22
  15.0 1.8 copy.69
  16.8 15.9 %all-to-all-start = ((bf16[16,2,10,1664]{3,1,2,0:T(2,128)(2,1)}), bf16[16,2,10,1664]{3,1,2,0:T(2,128)(2,1)S(1)}, u32[]{:S(2)}, u32[]{:S(2)}) async-start(bf16[16,2,10,1664]{3,1,2,0:T(2,128)(2,1)} %copy.69), calls=%async_computation | async-start | bytes 2129920 | tf_op jit(solution)/shard_map/all_to_all | solution.py:17
  32.8 0.8 pad_maximum_fusion
  33.7 1.4 convolution_convert_fusion
  35.0 1.4 reshape_reshape.17
  36.4 2.0 copy.72
  38.4 40.0 %all-to-all-done = bf16[16,2,10,1664]{3,1,2,0:T(2,128)(2,1)S(1)} async-done(((bf16[16,2,10,1664]{3,1,2,0:T(2,128)(2,1)}), bf16[16,2,10,1664]{3,1,2,0:T(2,128)(2,1)S(1)}, u32[]{:S(2)}, u32[]{:S(2)}) %all-to-all-start) | async-done | bytes 1064992 | tf_op jit(solution)/shard_map/all_to_all | solution.py:17
  78.4 10.1 %all_to_all.30 = bf16[16,2,10,1664]{3,0,2,1:T(8,128)(2,1)S(1)} all-to-all(bf16[16,2,10,1664]{3,0,2,1:T(8,128)(2,1)S(1)} %copy.70), channel_id=1, replica_groups=mesh['ez'=16,'ec'=2,'rh'=8,'rl'=2] {'ec'}, dimensions={1} | all-to-all | bytes 2129920 | tf_op jit(solution)/shard_map/all_to_all | solution.py:18
  88.5 7.7 %all-to-all-start.2 = ((bf16[16,2,10,1536]{3,1,2,0:T(2,128)(2,1)}), bf16[16,2,10,1536]{3,1,2,0:T(2,128)(2,1)}, u32[]{:S(2)}, u32[]{:S(2)}) async-start(bf16[16,2,10,1536]{3,1,2,0:T(2,128)(2,1)} %copy.72), calls=%async_computation.2 | async-start | bytes 1966080 | tf_op jit(solution)/shard_map/all_to_all | solution.py:17
  97.0 3.1 %collective-permute-start = (bf16[320,1664]{1,0:T(8,128)(2,1)S(1)}, bf16[320,1664]{1,0:T(8,128)(2,1)}, u32[]{:S(2)}, u32[]{:S(2)}) collective-permute-start(bf16[320,1664]{1,0:T(8,128)(2,1)S(1)} %reshape_reshape.16), channel_id=1, source_target_pairs={{0,1},{1,0},{2,3},{3,2},{4,5},{5,4},{6,7},{7,6},{8,9},{9,8},{10,11... | collective-permute-start | bytes 3194888 | tf_op jit(solution)/shard_map/ppermute | solution.py:11
  100.1 39.4 %all-to-all-done.2 = bf16[16,2,10,1536]{3,1,2,0:T(2,128)(2,1)} async-done(((bf16[16,2,10,1536]{3,1,2,0:T(2,128)(2,1)}), bf16[16,2,10,1536]{3,1,2,0:T(2,128)(2,1)}, u32[]{:S(2)}, u32[]{:S(2)}) %all-to-all-start.2) | async-done | bytes 983072 | tf_op jit(solution)/shard_map/all_to_all | solution.py:17
  139.5 1.4 copy.73
  140.9 9.5 %all_to_all.31 = bf16[16,2,10,1536]{3,0,2,1:T(8,128)(2,1)S(1)} all-to-all(bf16[16,2,10,1536]{3,0,2,1:T(8,128)(2,1)S(1)} %copy.73), channel_id=1, replica_groups=mesh['ez'=16,'ec'=2,'rh'=8,'rl'=2] {'ec'}, dimensions={1} | all-to-all | bytes 1966080 | tf_op jit(solution)/shard_map/all_to_all | solution.py:18
  151.0 1.2 reshape_reshape.18
  152.1 3.3 %collective-permute-start.1 = (bf16[320,1536]{1,0:T(8,128)(2,1)}, bf16[320,1536]{1,0:T(8,128)(2,1)S(1)}, u32[]{:S(2)}, u32[]{:S(2)}) collective-permute-start(bf16[320,1536]{1,0:T(8,128)(2,1)} %reshape_reshape.18), channel_id=1, source_target_pairs={{0,1},{1,0},{2,3},{3,2},{4,5},{5,4},{6,7},{7,6},{8,9},{9,8},{10,11... | collective-permute-start | bytes 2949128 | tf_op jit(solution)/shard_map/ppermute | solution.py:11
  155.6 1.0 convert_reduce_fusion
  156.6 2.1 fusion.11
  160.1 0.9 multiply_reduce_fusion.1
  161.1 0.8 convolution_bitcast_fusion.4
  161.9 0.8 convolution_bitcast_fusion.5
  162.7 0.9 convolution_bitcast_fusion.3
  163.6 1.9 fusion.9
  165.5 1.9 fusion.6
  167.4 9.7 %collective-permute-done.1 = bf16[320,1536]{1,0:T(8,128)(2,1)S(1)} collective-permute-done((bf16[320,1536]{1,0:T(8,128)(2,1)}, bf16[320,1536]{1,0:T(8,128)(2,1)S(1)}, u32[]{:S(2)}, u32[]{:S(2)}) %collective-permute-start.1) | collective-permute-done | bytes 983072 | tf_op jit(solution)/shard_map/ppermute | solution.py:11
  177.2 0.9 multiply_reduce_fusion
  178.1 0.9 convolution_bitcast_fusion
  179.0 2.0 convolution_bitcast_fusion.1
  181.1 2.0 convolution_bitcast_fusion.2
  183.1 2.3 fusion
  186.2 1.3 copy-done.3
  187.4 1.6 fusion.8
  189.1 1.7 fusion.2
  191.4 3.1 concatenate.25
  194.5 3.2 %collective-permute-start.2 = (bf16[320,1664]{1,0:T(8,128)(2,1)}, bf16[320,1664]{1,0:T(8,128)(2,1)}, u32[]{:S(2)}, u32[]{:S(2)}) collective-permute-start(bf16[320,1664]{1,0:T(8,128)(2,1)} %concatenate.25), channel_id=1, source_target_pairs={{0,1},{1,0},{2,3},{3,2},{4,5},{5,4},{6,7},{7,6},{8,9},{9,8},{10,11... | collective-permute-start | bytes 3194888 | tf_op jit(solution)/shard_map/ppermute | solution.py:11
  197.7 0.7 convert_element_type.116
  198.5 1.6 fusion.10
  200.1 1.7 fusion.1
  201.8 2.3 concatenate.24
  204.1 25.7 %collective-permute-done.2 = bf16[320,1664]{1,0:T(8,128)(2,1)} collective-permute-done((bf16[320,1664]{1,0:T(8,128)(2,1)}, bf16[320,1664]{1,0:T(8,128)(2,1)}, u32[]{:S(2)}, u32[]{:S(2)}) %collective-permute-start.2) | collective-permute-done | bytes 1064992 | tf_op jit(solution)/shard_map/ppermute | solution.py:11
  229.8 1.5 add_convert_fusion
  231.7 0.8 copy.77
  232.6 60.0 %all_to_all.32 = bf16[16,2,10,1664]{3,1,2,0:T(2,128)(2,1)S(1)} all-to-all(bf16[16,2,10,1664]{3,1,2,0:T(2,128)(2,1)S(1)} %copy.77), channel_id=1, replica_groups=mesh['ez'=16,'ec'=2,'rh'=8,'rl'=2] {'ez'}, dimensions={0} | all-to-all | bytes 2129920 | tf_op jit(solution)/shard_map/all_to_all | solution.py:17
  292.7 8.3 %all_to_all.33 = bf16[16,2,10,1664]{3,0,2,1:T(8,128)(2,1)S(1)} all-to-all(bf16[16,2,10,1664]{3,0,2,1:T(8,128)(2,1)S(1)} %copy.78), channel_id=1, replica_groups=mesh['ez'=16,'ec'=2,'rh'=8,'rl'=2] {'ec'}, dimensions={1} | all-to-all | bytes 2129920 | tf_op jit(solution)/shard_map/all_to_all | solution.py:18
  302.6 1.1 convolution_convert_fusion.2
  303.7 2.0 fusion.39
  (74 shorter events, 10.7 us)
Async XLA Ops:
  7.2 4.4 %copy-start = (bf16[128,1536]{1,0:T(8,128)(2,1)S(1)}, bf16[128,1536]{1,0:T(8,128)(2,1)}, u32[]{:S(2)}) copy-start(bf16[128,1536]{1,0:T(8,128)(2,1)} %param.7) | copy-start | bytes 1179652
  11.1 22.5 %copy-start.5 = (bf16[320,128]{1,0:T(8,128)(2,1)}, bf16[320,128]{1,0:T(8,128)(2,1)S(1)}, u32[]{:S(2)}) copy-start(bf16[320,128]{1,0:T(8,128)(2,1)S(1)} %fusion.31) | copy-start | bytes 245764
  15.0 17.7 %copy-start.14 = (bf16[1,48,1536]{2,1,0:T(8,128)(2,1)S(1)}, bf16[1,48,1536]{2,1,0:T(8,128)(2,1)}, u32[]{:S(2)}) copy-start(bf16[1,48,1536]{2,1,0:T(8,128)(2,1)} %param.13) | copy-start | bytes 442372
  15.0 17.7 %copy-start.15 = (bf16[1,48,1536]{2,1,0:T(8,128)(2,1)S(1)}, bf16[1,48,1536]{2,1,0:T(8,128)(2,1)}, u32[]{:S(2)}) copy-start(bf16[1,48,1536]{2,1,0:T(8,128)(2,1)} %param.12) | copy-start | bytes 442372
  16.8 15.9 %copy-start.16 = (bf16[1,48,1536]{2,1,0:T(8,128)(2,1)S(1)}, bf16[1,48,1536]{2,1,0:T(8,128)(2,1)}, u32[]{:S(2)}) copy-start(bf16[1,48,1536]{2,1,0:T(8,128)(2,1)} %param.11) | copy-start | bytes 442372
  16.8 16.8 %copy-start.13 = (bf16[128,1536]{1,0:T(8,128)(2,1)S(1)}, bf16[128,1536]{1,0:T(8,128)(2,1)}, u32[]{:S(2)}) copy-start(bf16[128,1536]{1,0:T(8,128)(2,1)} %param.8) | copy-start | bytes 1179652
  16.8 61.5 %all-to-all-start = ((bf16[16,2,10,1664]{3,1,2,0:T(2,128)(2,1)}), bf16[16,2,10,1664]{3,1,2,0:T(2,128)(2,1)S(1)}, u32[]{:S(2)}, u32[]{:S(2)}) async-start(bf16[16,2,10,1664]{3,1,2,0:T(2,128)(2,1)} %copy.69), calls=%async_computation | async-start | bytes 2129920 | tf_op jit(solution)/shard_map/all_to_all | solution.py:17
  32.7 123.9 %all-gather.2.cloned.1.call-start = ((), (), s32[]{:S(2)}) async-start(), calls=%async_computation.7 | async-start | bytes 3981312 | tf_op jit(solution)/shard_map/all_gather | solution.py:46
  88.5 51.0 %all-to-all-start.2 = ((bf16[16,2,10,1536]{3,1,2,0:T(2,128)(2,1)}), bf16[16,2,10,1536]{3,1,2,0:T(2,128)(2,1)}, u32[]{:S(2)}, u32[]{:S(2)}) async-start(bf16[16,2,10,1536]{3,1,2,0:T(2,128)(2,1)} %copy.72), calls=%async_computation.2 | async-start | bytes 1966080 | tf_op jit(solution)/shard_map/all_to_all | solution.py:17
  96.3 207.5 %reduce-scatter.2.cloned.1.call-start = ((), (), s32[]{:S(2)}) async-start(), calls=%async_computation.8 | async-start | bytes 3981312 | tf_op jit(solution)/shard_map/reduce_scatter | solution.py:89
  97.0 58.5 %collective-permute-start = (bf16[320,1664]{1,0:T(8,128)(2,1)S(1)}, bf16[320,1664]{1,0:T(8,128)(2,1)}, u32[]{:S(2)}, u32[]{:S(2)}) collective-permute-start(bf16[320,1664]{1,0:T(8,128)(2,1)S(1)} %reshape_reshape.16), channel_id=1, source_target_pairs={{0,1},{1,0},{2,3},{3,2},{4,5},{5,4},{6,7},{7,6},{8,9},{9,8},{10,11... | collective-permute-start | bytes 3194888 | tf_op jit(solution)/shard_map/ppermute | solution.py:11
  152.1 25.0 %collective-permute-start.1 = (bf16[320,1536]{1,0:T(8,128)(2,1)}, bf16[320,1536]{1,0:T(8,128)(2,1)S(1)}, u32[]{:S(2)}, u32[]{:S(2)}) collective-permute-start(bf16[320,1536]{1,0:T(8,128)(2,1)} %reshape_reshape.18), channel_id=1, source_target_pairs={{0,1},{1,0},{2,3},{3,2},{4,5},{5,4},{6,7},{7,6},{8,9},{9,8},{10,11... | collective-permute-start | bytes 2949128 | tf_op jit(solution)/shard_map/ppermute | solution.py:11
  156.6 2.4 copy-start.2
  158.9 1.2 copy-start.4
  161.1 1.6 copy-start.7
  161.1 1.6 copy-start.9
  178.1 0.9 copy-start.10
  178.1 3.0 copy-start.12
  185.4 2.0 copy-start.3
  185.4 3.6 %copy-start.11 = (bf16[320,384]{1,0:T(8,128)(2,1)S(1)}, bf16[320,384]{1,0:T(8,128)(2,1)}, u32[]{:S(2)}) copy-start(bf16[320,384]{1,0:T(8,128)(2,1)} %copy-done.10) | copy-start | bytes 737284
  194.5 5.6 %copy-start.8 = (bf16[320,384]{1,0:T(8,128)(2,1)S(1)}, bf16[320,384]{1,0:T(8,128)(2,1)}, u32[]{:S(2)}) copy-start(bf16[320,384]{1,0:T(8,128)(2,1)} %copy-done.7) | copy-start | bytes 737284
  194.5 35.4 %collective-permute-start.2 = (bf16[320,1664]{1,0:T(8,128)(2,1)}, bf16[320,1664]{1,0:T(8,128)(2,1)}, u32[]{:S(2)}, u32[]{:S(2)}) collective-permute-start(bf16[320,1664]{1,0:T(8,128)(2,1)} %concatenate.25), channel_id=1, source_target_pairs={{0,1},{1,0},{2,3},{3,2},{4,5},{5,4},{6,7},{7,6},{8,9},{9,8},{10,11... | collective-permute-start | bytes 3194888 | tf_op jit(solution)/shard_map/ppermute | solution.py:11
  301.3 1.3 copy-start.6
  301.3 4.4 %copy-start.1 = (bf16[128,1536]{1,0:T(8,128)(2,1)S(1)}, bf16[128,1536]{1,0:T(8,128)(2,1)}, u32[]{:S(2)}) copy-start(bf16[128,1536]{1,0:T(8,128)(2,1)} %param.7) | copy-start | bytes 1179652
Sparse Core Ops, SparseCore 0:
  36.7 86.7 all-gather.1
  185.6 100.5 reduce-scatter.1

commit v8 on v7

--- a/solution.py
+++ b/solution.py
@@ -16,6 +16,14 @@
     split = blocks.reshape((lax.axis_size("ez"), lax.axis_size("ec")) + shape[1:])
     split = lax.all_to_all(split, "ez", split_axis=0, concat_axis=0, tiled=True)
     split = lax.all_to_all(split, "ec", split_axis=1, concat_axis=1, tiled=True)
+    return split.reshape(shape)
+
+
+def exchange_back(blocks):
+    shape = blocks.shape
+    split = blocks.reshape((lax.axis_size("ez"), lax.axis_size("ec")) + shape[1:])
+    split = lax.all_to_all(split, "ec", split_axis=1, concat_axis=1, tiled=True)
+    split = lax.all_to_all(split, "ez", split_axis=0, concat_axis=0, tiled=True)
     return split.reshape(shape)
 
 
@@ -90,7 +98,7 @@
         (local_own + local_partner).astype(jnp.bfloat16), "rh", scatter_dimension=1, tiled=True
     ).astype(jnp.float32)
     summed = (packed_own.astype(jnp.float32) + received.astype(jnp.float32)).astype(jnp.bfloat16)
-    returned = exchange(summed.reshape(exp_count, capacity, -1)).reshape(slots, -1)
+    returned = exchange_back(summed.reshape(exp_count, capacity, -1)).reshape(slots, -1)
 
     grad_tokens = jnp.dot(
         token_routing.T, returned[:, :width], preferred_element_type=jnp.float32

time: 314 us -> 315 us (level)
    all_to_all x1 -> x2, blocking collectives: 60 us -> 69 us  [the longest x1 62.4 us: exchange_back(): split = lax.all_to_all(split, 'ez', split_axis=0, concat_axis=0, tiled=True)]
    all_to_all x3 -> x2, blocking collectives: 27.9 us -> 19.5 us  [exchange(): split = lax.all_to_all(split, 'ec', split_axis=1, concat_axis=1, tiled=True)]
where the time goes in v8:
time: 315 us; the launch traced here: 313 us
  waiting for transfers between devices  115 us (37%)
  blocking collectives  88.5 us (28%)
  starting transfers between devices  33.4 us (11%)
  local copies, waits for them, and re-layouts  28.5 us (9%)
  matrix products  26.3 us (8%)
  between operations  14.5 us (5%)
  other arithmetic  7.28 us (2%)
    all_to_all x2, waiting for transfers between devices, exchange(): split = lax.all_to_all(split, 'ez', split_axis=0, concat_axis=0, tiled=True)  79.3 us
    all_to_all x1, blocking collectives, exchange_back(): split = lax.all_to_all(split, 'ez', split_axis=0, concat_axis=0, tiled=True)  62.4 us
    ppermute x3, waiting for transfers between devices, swap_pair(): return lax.ppermute(value, 'rl', [(0, 1), (1, 0)])  35.5 us
    all_to_all x2, starting transfers between devices, exchange(): split = lax.all_to_all(split, 'ez', split_axis=0, concat_axis=0, tiled=True)  23.6 us
    all_to_all x2, blocking collectives, exchange(): split = lax.all_to_all(split, 'ec', split_axis=1, concat_axis=1, tiled=True)  19.5 us
    ppermute x3, starting transfers between devices, swap_pair(): return lax.ppermute(value, 'rl', [(0, 1), (1, 0)])  9.67 us
    all_to_all x1, blocking collectives, exchange_back(): split = lax.all_to_all(split, 'ec', split_axis=1, concat_axis=1, tiled=True)  6.57 us
  transfers between devices with their start and end apart: 7, of which 4 were waited for; matrix products, arithmetic and copies ran while one was open for 13% of the time, Pallas kernels for 0%

profile of v8, /device:TPU:1, one launch (start us, length us, event | category | flops | bytes accessed | tf_op | source)
XLA Modules:
  0.0 313.3 jit_solution(16360680444818445664)
XLA Ops:
  7.2 0.8 copy.63
  9.4 0.8 copy.67
  13.1 1.9 concatenate.22
  15.0 1.8 copy.69
  16.8 15.9 %all-to-all-start = ((bf16[16,2,10,1664]{3,1,2,0:T(2,128)(2,1)}), bf16[16,2,10,1664]{3,1,2,0:T(2,128)(2,1)S(1)}, u32[]{:S(2)}, u32[]{:S(2)}) async-start(bf16[16,2,10,1664]{3,1,2,0:T(2,128)(2,1)} %copy.69), calls=%async_computation | async-start | bytes 2129920 | tf_op jit(solution)/shard_map/all_to_all | solution.py:17
  32.8 0.8 pad_maximum_fusion
  33.7 1.4 convolution_convert_fusion
  35.0 1.4 reshape_reshape.17
  36.4 2.0 copy.72
  38.4 40.0 %all-to-all-done = bf16[16,2,10,1664]{3,1,2,0:T(2,128)(2,1)S(1)} async-done(((bf16[16,2,10,1664]{3,1,2,0:T(2,128)(2,1)}), bf16[16,2,10,1664]{3,1,2,0:T(2,128)(2,1)S(1)}, u32[]{:S(2)}, u32[]{:S(2)}) %all-to-all-start) | async-done | bytes 1064992 | tf_op jit(solution)/shard_map/all_to_all | solution.py:17
  78.4 10.1 %all_to_all.30 = bf16[16,2,10,1664]{3,0,2,1:T(8,128)(2,1)S(1)} all-to-all(bf16[16,2,10,1664]{3,0,2,1:T(8,128)(2,1)S(1)} %copy.70), channel_id=1, replica_groups=mesh['ez'=16,'ec'=2,'rh'=8,'rl'=2] {'ec'}, dimensions={1} | all-to-all | bytes 2129920 | tf_op jit(solution)/shard_map/all_to_all | solution.py:18
  88.5 7.7 %all-to-all-start.2 = ((bf16[16,2,10,1536]{3,1,2,0:T(2,128)(2,1)}), bf16[16,2,10,1536]{3,1,2,0:T(2,128)(2,1)}, u32[]{:S(2)}, u32[]{:S(2)}) async-start(bf16[16,2,10,1536]{3,1,2,0:T(2,128)(2,1)} %copy.72), calls=%async_computation.2 | async-start | bytes 1966080 | tf_op jit(solution)/shard_map/all_to_all | solution.py:17
  97.0 3.1 collective-permute-start
  100.1 39.4 %all-to-all-done.2 = bf16[16,2,10,1536]{3,1,2,0:T(2,128)(2,1)} async-done(((bf16[16,2,10,1536]{3,1,2,0:T(2,128)(2,1)}), bf16[16,2,10,1536]{3,1,2,0:T(2,128)(2,1)}, u32[]{:S(2)}, u32[]{:S(2)}) %all-to-all-start.2) | async-done | bytes 983072 | tf_op jit(solution)/shard_map/all_to_all | solution.py:17
  139.5 1.4 copy.73
  140.9 9.5 %all_to_all.31 = bf16[16,2,10,1536]{3,0,2,1:T(8,128)(2,1)S(1)} all-to-all(bf16[16,2,10,1536]{3,0,2,1:T(8,128)(2,1)S(1)} %copy.73), channel_id=1, replica_groups=mesh['ez'=16,'ec'=2,'rh'=8,'rl'=2] {'ec'}, dimensions={1} | all-to-all | bytes 1966080 | tf_op jit(solution)/shard_map/all_to_all | solution.py:18
  151.0 1.2 reshape_reshape.18
  152.1 3.3 %collective-permute-start.1 = (bf16[320,1536]{1,0:T(8,128)(2,1)}, bf16[320,1536]{1,0:T(8,128)(2,1)S(1)}, u32[]{:S(2)}, u32[]{:S(2)}) collective-permute-start(bf16[320,1536]{1,0:T(8,128)(2,1)} %reshape_reshape.18), channel_id=1, source_target_pairs={{0,1},{1,0},{2,3},{3,2},{4,5},{5,4},{6,7},{7,6},{8,9},{9,8},{10,11... | collective-permute-start | bytes 2949128 | tf_op jit(solution)/shard_map/ppermute | solution.py:11
  155.6 1.0 convert_reduce_fusion
  156.6 2.1 fusion.11
  160.1 0.9 multiply_reduce_fusion.1
  161.1 0.8 convolution_bitcast_fusion.4
  161.9 0.8 convolution_bitcast_fusion.5
  162.7 0.9 convolution_bitcast_fusion.3
  163.6 1.9 fusion.9
  165.5 1.9 fusion.6
  167.4 9.7 %collective-permute-done.1 = bf16[320,1536]{1,0:T(8,128)(2,1)S(1)} collective-permute-done((bf16[320,1536]{1,0:T(8,128)(2,1)}, bf16[320,1536]{1,0:T(8,128)(2,1)S(1)}, u32[]{:S(2)}, u32[]{:S(2)}) %collective-permute-start.1) | collective-permute-done | bytes 983072 | tf_op jit(solution)/shard_map/ppermute | solution.py:11
  177.2 0.9 multiply_reduce_fusion
  178.1 0.9 convolution_bitcast_fusion
  179.0 2.0 convolution_bitcast_fusion.1
  181.1 2.0 convolution_bitcast_fusion.2
  183.1 2.3 fusion
  186.2 1.3 copy-done.3
  187.4 1.6 fusion.8
  189.1 1.7 fusion.2
  191.4 3.1 concatenate.25
  194.5 3.2 %collective-permute-start.2 = (bf16[320,1664]{1,0:T(8,128)(2,1)}, bf16[320,1664]{1,0:T(8,128)(2,1)}, u32[]{:S(2)}, u32[]{:S(2)}) collective-permute-start(bf16[320,1664]{1,0:T(8,128)(2,1)} %concatenate.25), channel_id=1, source_target_pairs={{0,1},{1,0},{2,3},{3,2},{4,5},{5,4},{6,7},{7,6},{8,9},{9,8},{10,11... | collective-permute-start | bytes 3194888 | tf_op jit(solution)/shard_map/ppermute | solution.py:11
  197.7 0.7 convert_element_type.116
  198.5 1.6 fusion.10
  200.1 1.7 fusion.1
  201.8 2.3 concatenate.24
  204.1 25.7 %collective-permute-done.2 = bf16[320,1664]{1,0:T(8,128)(2,1)} collective-permute-done((bf16[320,1664]{1,0:T(8,128)(2,1)}, bf16[320,1664]{1,0:T(8,128)(2,1)}, u32[]{:S(2)}, u32[]{:S(2)}) %collective-permute-start.2) | collective-permute-done | bytes 1064992 | tf_op jit(solution)/shard_map/ppermute | solution.py:11
  229.8 1.5 add_convert_fusion
  232.1 6.6 %all_to_all.32 = bf16[16,2,10,1664]{3,0,2,1:T(8,128)(2,1)S(1)} all-to-all(bf16[16,2,10,1664]{3,0,2,1:T(8,128)(2,1)S(1)} %copy.77), channel_id=1, replica_groups=mesh['ez'=16,'ec'=2,'rh'=8,'rl'=2] {'ec'}, dimensions={1} | all-to-all | bytes 2129920 | tf_op jit(solution)/shard_map/all_to_all | solution.py:25
  238.6 0.8 copy.78
  239.5 62.4 %all_to_all.33 = bf16[16,2,10,1664]{3,1,2,0:T(2,128)(2,1)S(1)} all-to-all(bf16[16,2,10,1664]{3,1,2,0:T(2,128)(2,1)S(1)} %copy.78), channel_id=1, replica_groups=mesh['ez'=16,'ec'=2,'rh'=8,'rl'=2] {'ez'}, dimensions={0} | all-to-all | bytes 2129920 | tf_op jit(solution)/shard_map/all_to_all | solution.py:26
  303.4 1.1 convolution_convert_fusion.2
  304.5 2.0 fusion.39
  (74 shorter events, 10.8 us)
Async XLA Ops:
  7.2 4.4 %copy-start = (bf16[128,1536]{1,0:T(8,128)(2,1)S(1)}, bf16[128,1536]{1,0:T(8,128)(2,1)}, u32[]{:S(2)}) copy-start(bf16[128,1536]{1,0:T(8,128)(2,1)} %param.7) | copy-start | bytes 1179652
  11.1 22.5 %copy-start.5 = (bf16[320,128]{1,0:T(8,128)(2,1)}, bf16[320,128]{1,0:T(8,128)(2,1)S(1)}, u32[]{:S(2)}) copy-start(bf16[320,128]{1,0:T(8,128)(2,1)S(1)} %fusion.31) | copy-start | bytes 245764
  15.0 17.7 %copy-start.14 = (bf16[1,48,1536]{2,1,0:T(8,128)(2,1)S(1)}, bf16[1,48,1536]{2,1,0:T(8,128)(2,1)}, u32[]{:S(2)}) copy-start(bf16[1,48,1536]{2,1,0:T(8,128)(2,1)} %param.13) | copy-start | bytes 442372
  15.0 17.7 %copy-start.15 = (bf16[1,48,1536]{2,1,0:T(8,128)(2,1)S(1)}, bf16[1,48,1536]{2,1,0:T(8,128)(2,1)}, u32[]{:S(2)}) copy-start(bf16[1,48,1536]{2,1,0:T(8,128)(2,1)} %param.12) | copy-start | bytes 442372
  16.8 15.9 %copy-start.16 = (bf16[1,48,1536]{2,1,0:T(8,128)(2,1)S(1)}, bf16[1,48,1536]{2,1,0:T(8,128)(2,1)}, u32[]{:S(2)}) copy-start(bf16[1,48,1536]{2,1,0:T(8,128)(2,1)} %param.11) | copy-start | bytes 442372
  16.8 16.8 %copy-start.13 = (bf16[128,1536]{1,0:T(8,128)(2,1)S(1)}, bf16[128,1536]{1,0:T(8,128)(2,1)}, u32[]{:S(2)}) copy-start(bf16[128,1536]{1,0:T(8,128)(2,1)} %param.8) | copy-start | bytes 1179652
  16.8 61.5 %all-to-all-start = ((bf16[16,2,10,1664]{3,1,2,0:T(2,128)(2,1)}), bf16[16,2,10,1664]{3,1,2,0:T(2,128)(2,1)S(1)}, u32[]{:S(2)}, u32[]{:S(2)}) async-start(bf16[16,2,10,1664]{3,1,2,0:T(2,128)(2,1)} %copy.69), calls=%async_computation | async-start | bytes 2129920 | tf_op jit(solution)/shard_map/all_to_all | solution.py:17
  32.7 123.9 %all-gather.2.cloned.1.call-start = ((), (), s32[]{:S(2)}) async-start(), calls=%async_computation.7 | async-start | bytes 3981312 | tf_op jit(solution)/shard_map/all_gather | solution.py:54
  88.5 51.0 %all-to-all-start.2 = ((bf16[16,2,10,1536]{3,1,2,0:T(2,128)(2,1)}), bf16[16,2,10,1536]{3,1,2,0:T(2,128)(2,1)}, u32[]{:S(2)}, u32[]{:S(2)}) async-start(bf16[16,2,10,1536]{3,1,2,0:T(2,128)(2,1)} %copy.72), calls=%async_computation.2 | async-start | bytes 1966080 | tf_op jit(solution)/shard_map/all_to_all | solution.py:17
  96.3 208.2 %reduce-scatter.2.cloned.1.call-start = ((), (), s32[]{:S(2)}) async-start(), calls=%async_computation.8 | async-start | bytes 3981312 | tf_op jit(solution)/shard_map/reduce_scatter | solution.py:97
  97.0 58.5 %collective-permute-start = (bf16[320,1664]{1,0:T(8,128)(2,1)S(1)}, bf16[320,1664]{1,0:T(8,128)(2,1)}, u32[]{:S(2)}, u32[]{:S(2)}) collective-permute-start(bf16[320,1664]{1,0:T(8,128)(2,1)S(1)} %reshape_reshape.16), channel_id=1, source_target_pairs={{0,1},{1,0},{2,3},{3,2},{4,5},{5,4},{6,7},{7,6},{8,9},{9,8},{10,11... | collective-permute-start | bytes 3194888 | tf_op jit(solution)/shard_map/ppermute | solution.py:11
  152.1 25.0 %collective-permute-start.1 = (bf16[320,1536]{1,0:T(8,128)(2,1)}, bf16[320,1536]{1,0:T(8,128)(2,1)S(1)}, u32[]{:S(2)}, u32[]{:S(2)}) collective-permute-start(bf16[320,1536]{1,0:T(8,128)(2,1)} %reshape_reshape.18), channel_id=1, source_target_pairs={{0,1},{1,0},{2,3},{3,2},{4,5},{5,4},{6,7},{7,6},{8,9},{9,8},{10,11... | collective-permute-start | bytes 2949128 | tf_op jit(solution)/shard_map/ppermute | solution.py:11
  156.6 2.4 copy-start.2
  158.9 1.2 copy-start.4
  161.1 1.6 copy-start.7
  161.1 1.6 copy-start.9
  178.1 0.9 copy-start.10
  178.1 3.0 copy-start.12
  185.4 2.0 copy-start.3
  185.4 3.6 %copy-start.11 = (bf16[320,384]{1,0:T(8,128)(2,1)S(1)}, bf16[320,384]{1,0:T(8,128)(2,1)}, u32[]{:S(2)}) copy-start(bf16[320,384]{1,0:T(8,128)(2,1)} %copy-done.10) | copy-start | bytes 737284
  194.5 5.6 %copy-start.8 = (bf16[320,384]{1,0:T(8,128)(2,1)S(1)}, bf16[320,384]{1,0:T(8,128)(2,1)}, u32[]{:S(2)}) copy-start(bf16[320,384]{1,0:T(8,128)(2,1)} %copy-done.7) | copy-start | bytes 737284
  194.5 35.4 %collective-permute-start.2 = (bf16[320,1664]{1,0:T(8,128)(2,1)}, bf16[320,1664]{1,0:T(8,128)(2,1)}, u32[]{:S(2)}, u32[]{:S(2)}) collective-permute-start(bf16[320,1664]{1,0:T(8,128)(2,1)} %concatenate.25), channel_id=1, source_target_pairs={{0,1},{1,0},{2,3},{3,2},{4,5},{5,4},{6,7},{7,6},{8,9},{9,8},{10,11... | collective-permute-start | bytes 3194888 | tf_op jit(solution)/shard_map/ppermute | solution.py:11
  302.1 1.3 copy-start.6
  302.1 4.4 %copy-start.1 = (bf16[128,1536]{1,0:T(8,128)(2,1)S(1)}, bf16[128,1536]{1,0:T(8,128)(2,1)}, u32[]{:S(2)}) copy-start(bf16[128,1536]{1,0:T(8,128)(2,1)} %param.7) | copy-start | bytes 1179652
Sparse Core Ops, SparseCore 0:
  36.7 86.7 all-gather.1
  185.6 100.5 reduce-scatter.1
